TPU v7x, 256 devices: a whole 4x4x8 slice. The times are simulated.
256 devices in a mesh: dom: 32 (over x_lo, z, core), band: 8 (over x_hi, y).
Axes of the slice: x: 4 (x_hi: 2, x_lo: 2; x = x_hi * 2 + x_lo), y: 4, z: 8, core: 2. Of those that a mesh axis runs over, the one named last changes fastest.
Arguments:
- ensemble: float32 [32, 3, 128, 4096], P('dom', None, 'band'), may hold values from -6 to 6
- ancestors: int32 [32], P('dom'), may hold values from 0 to 31
- sea_depth: float32 [128, 4096], P('band'), may hold values from 1 to 2
- obs_rows: int32 [16384], P('band'), may hold values from 0 to 127, as said below
- obs_cols: int32 [16384], P('band'), may hold values from 0 to 4095
- obs_values: float32 [16384], P('band'), may hold values from -6 to 6
Outputs:
- forecast: float32 [32, 3, 128, 4096], P('dom', None, 'band')
Inputs may be any that keep to these rules, and one draw needn't show every extreme that they name: `obs_rows`: observations b * 2048 to (b + 1) * 2048 - 1 lie in rows b * 16 to (b + 1) * 16 - 1; no two observations share a cell.
All inputs are finite; a program needn't handle non-finite values.
Results may differ from a plain program's by a relative error of at most 0.00016.
Values sent between devices are 32-bit elements; how exact they have to be, the bound alone decides.
No kernel may reach another device: no remote copies, remote signals or barrier semaphores. Data moves between devices by JAX's collectives and lax.ppermute only.
A program may use at most 64 MiB of HBM per device.

v0:
```python
import jax
import jax.numpy as jnp
from jax import lax
from jax.sharding import PartitionSpec as P

STEPS = 4
BW = 8


TIME_STEP = 0.8
NUDGE_GAIN = 0.5
LENGTH_SCALE = 3.0


def extended(cells, sides, width):
    for axis, dim in sides:
        count = lax.axis_size(axis)
        ends = count - 1
        head = lax.slice_in_dim(cells, 0, width, axis=dim)
        tail = lax.slice_in_dim(cells, cells.shape[dim] - width, cells.shape[dim], axis=dim)
        cells = jnp.concatenate(
            [
                lax.ppermute(tail, axis, [(i, (i + 1) % count) for i in range(ends)]),
                cells,
                lax.ppermute(head, axis, [((i + 1) % count, i) for i in range(ends)]),
            ],
            axis=dim,
        )
    return cells


def kernel(offset):
    distance = jnp.abs(offset).astype(jnp.float32)
    return jnp.where(distance <= BW, jnp.exp(-distance / LENGTH_SCALE), jnp.float32(0.0))


def advance(height, east_vel, north_vel, sea_depth, coriolis, inside):
    flux_east = sea_depth * east_vel
    flux_north = sea_depth * north_vel
    east_diff = 0.5 * (jnp.roll(flux_east, -1, -1) - jnp.roll(flux_east, 1, -1))[:, 1:-1]
    north_diff = 0.5 * (flux_north[:, 2:] - flux_north[:, :-2])
    new_height = jnp.where(
        inside[1:-1, None], height[:, 1:-1] - TIME_STEP * (east_diff + north_diff), jnp.float32(0.0)
    )
    slope_east = 0.5 * (jnp.roll(new_height, -1, -1) - jnp.roll(new_height, 1, -1))[:, 1:-1]
    slope_north = 0.5 * (new_height[:, 2:] - new_height[:, :-2])
    turning = coriolis[2:-2, None]
    keeping = inside[2:-2, None]
    new_east = jnp.where(
        keeping,
        east_vel[:, 2:-2] + TIME_STEP * (turning * north_vel[:, 2:-2] - slope_east),
        jnp.float32(0.0),
    )
    new_north = jnp.where(
        keeping,
        north_vel[:, 2:-2] + TIME_STEP * (-turning * east_vel[:, 2:-2] - slope_north),
        jnp.float32(0.0),
    )
    return (new_height[:, 1:-1], new_east, new_north)


def on_device(ensemble, ancestors, sea_depth, obs_rows, obs_cols, obs_values):
    local_count, fields, band_rows, columns = ensemble.shape
    lineage = lax.all_gather(ancestors, "dom", axis=0, tiled=True)
    crossed = lax.all_to_all(ensemble, "dom", split_axis=3, concat_axis=0, tiled=True)
    chosen = jnp.take(crossed, lineage, axis=0)
    state = lax.all_to_all(chosen, "dom", split_axis=0, concat_axis=3, tiled=True)
    band_start = lax.axis_index("band") * band_rows
    local_rows = obs_rows - band_start
    position = local_rows * columns + obs_cols
    height = state[:, 0]
    east_vel = state[:, 1]
    north_vel = state[:, 2]
    sampled = jnp.take(height.reshape(local_count, band_rows * columns), position, axis=1)
    innovation = obs_values[None, :] - sampled
    col_index = jnp.arange(columns)
    col_kernel = kernel(col_index[:, None] - col_index[None, :])
    scattered = (
        jnp.zeros((local_count, band_rows * columns), jnp.float32).at[:, position].add(innovation)
    )
    spread_field = jnp.dot(
        scattered.reshape(local_count * band_rows, columns),
        col_kernel,
        precision=lax.Precision.HIGHEST,
    )
    spread_field = spread_field.reshape(local_count, band_rows, columns)
    widened = extended(spread_field, (("band", 1),), BW)
    row_kernel = kernel(
        jnp.arange(band_rows)[:, None] - jnp.arange(band_rows + 2 * BW)[None, :] + BW
    )
    increment = jnp.einsum("rm,pmc->prc", row_kernel, widened, precision=lax.Precision.HIGHEST)
    height = height + NUDGE_GAIN * increment
    margin = 2 * STEPS
    total_rows = band_rows * lax.axis_size("band")
    depth_wide = extended(sea_depth, (("band", 0),), margin)
    global_rows = band_start - margin + jnp.arange(band_rows + 2 * margin)
    inside_all = (global_rows >= 0) & (global_rows < total_rows)
    coriolis_all = 0.1 + 0.4 * ((global_rows.astype(jnp.float32) + 0.5) / total_rows)
    first_row = margin - 2
    last_row = first_row + band_rows + 4
    for section_no in range(STEPS):
        stacked = jnp.stack([height, east_vel, north_vel], axis=1)
        widened_state = extended(stacked, (("band", 2),), 2)
        height, east_vel, north_vel = advance(
            widened_state[:, 0],
            widened_state[:, 1],
            widened_state[:, 2],
            depth_wide[first_row:last_row],
            coriolis_all[first_row:last_row],
            inside_all[first_row:last_row],
        )
    return jnp.stack([height, east_vel, north_vel], axis=1)


def solution(mesh):
    placed = (
        P("dom", None, "band", None),
        P("dom"),
        P("band", None),
        P("band"),
        P("band"),
        P("band"),
    )
    return jax.shard_map(
        on_device,
        mesh=mesh,
        in_specs=placed,
        out_specs=P("dom", None, "band", None),
        check_vma=False,
    )
```

profile of v0, /device:TPU:36, one launch (start us, length us, event | category | flops | bytes accessed | tf_op | source)
XLA Modules:
  0.0 254.7 jit_solution(9217861962924951535)
XLA Ops:
  0.0 6.9 %copy.10 = f32[1,3,16,4096]{2,1,0,3:T(4,128)} copy(f32[1,3,16,4096]{3,2,1,0:T(8,128)} %param.6) | data formatting | bytes 1572864 | tf_op args[0]
  6.9 9.1 %reshape.512 = f32[32,1,6144]{2,1,0:T(1,128)} reshape(f32[4096,1,3,16]{3,2,1,0:T(4,128)} %bitcast.134) | data formatting | bytes 1572864
  16.0 9.5 %all-to-all-start = ((f32[32,1,6144]{2,1,0:T(1,128)}), f32[32,1,6144]{2,1,0:T(1,128)S(1)}, u32[]{:S(2)}, u32[]{:S(2)}) async-start(f32[32,1,6144]{2,1,0:T(1,128)} %reshape.512), calls=%async_computation | async-start | bytes 1572864 | tf_op jit(solution)/shard_map/all_to_all | solution.py:65
  27.4 28.7 %all-reduce = s32[32]{0:T(128)S(1)} all-reduce(s32[32]{0:T(128)S(1)} %dynamic-update-slice), channel_id=1, replica_groups=mesh['dom'=32,'band'=8] {'dom'}, use_global_device_ids=true, to_apply=%add | all-reduce | flops 32 | bytes 256
  56.6 2.5 reduce
  59.1 7.1 %reshape.513 = f32[4096,1,3,16]{3,2,1,0:T(4,128)} reshape(f32[32,6144]{1,0:T(8,128)S(1)} %reduce) | data formatting | bytes 1572864
  66.2 6.4 %copy.12 = f32[1,3,16,32,128]{4,2,1,3,0:T(8,128)S(1)} copy(f32[1,3,16,32,128]{2,1,4,3,0:T(4,128)} %bitcast.133) | data formatting | bytes 1572864 | tf_op jit(solution)/shard_map/all_to_all | solution.py:65
  74.3 5.7 %all-to-all-start.1 = ((f32[32,3,16,128]{3,2,1,0:T(8,128)}), f32[32,3,16,128]{3,2,1,0:T(8,128)S(1)}, u32[]{:S(2)}, u32[]{:S(2)}) async-start(f32[32,3,16,128]{3,2,1,0:T(8,128)} %broadcast_select_fusion), calls=%async_computation.1 | async-start | bytes 1572864 | tf_op jit(solution)/shard_map/all_to_all | solution.py:67
  80.0 5.2 %collective-permute-start.5 = (f32[8,4096]{1,0:T(8,128)S(1)}, f32[8,4096]{1,0:T(8,128)S(1)}, u32[]{:S(2)}, u32[]{:S(2)}) collective-permute-start(f32[8,4096]{1,0:T(8,128)S(1)} %get-tuple-element.80), channel_id=1, source_target_pairs={{1,0},{2,1},{3,2},{4,3},{5,4},{6,5},{7,6},{9,8},{10,9},{11,10},{12... | collective-permute-start | bytes 393224 | tf_op jit(solution)/shard_map/ppermute | solution.py:25
  87.2 16.2 %all-to-all-done.1 = f32[32,3,16,128]{3,2,1,0:T(8,128)S(1)} async-done(((f32[32,3,16,128]{3,2,1,0:T(8,128)}), f32[32,3,16,128]{3,2,1,0:T(8,128)S(1)}, u32[]{:S(2)}, u32[]{:S(2)}) %all-to-all-start.1) | async-done | bytes 786464 | tf_op jit(solution)/shard_map/all_to_all | solution.py:67
  103.5 11.8 %gather_fusion.1 = f32[2048]{0:T(1024)S(1)} fusion(f32[65536]{0:T(1024)S(1)} %bitcast.132, s32[2048]{0:T(1024)S(1)} %get-tuple-element.7), kind=kCustom, calls=%fused_computation.1 | custom fusion | bytes 24576 | tf_op jit(solution)/shard_map/jit(_take)/gather | solution.py:74
  115.3 11.5 %scatter_custom_fusion = f32[65536]{0:T(1024)S(1)} fusion(s32[2048]{0:T(1024)S(1)} %get-tuple-element.8, f32[2048]{0:T(1024)S(1)} %select_subtract_fusion, f32[]{:T(128)} %constant.36.clone.1), kind=kCustom, calls=%fused_computation.165 | custom fusion | flops 2048 | bytes 262148 | tf_op jit(solution)/shard_map/scatter-add | solution.py:79
  126.9 56.7 %fusion.13 = f32[1,16,4096]{2,1,0:T(8,128)S(1)} fusion(f32[16,4096]{1,0:T(8,128)S(1)} %reshape.467), kind=kOutput, calls=%fused_computation.17 | convolution fusion | flops 3338665984 | bytes 524288 | tf_op jit(solution)/shard_map/dot_general | solution.py:81
  183.6 5.2 %collective-permute-start.1 = (f32[1,8,4096]{2,1,0:T(8,128)S(1)}, f32[1,8,4096]{2,1,0:T(8,128)S(1)}, u32[]{:S(2)}, u32[]{:S(2)}) collective-permute-start(f32[1,8,4096]{2,1,0:T(8,128)S(1)} %get-tuple-element.82), channel_id=1, source_target_pairs={{1,0},{2,1},{3,2},{4,3},{5,4},{6,5},{7,6},{9,8},{10,9},{11,10},{12... | collective-permute-start | bytes 393224 | tf_op jit(solution)/shard_map/ppermute | solution.py:25
  191.3 8.0 %collective-permute-done = f32[1,8,4096]{2,1,0:T(8,128)S(1)} collective-permute-done((f32[1,8,4096]{2,1,0:T(8,128)S(1)}, f32[1,8,4096]{2,1,0:T(8,128)S(1)}, u32[]{:S(2)}, u32[]{:S(2)}) %collective-permute-start) | collective-permute-done | bytes 131104 | tf_op jit(solution)/shard_map/ppermute | solution.py:23
  199.8 1.9 collective-permute-start.3
  201.7 3.9 %collective-permute-start.2 = (f32[1,3,2,4096]{3,2,1,0:T(2,128)S(1)}, f32[1,3,2,4096]{3,2,1,0:T(2,128)S(1)}, u32[]{:S(2)}, u32[]{:S(2)}) collective-permute-start(f32[1,3,2,4096]{3,2,1,0:T(2,128)S(1)} %get-tuple-element.41), channel_id=1, source_target_pairs={{0,1},{1,2},{2,3},{3,4},{4,5},{5,6},{6,7},{8,9},{9,10},{10,11},{11... | collective-permute-start | bytes 294920 | tf_op jit(solution)/shard_map/ppermute | solution.py:23
  206.3 5.5 %collective-permute-done.2 = f32[1,3,2,4096]{3,2,1,0:T(2,128)S(1)} collective-permute-done((f32[1,3,2,4096]{3,2,1,0:T(2,128)S(1)}, f32[1,3,2,4096]{3,2,1,0:T(2,128)S(1)}, u32[]{:S(2)}, u32[]{:S(2)}) %collective-permute-start.2) | collective-permute-done | bytes 98336 | tf_op jit(solution)/shard_map/ppermute | solution.py:23
  215.3 3.9 %collective-permute-start.6 = (f32[1,3,2,4096]{3,2,1,0:T(2,128)S(1)}, f32[1,3,2,4096]{3,2,1,0:T(2,128)S(1)}, u32[]{:S(2)}, u32[]{:S(2)}) collective-permute-start(f32[1,3,2,4096]{3,2,1,0:T(2,128)S(1)} %get-tuple-element.39), channel_id=1, source_target_pairs={{0,1},{1,2},{2,3},{3,4},{4,5},{5,6},{6,7},{8,9},{9,10},{10,11},{11... | collective-permute-start | bytes 294920 | tf_op jit(solution)/shard_map/ppermute | solution.py:23
  219.8 5.5 %collective-permute-done.6 = f32[1,3,2,4096]{3,2,1,0:T(2,128)S(1)} collective-permute-done((f32[1,3,2,4096]{3,2,1,0:T(2,128)S(1)}, f32[1,3,2,4096]{3,2,1,0:T(2,128)S(1)}, u32[]{:S(2)}, u32[]{:S(2)}) %collective-permute-start.6) | collective-permute-done | bytes 98336 | tf_op jit(solution)/shard_map/ppermute | solution.py:23
  228.8 4.1 %collective-permute-start.8 = (f32[1,3,2,4096]{3,2,1,0:T(2,128)S(1)}, f32[1,3,2,4096]{3,2,1,0:T(2,128)S(1)}, u32[]{:S(2)}, u32[]{:S(2)}) collective-permute-start(f32[1,3,2,4096]{3,2,1,0:T(2,128)S(1)} %get-tuple-element.37), channel_id=1, source_target_pairs={{0,1},{1,2},{2,3},{3,4},{4,5},{5,6},{6,7},{8,9},{9,10},{10,11},{11... | collective-permute-start | bytes 294920 | tf_op jit(solution)/shard_map/ppermute | solution.py:23
  233.4 5.5 %collective-permute-done.8 = f32[1,3,2,4096]{3,2,1,0:T(2,128)S(1)} collective-permute-done((f32[1,3,2,4096]{3,2,1,0:T(2,128)S(1)}, f32[1,3,2,4096]{3,2,1,0:T(2,128)S(1)}, u32[]{:S(2)}, u32[]{:S(2)}) %collective-permute-start.8) | collective-permute-done | bytes 98336 | tf_op jit(solution)/shard_map/ppermute | solution.py:23
  242.3 3.9 %collective-permute-start.10 = (f32[1,3,2,4096]{3,2,1,0:T(2,128)S(1)}, f32[1,3,2,4096]{3,2,1,0:T(2,128)S(1)}, u32[]{:S(2)}, u32[]{:S(2)}) collective-permute-start(f32[1,3,2,4096]{3,2,1,0:T(2,128)S(1)} %get-tuple-element.35), channel_id=1, source_target_pairs={{0,1},{1,2},{2,3},{3,4},{4,5},{5,6},{6,7},{8,9},{9,10},{10,11},{11... | collective-permute-start | bytes 294920 | tf_op jit(solution)/shard_map/ppermute | solution.py:23
  246.9 5.5 %collective-permute-done.10 = f32[1,3,2,4096]{3,2,1,0:T(2,128)S(1)} collective-permute-done((f32[1,3,2,4096]{3,2,1,0:T(2,128)S(1)}, f32[1,3,2,4096]{3,2,1,0:T(2,128)S(1)}, u32[]{:S(2)}, u32[]{:S(2)}) %collective-permute-start.10) | collective-permute-done | bytes 98336 | tf_op jit(solution)/shard_map/ppermute | solution.py:23
  (89 shorter events, 23.3 us)
Async XLA Ops:
  16.0 10.2 %copy-start.4 = (u32[256]{0:T(256)S(1)}, u32[256]{0:T(256)}, u32[]{:S(2)}) copy-start(u32[256]{0:T(256)} %constant.82) | copy-start | bytes 3076
  16.0 40.1 %all-to-all-start = ((f32[32,1,6144]{2,1,0:T(1,128)}), f32[32,1,6144]{2,1,0:T(1,128)S(1)}, u32[]{:S(2)}, u32[]{:S(2)}) async-start(f32[32,1,6144]{2,1,0:T(1,128)} %reshape.512), calls=%async_computation | async-start | bytes 1572864 | tf_op jit(solution)/shard_map/all_to_all | solution.py:65
  74.3 5.7 %copy-start = (f32[16,4096]{1,0:T(8,128)S(1)}, f32[16,4096]{1,0:T(8,128)}, u32[]{:S(2)}) copy-start(f32[16,4096]{1,0:T(8,128)} %param.8) | copy-start | bytes 786436
  74.3 12.8 %copy-start.1 = (s32[2048]{0:T(1024)S(1)}, s32[2048]{0:T(1024)}, u32[]{:S(2)}) copy-start(s32[2048]{0:T(1024)} %param.10) | copy-start | bytes 24580
  74.3 12.8 %copy-start.2 = (s32[2048]{0:T(1024)S(1)}, s32[2048]{0:T(1024)}, u32[]{:S(2)}) copy-start(s32[2048]{0:T(1024)} %param.9) | copy-start | bytes 24580
  74.3 29.0 %all-to-all-start.1 = ((f32[32,3,16,128]{3,2,1,0:T(8,128)}), f32[32,3,16,128]{3,2,1,0:T(8,128)S(1)}, u32[]{:S(2)}, u32[]{:S(2)}) async-start(f32[32,3,16,128]{3,2,1,0:T(8,128)} %broadcast_select_fusion), calls=%async_computation.1 | async-start | bytes 1572864 | tf_op jit(solution)/shard_map/all_to_all | solution.py:67
  80.0 132.0 %collective-permute-start.5 = (f32[8,4096]{1,0:T(8,128)S(1)}, f32[8,4096]{1,0:T(8,128)S(1)}, u32[]{:S(2)}, u32[]{:S(2)}) collective-permute-start(f32[8,4096]{1,0:T(8,128)S(1)} %get-tuple-element.80), channel_id=1, source_target_pairs={{1,0},{2,1},{3,2},{4,3},{5,4},{6,5},{7,6},{9,8},{10,9},{11,10},{12... | collective-permute-start | bytes 393224 | tf_op jit(solution)/shard_map/ppermute | solution.py:25
  85.2 126.8 %collective-permute-start.4 = (f32[8,4096]{1,0:T(8,128)S(1)}, f32[8,4096]{1,0:T(8,128)S(1)}, u32[]{:S(2)}, u32[]{:S(2)}) collective-permute-start(f32[8,4096]{1,0:T(8,128)S(1)} %get-tuple-element.79), channel_id=1, source_target_pairs={{0,1},{1,2},{2,3},{3,4},{4,5},{5,6},{6,7},{8,9},{9,10},{10,11},{11... | collective-permute-start | bytes 393224 | tf_op jit(solution)/shard_map/ppermute | solution.py:23
  103.5 11.8 %copy-start.3 = (f32[2048]{0:T(1024)S(1)}, f32[2048]{0:T(1024)}, u32[]{:S(2)}) copy-start(f32[2048]{0:T(1024)} %param.11) | copy-start | bytes 24580
  183.6 7.7 %collective-permute-start.1 = (f32[1,8,4096]{2,1,0:T(8,128)S(1)}, f32[1,8,4096]{2,1,0:T(8,128)S(1)}, u32[]{:S(2)}, u32[]{:S(2)}) collective-permute-start(f32[1,8,4096]{2,1,0:T(8,128)S(1)} %get-tuple-element.82), channel_id=1, source_target_pairs={{1,0},{2,1},{3,2},{4,3},{5,4},{6,5},{7,6},{9,8},{10,9},{11,10},{12... | collective-permute-start | bytes 393224 | tf_op jit(solution)/shard_map/ppermute | solution.py:25
  188.8 10.5 %collective-permute-start = (f32[1,8,4096]{2,1,0:T(8,128)S(1)}, f32[1,8,4096]{2,1,0:T(8,128)S(1)}, u32[]{:S(2)}, u32[]{:S(2)}) collective-permute-start(f32[1,8,4096]{2,1,0:T(8,128)S(1)} %get-tuple-element.81), channel_id=1, source_target_pairs={{0,1},{1,2},{2,3},{3,4},{4,5},{5,6},{6,7},{8,9},{9,10},{10,11},{11... | collective-permute-start | bytes 393224 | tf_op jit(solution)/shard_map/ppermute | solution.py:23
  199.8 6.5 %collective-permute-start.3 = (f32[1,3,2,4096]{3,2,1,0:T(2,128)S(1)}, f32[1,3,2,4096]{3,2,1,0:T(2,128)S(1)}, u32[]{:S(2)}, u32[]{:S(2)}) collective-permute-start(f32[1,3,2,4096]{3,2,1,0:T(2,128)S(1)} %get-tuple-element.42), channel_id=1, source_target_pairs={{1,0},{2,1},{3,2},{4,3},{5,4},{6,5},{7,6},{9,8},{10,9},{11,10},{12... | collective-permute-start | bytes 294920 | tf_op jit(solution)/shard_map/ppermute | solution.py:25
  201.7 10.1 %collective-permute-start.2 = (f32[1,3,2,4096]{3,2,1,0:T(2,128)S(1)}, f32[1,3,2,4096]{3,2,1,0:T(2,128)S(1)}, u32[]{:S(2)}, u32[]{:S(2)}) collective-permute-start(f32[1,3,2,4096]{3,2,1,0:T(2,128)S(1)} %get-tuple-element.41), channel_id=1, source_target_pairs={{0,1},{1,2},{2,3},{3,4},{4,5},{5,6},{6,7},{8,9},{9,10},{10,11},{11... | collective-permute-start | bytes 294920 | tf_op jit(solution)/shard_map/ppermute | solution.py:23
  213.3 6.5 %collective-permute-start.7 = (f32[1,3,2,4096]{3,2,1,0:T(2,128)S(1)}, f32[1,3,2,4096]{3,2,1,0:T(2,128)S(1)}, u32[]{:S(2)}, u32[]{:S(2)}) collective-permute-start(f32[1,3,2,4096]{3,2,1,0:T(2,128)S(1)} %get-tuple-element.40), channel_id=1, source_target_pairs={{1,0},{2,1},{3,2},{4,3},{5,4},{6,5},{7,6},{9,8},{10,9},{11,10},{12... | collective-permute-start | bytes 294920 | tf_op jit(solution)/shard_map/ppermute | solution.py:25
  215.3 10.1 %collective-permute-start.6 = (f32[1,3,2,4096]{3,2,1,0:T(2,128)S(1)}, f32[1,3,2,4096]{3,2,1,0:T(2,128)S(1)}, u32[]{:S(2)}, u32[]{:S(2)}) collective-permute-start(f32[1,3,2,4096]{3,2,1,0:T(2,128)S(1)} %get-tuple-element.39), channel_id=1, source_target_pairs={{0,1},{1,2},{2,3},{3,4},{4,5},{5,6},{6,7},{8,9},{9,10},{10,11},{11... | collective-permute-start | bytes 294920 | tf_op jit(solution)/shard_map/ppermute | solution.py:23
  226.8 6.5 %collective-permute-start.9 = (f32[1,3,2,4096]{3,2,1,0:T(2,128)S(1)}, f32[1,3,2,4096]{3,2,1,0:T(2,128)S(1)}, u32[]{:S(2)}, u32[]{:S(2)}) collective-permute-start(f32[1,3,2,4096]{3,2,1,0:T(2,128)S(1)} %get-tuple-element.38), channel_id=1, source_target_pairs={{1,0},{2,1},{3,2},{4,3},{5,4},{6,5},{7,6},{9,8},{10,9},{11,10},{12... | collective-permute-start | bytes 294920 | tf_op jit(solution)/shard_map/ppermute | solution.py:25
  228.8 10.1 %collective-permute-start.8 = (f32[1,3,2,4096]{3,2,1,0:T(2,128)S(1)}, f32[1,3,2,4096]{3,2,1,0:T(2,128)S(1)}, u32[]{:S(2)}, u32[]{:S(2)}) collective-permute-start(f32[1,3,2,4096]{3,2,1,0:T(2,128)S(1)} %get-tuple-element.37), channel_id=1, source_target_pairs={{0,1},{1,2},{2,3},{3,4},{4,5},{5,6},{6,7},{8,9},{9,10},{10,11},{11... | collective-permute-start | bytes 294920 | tf_op jit(solution)/shard_map/ppermute | solution.py:23
  240.4 6.5 %collective-permute-start.11 = (f32[1,3,2,4096]{3,2,1,0:T(2,128)S(1)}, f32[1,3,2,4096]{3,2,1,0:T(2,128)S(1)}, u32[]{:S(2)}, u32[]{:S(2)}) collective-permute-start(f32[1,3,2,4096]{3,2,1,0:T(2,128)S(1)} %get-tuple-element.36), channel_id=1, source_target_pairs={{1,0},{2,1},{3,2},{4,3},{5,4},{6,5},{7,6},{9,8},{10,9},{11,10},{12... | collective-permute-start | bytes 294920 | tf_op jit(solution)/shard_map/ppermute | solution.py:25
  242.3 10.1 %collective-permute-start.10 = (f32[1,3,2,4096]{3,2,1,0:T(2,128)S(1)}, f32[1,3,2,4096]{3,2,1,0:T(2,128)S(1)}, u32[]{:S(2)}, u32[]{:S(2)}) collective-permute-start(f32[1,3,2,4096]{3,2,1,0:T(2,128)S(1)} %get-tuple-element.35), channel_id=1, source_target_pairs={{0,1},{1,2},{2,3},{3,4},{4,5},{5,6},{6,7},{8,9},{9,10},{10,11},{11... | collective-permute-start | bytes 294920 | tf_op jit(solution)/shard_map/ppermute | solution.py:23
where the time goes:
time: 256 us; the launch traced here: 255 us
  matrix products  57.1 us (22%)
  starting transfers between devices  52.9 us (21%)
  waiting for transfers between devices  49 us (19%)
  local copies, waits for them, and re-layouts  46.4 us (18%)
  blocking collectives  28.7 us (11%)
  other arithmetic  19.4 us (8%)
    dot_general x1, matrix products, on_device(): jnp.dot(scattered.reshape(local_count * band_rows, columns), col_kernel,...  56.7 us
    ppermute x6, waiting for transfers between devices, extended(): lax.ppermute(tail, axis, [(i, (i + 1) % count) for i in range(ends)])  30.1 us
    unnamed x1, blocking collectives  28.7 us
    unnamed x17, local copies, waits for them, and re-layouts  24.4 us
    ppermute x6, starting transfers between devices, extended(): lax.ppermute(tail, axis, [(i, (i + 1) % count) for i in range(ends)])  19.7 us
    ppermute x6, starting transfers between devices, extended(): lax.ppermute(head, axis, [((i + 1) % count, i) for i in range(ends)])  18 us
    all_to_all x1, waiting for transfers between devices, on_device(): lax.all_to_all(chosen, 'dom', split_axis=0, concat_axis=3, tiled=True)  16.2 us
    gather x1, local copies, waits for them, and re-layouts, on_device(): jnp.take(height.reshape(local_count, band_rows * columns), position, axis=1)  11.8 us
  transfers between devices with their start and end apart: 14, of which 11 were waited for; matrix products, arithmetic and copies ran while one was open for 32% of the time, Pallas kernels for 0%

commit v1 on v0

v1 whole, which is shorter than its diff:
```python
import numpy as np
import jax
import jax.numpy as jnp
from jax import lax
from jax.sharding import PartitionSpec as P

STEPS = 4
BW = 8


TIME_STEP = 0.8
NUDGE_GAIN = 0.5
LENGTH_SCALE = 3.0


def weights():
    return [np.float32(np.exp(np.float32(-abs(o) / LENGTH_SCALE))) for o in range(-BW, BW + 1)]


def smooth(field, axis_no):
    count = field.shape[axis_no]
    widths = [(0, 0)] * field.ndim
    widths[axis_no] = (BW, BW)
    padded = jnp.pad(field, widths)
    total = jnp.zeros_like(field)
    for offset, weight in zip(range(-BW, BW + 1), weights()):
        piece = lax.slice_in_dim(padded, BW + offset, BW + offset + count, axis=axis_no)
        total = total + weight * piece
    return total


def shift_rows(q, d):
    if d > 0:
        return jnp.concatenate([q[d:], jnp.zeros_like(q[:d])], axis=0)
    return jnp.concatenate([jnp.zeros_like(q[:(-d)]), q[:d]], axis=0)


def advance(height, east_vel, north_vel, depth, coriolis, inside):
    flux_east = depth * east_vel
    flux_north = depth * north_vel
    east_diff = 0.5 * (jnp.roll(flux_east, -1, -1) - jnp.roll(flux_east, 1, -1))
    north_diff = 0.5 * (shift_rows(flux_north, 1) - shift_rows(flux_north, -1))
    new_height = jnp.where(inside, height - TIME_STEP * (east_diff + north_diff), jnp.float32(0.0))
    slope_east = 0.5 * (jnp.roll(new_height, -1, -1) - jnp.roll(new_height, 1, -1))
    slope_north = 0.5 * (shift_rows(new_height, 1) - shift_rows(new_height, -1))
    new_east = east_vel + TIME_STEP * (coriolis * north_vel - slope_east)
    new_north = north_vel + TIME_STEP * (-coriolis * east_vel - slope_north)
    return new_height, new_east, new_north


def on_device(ensemble, ancestors, sea_depth, obs_rows, obs_cols, obs_values):
    _, fields, rows, columns = ensemble.shape
    parts = lax.axis_size("dom")
    bands = lax.axis_size("band")
    band = lax.axis_index("band")
    down = [(i, i + 1) for i in range(bands - 1)]
    up = [(i + 1, i) for i in range(bands - 1)]
    margin = 2 * STEPS

    block = ensemble.reshape(fields * rows, parts, columns // parts).transpose(1, 0, 2)
    lineage = lax.all_gather(ancestors, "dom", axis=0, tiled=True)
    crossed = lax.all_to_all(block, "dom", 0, 0, tiled=True)
    chosen = jnp.take(crossed, lineage, axis=0)
    back = lax.all_to_all(chosen, "dom", 0, 0, tiled=True)
    state = back.transpose(1, 0, 2).reshape(fields, rows, columns)

    band_start = band * rows
    position = (obs_rows - band_start) * columns + obs_cols
    observed = jnp.zeros((rows * columns,), jnp.bool_).at[position].set(True).reshape(rows, columns)
    values = jnp.zeros((rows * columns,), jnp.float32).at[position].set(obs_values).reshape(rows, columns)

    depth_ext = jnp.concatenate(
        [
            lax.ppermute(sea_depth[rows - margin:], "band", down),
            sea_depth,
            lax.ppermute(sea_depth[:margin], "band", up),
        ],
        axis=0,
    )

    height, east_vel, north_vel = state[0], state[1], state[2]
    scattered = jnp.where(observed, values - height, jnp.float32(0.0))
    spread = smooth(scattered, 1)

    to_below = jnp.concatenate(
        [spread, height[rows - margin:], east_vel[rows - margin:], north_vel[rows - margin:]], axis=0
    )
    to_above = jnp.concatenate(
        [spread, height[:margin], east_vel[:margin], north_vel[:margin]], axis=0
    )
    from_above = lax.ppermute(to_below, "band", down)
    from_below = lax.ppermute(to_above, "band", up)

    spread_ext = jnp.concatenate([from_above[:rows], spread, from_below[:rows]], axis=0)
    increment = smooth(spread_ext, 0)[rows - margin: 2 * rows + margin]

    def ext(i, own):
        lo = rows + i * margin
        return jnp.concatenate([from_above[lo:lo + margin], own, from_below[lo:lo + margin]], axis=0)

    height = ext(0, height) + NUDGE_GAIN * increment
    east_vel = ext(1, east_vel)
    north_vel = ext(2, north_vel)

    total_rows = rows * bands
    global_rows = band_start - margin + jnp.arange(rows + 2 * margin)
    inside = ((global_rows >= 0) & (global_rows < total_rows))[:, None]
    coriolis = (0.1 + 0.4 * ((global_rows.astype(jnp.float32) + 0.5) / total_rows))[:, None]
    for _ in range(STEPS):
        height, east_vel, north_vel = advance(height, east_vel, north_vel, depth_ext, coriolis, inside)
    out = jnp.stack([height, east_vel, north_vel], axis=0)[:, margin:margin + rows]
    return out[None]


def solution(mesh):
    placed = (
        P("dom", None, "band", None),
        P("dom"),
        P("band", None),
        P("band"),
        P("band"),
        P("band"),
    )
    return jax.shard_map(
        on_device,
        mesh=mesh,
        in_specs=placed,
        out_specs=P("dom", None, "band", None),
        check_vma=False,
    )
```

time: 256 us -> 110 us (0.43)
  matrix products: 57.1 us -> 0 us
  waiting for transfers between devices: 49 us -> 24.4 us
  starting transfers between devices: 52.9 us -> 31.7 us
  local copies, waits for them, and re-layouts: 46.4 us -> 26.9 us
  other arithmetic: 19.4 us -> 7.37 us
  blocking collectives: 28.7 us -> 18.3 us
    dot_general x2 -> x0, matrix products: 57.1 us -> none  [the longest x1 56.7 us: on_device(): jnp.dot(scattered.reshape(local_count * band_rows, columns), col_kernel,...]
    ppermute x12 -> x4, starting transfers between devices: 37.8 us -> 16.7 us  [the longest x1 5.97 us: on_device(): lax.ppermute(sea_depth[:margin], 'band', up)]
    unnamed x17 -> x16, local copies, waits for them, and re-layouts: 24.4 us -> 3.45 us
    scatter x0 -> x2, local copies, waits for them, and re-layouts: none -> 17.5 us  [the longest x1 9.19 us: on_device(): jnp.zeros((rows * columns,), jnp.bool_).at[position].set(True)]
    ppermute x12 -> x4, waiting for transfers between devices: 32.8 us -> 18.9 us  [the longest x1 11.2 us: on_device(): from_below = lax.ppermute(to_above, 'band', up)]
    gather x1 -> x0, local copies, waits for them, and re-layouts: 11.8 us -> none  [on_device(): jnp.take(height.reshape(local_count, band_rows * columns), position, axis=1)]
    scatter-add x1 -> x0, other arithmetic: 11.5 us -> none  [on_device(): jnp.zeros((local_count, band_rows * columns), jnp.float32).at[:, position]]
    all_to_all x2, waiting for transfers between devices: 16.2 us -> 5.57 us  [the longest x1 5.56 us: on_device(): back = lax.all_to_all(chosen, 'dom', 0, 0, tiled=True)]
  transfers between devices with their start and end apart: 14 -> 6, of which waited for: 11 -> 3; matrix products, arithmetic and copies ran while one was open for 32% -> 19% of each run, Pallas kernels for 0% -> 0%
where the time goes in v1:
time: 110 us
  starting transfers between devices  31.7 us (29%)
  local copies, waits for them, and re-layouts  26.9 us (24%)
  waiting for transfers between devices  24.4 us (22%)
  blocking collectives  18.3 us (17%)
  other arithmetic  7.37 us (7%)
    unnamed x1, blocking collectives  18.3 us
    ppermute x1, waiting for transfers between devices, on_device(): from_below = lax.ppermute(to_above, 'band', up)  11.2 us
    all_to_all x1, starting transfers between devices, on_device(): crossed = lax.all_to_all(block, 'dom', 0, 0, tiled=True)  9.49 us
    scatter x1, local copies, waits for them, and re-layouts, on_device(): jnp.zeros((rows * columns,), jnp.bool_).at[position].set(True)  9.19 us
    scatter x1, local copies, waits for them, and re-layouts, on_device(): jnp.zeros((rows * columns,), jnp.float32).at[position].set(obs_values)  8.3 us
    ppermute x1, waiting for transfers between devices, on_device(): from_above = lax.ppermute(to_below, 'band', down)  7.7 us
    ppermute x1, starting transfers between devices, on_device(): lax.ppermute(sea_depth[:margin], 'band', up)  5.97 us
    all_to_all x1, waiting for transfers between devices, on_device(): back = lax.all_to_all(chosen, 'dom', 0, 0, tiled=True)  5.56 us
  transfers between devices with their start and end apart: 6, of which 3 were waited for; matrix products, arithmetic and copies ran while one was open for 19% of the time, Pallas kernels for 0%

profile of v1, /device:TPU:36, one launch (start us, length us, event | category | flops | bytes accessed | tf_op | source)
XLA Modules:
  0.0 109.8 jit_solution(4158186565284987038)
XLA Ops:
  0.0 1.3 %copy.17 = f32[6,8,32,128]{3,2,1,0:T(8,128)S(1)} copy(f32[6,8,32,128]{3,1,2,0:T(8,128)} %bitcast.48) | data formatting | bytes 1572864
  1.3 1.3 %copy.24 = f32[48,32,128]{2,0,1:T(8,128)} copy(f32[48,32,128]{2,1,0:T(8,128)S(1)} %bitcast.46) | data formatting | bytes 1572864 | tf_op jit(solution)/shard_map/reshape | solution.py:60
  2.6 9.5 %all-to-all-start = ((f32[32,48,128]{2,1,0:T(8,128)}), f32[32,48,128]{2,1,0:T(8,128)S(1)}, u32[]{:S(2)}, u32[]{:S(2)}) async-start(f32[32,48,128]{2,1,0:T(8,128)} %bitcast.41), calls=%async_computation | async-start | bytes 1572864 | tf_op jit(solution)/shard_map/all_to_all | solution.py:62
  12.2 3.5 %collective-permute-start.2 = (f32[8,4096]{1,0:T(8,128)S(1)}, f32[8,4096]{1,0:T(8,128)S(1)}, u32[]{:S(2)}, u32[]{:S(2)}) collective-permute-start(f32[8,4096]{1,0:T(8,128)S(1)} %get-tuple-element.98), channel_id=1, source_target_pairs={{0,1},{1,2},{2,3},{3,4},{4,5},{5,6},{6,7},{8,9},{9,10},{10,11},{11... | collective-permute-start | bytes 393224 | tf_op jit(solution)/shard_map/ppermute | solution.py:74
  15.6 6.0 %collective-permute-start.3 = (f32[8,4096]{1,0:T(8,128)S(1)}, f32[8,4096]{1,0:T(8,128)S(1)}, u32[]{:S(2)}, u32[]{:S(2)}) collective-permute-start(f32[8,4096]{1,0:T(8,128)S(1)} %get-tuple-element.97), channel_id=1, source_target_pairs={{1,0},{2,1},{3,2},{4,3},{5,4},{6,5},{7,6},{9,8},{10,9},{11,10},{12... | collective-permute-start | bytes 393224 | tf_op jit(solution)/shard_map/ppermute | solution.py:76
  22.3 0.7 copy-done.4
  23.0 0.6 dynamic-slice
  23.6 0.8 dynamic-update-slice
  24.4 18.3 %all-reduce.18 = s32[32]{0:T(128)S(1)} all-reduce(s32[32]{0:T(128)S(1)} %dynamic-update-slice), channel_id=1, replica_groups=mesh['dom'=32,'band'=8] {'dom'}, use_global_device_ids=true, to_apply=%add.18 | all-reduce | flops 32 | bytes 256
  42.8 0.6 gather_fusion
  43.4 1.0 broadcast_select_fusion
  44.4 5.5 %all-to-all-start.1 = ((f32[32,48,128]{2,1,0:T(8,128)}), f32[32,48,128]{2,1,0:T(8,128)S(1)}, u32[]{:S(2)}, u32[]{:S(2)}) async-start(f32[32,48,128]{2,1,0:T(8,128)} %broadcast_select_fusion), calls=%async_computation.1 | async-start | bytes 1572864 | tf_op jit(solution)/shard_map/all_to_all | solution.py:64
  49.9 9.2 %scatter_custom_fusion = pred[65536]{0:T(1024)(128)(4,1)S(1)} fusion(s32[2048]{0:T(1024)S(1)} %compare_select_fusion, pred[2048]{0:T(1024)(128)(4,1)S(1)} %broadcast.165, pred[]{:T(512)} %constant.31.clone.1), kind=kCustom, calls=%fused_computation.150 | custom fusion | bytes 65537 | tf_op jit(solution)/shard_map/scatter | solution.py:69
  59.2 8.3 %scatter_custom_fusion.1 = f32[65536]{0:T(1024)S(1)} fusion(s32[2048]{0:T(1024)S(1)} %compare_select_fusion, f32[2048]{0:T(1024)} %param.11, f32[]{:T(128)} %constant.35.clone.1), kind=kCustom, calls=%fused_computation.148 | custom fusion | bytes 262656 | tf_op jit(solution)/shard_map/scatter | solution.py:70
  67.7 5.6 %all-to-all-done.1 = f32[32,48,128]{2,1,0:T(8,128)S(1)} async-done(((f32[32,48,128]{2,1,0:T(8,128)}), f32[32,48,128]{2,1,0:T(8,128)S(1)}, u32[]{:S(2)}, u32[]{:S(2)}) %all-to-all-start.1) | async-done | bytes 786464 | tf_op jit(solution)/shard_map/all_to_all | solution.py:64
  73.5 1.1 %multiply_add_fusion.3 = f32[16,4096]{1,0:T(8,128)S(1)} fusion(f32[16,4096]{1,0:T(8,128)S(1)} %subtract_select_fusion), kind=kLoop, calls=%fused_computation.118 | loop fusion | flops 2097152 | bytes 524288 | tf_op jit(solution)/shard_map/add | solution.py:28
  74.7 5.2 %collective-permute-start.1 = (f32[40,4096]{1,0:T(8,128)S(1)}, f32[40,4096]{1,0:T(8,128)S(1)}, u32[]{:S(2)}, u32[]{:S(2)}) collective-permute-start(f32[40,4096]{1,0:T(8,128)S(1)} %get-tuple-element.96), channel_id=1, source_target_pairs={{1,0},{2,1},{3,2},{4,3},{5,4},{6,5},{7,6},{9,8},{10,9},{11,10},{12... | collective-permute-start | bytes 1966088 | tf_op jit(solution)/shard_map/ppermute | solution.py:92
  79.9 2.1 %collective-permute-start = (f32[40,4096]{1,0:T(8,128)S(1)}, f32[40,4096]{1,0:T(8,128)S(1)}, u32[]{:S(2)}, u32[]{:S(2)}) collective-permute-start(f32[40,4096]{1,0:T(8,128)S(1)} %get-tuple-element.95), channel_id=1, source_target_pairs={{0,1},{1,2},{2,3},{3,4},{4,5},{5,6},{6,7},{8,9},{9,10},{10,11},{11... | collective-permute-start | bytes 1966088 | tf_op jit(solution)/shard_map/ppermute | solution.py:91
  82.0 11.2 %collective-permute-done.1 = f32[40,4096]{1,0:T(8,128)S(1)} collective-permute-done((f32[40,4096]{1,0:T(8,128)S(1)}, f32[40,4096]{1,0:T(8,128)S(1)}, u32[]{:S(2)}, u32[]{:S(2)}) %collective-permute-start.1) | collective-permute-done | bytes 655392 | tf_op jit(solution)/shard_map/ppermute | solution.py:92
  93.2 7.7 %collective-permute-done = f32[40,4096]{1,0:T(8,128)S(1)} collective-permute-done((f32[40,4096]{1,0:T(8,128)S(1)}, f32[40,4096]{1,0:T(8,128)S(1)}, u32[]{:S(2)}, u32[]{:S(2)}) %collective-permute-start) | collective-permute-done | bytes 655392 | tf_op jit(solution)/shard_map/ppermute | solution.py:91
  101.4 0.9 slice-done
  102.4 0.9 fusion.10
  103.4 0.5 fusion.30
  108.9 0.9 fusion.21
  (70 shorter events, 6.0 us)
Async XLA Ops:
  2.6 9.5 %copy-start = (f32[16,4096]{1,0:T(8,128)S(1)}, f32[16,4096]{1,0:T(8,128)}, u32[]{:S(2)}) copy-start(f32[16,4096]{1,0:T(8,128)} %param.8) | copy-start | bytes 786436
  2.6 40.1 %all-to-all-start = ((f32[32,48,128]{2,1,0:T(8,128)}), f32[32,48,128]{2,1,0:T(8,128)S(1)}, u32[]{:S(2)}, u32[]{:S(2)}) async-start(f32[32,48,128]{2,1,0:T(8,128)} %bitcast.41), calls=%async_computation | async-start | bytes 1572864 | tf_op jit(solution)/shard_map/all_to_all | solution.py:62
  12.2 55.4 %collective-permute-start.2 = (f32[8,4096]{1,0:T(8,128)S(1)}, f32[8,4096]{1,0:T(8,128)S(1)}, u32[]{:S(2)}, u32[]{:S(2)}) collective-permute-start(f32[8,4096]{1,0:T(8,128)S(1)} %get-tuple-element.98), channel_id=1, source_target_pairs={{0,1},{1,2},{2,3},{3,4},{4,5},{5,6},{6,7},{8,9},{9,10},{10,11},{11... | collective-permute-start | bytes 393224 | tf_op jit(solution)/shard_map/ppermute | solution.py:74
  15.6 52.0 %collective-permute-start.3 = (f32[8,4096]{1,0:T(8,128)S(1)}, f32[8,4096]{1,0:T(8,128)S(1)}, u32[]{:S(2)}, u32[]{:S(2)}) collective-permute-start(f32[8,4096]{1,0:T(8,128)S(1)} %get-tuple-element.97), channel_id=1, source_target_pairs={{1,0},{2,1},{3,2},{4,3},{5,4},{6,5},{7,6},{9,8},{10,9},{11,10},{12... | collective-permute-start | bytes 393224 | tf_op jit(solution)/shard_map/ppermute | solution.py:76
  22.3 0.7 copy-start.4
  23.6 19.1 %copy-start.3 = (s32[2048]{0:T(1024)S(1)}, s32[2048]{0:T(1024)}, u32[]{:S(2)}) copy-start(s32[2048]{0:T(1024)} %param.9) | copy-start | bytes 24580
  23.6 19.1 %copy-start.2 = (s32[2048]{0:T(1024)S(1)}, s32[2048]{0:T(1024)}, u32[]{:S(2)}) copy-start(s32[2048]{0:T(1024)} %param.10) | copy-start | bytes 24580
  44.4 28.9 %all-to-all-start.1 = ((f32[32,48,128]{2,1,0:T(8,128)}), f32[32,48,128]{2,1,0:T(8,128)S(1)}, u32[]{:S(2)}, u32[]{:S(2)}) async-start(f32[32,48,128]{2,1,0:T(8,128)} %broadcast_select_fusion), calls=%async_computation.1 | async-start | bytes 1572864 | tf_op jit(solution)/shard_map/all_to_all | solution.py:64
  74.7 18.5 %collective-permute-start.1 = (f32[40,4096]{1,0:T(8,128)S(1)}, f32[40,4096]{1,0:T(8,128)S(1)}, u32[]{:S(2)}, u32[]{:S(2)}) collective-permute-start(f32[40,4096]{1,0:T(8,128)S(1)} %get-tuple-element.96), channel_id=1, source_target_pairs={{1,0},{2,1},{3,2},{4,3},{5,4},{6,5},{7,6},{9,8},{10,9},{11,10},{12... | collective-permute-start | bytes 1966088 | tf_op jit(solution)/shard_map/ppermute | solution.py:92
  79.9 21.0 %collective-permute-start = (f32[40,4096]{1,0:T(8,128)S(1)}, f32[40,4096]{1,0:T(8,128)S(1)}, u32[]{:S(2)}, u32[]{:S(2)}) collective-permute-start(f32[40,4096]{1,0:T(8,128)S(1)} %get-tuple-element.95), channel_id=1, source_target_pairs={{0,1},{1,2},{2,3},{3,4},{4,5},{5,6},{6,7},{8,9},{9,10},{10,11},{11... | collective-permute-start | bytes 1966088 | tf_op jit(solution)/shard_map/ppermute | solution.py:91
  93.2 8.1 %copy-start.1 = (f32[40,4096]{1,0:T(8,128)}, f32[40,4096]{1,0:T(8,128)S(1)}, u32[]{:S(2)}) copy-start(f32[40,4096]{1,0:T(8,128)S(1)} %collective-permute-done.1) | copy-start | bytes 1966084
  101.4 1.0 slice-start

commit v2 on v1

--- a/solution.py
+++ b/solution.py
@@ -58,9 +58,10 @@
     margin = 2 * STEPS
 
     block = ensemble.reshape(fields * rows, parts, columns // parts).transpose(1, 0, 2)
-    lineage = lax.all_gather(ancestors, "dom", axis=0, tiled=True)
-    crossed = lax.all_to_all(block, "dom", 0, 0, tiled=True)
-    chosen = jnp.take(crossed, lineage, axis=0)
+    tag = jnp.broadcast_to(ancestors.astype(jnp.float32)[:, None, None], (parts, 8, columns // parts))
+    crossed = lax.all_to_all(jnp.concatenate([block, tag], axis=1), "dom", 0, 0, tiled=True)
+    lineage = crossed[:, fields * rows, 0].astype(jnp.int32)
+    chosen = jnp.take(crossed[:, :fields * rows], lineage, axis=0)
     back = lax.all_to_all(chosen, "dom", 0, 0, tiled=True)
     state = back.transpose(1, 0, 2).reshape(fields, rows, columns)
 

time: 110 us -> 105 us (0.955)
  blocking collectives: 18.3 us -> 0 us
  waiting for transfers between devices: 24.4 us -> 41 us
  local copies, waits for them, and re-layouts: 26.9 us -> 25 us
  starting transfers between devices: 31.7 us -> 29.9 us
    unnamed x1 -> x0, blocking collectives: 18.3 us -> none
    all_to_all x1, waiting for transfers between devices: 0.01 us -> 16.6 us  [on_device(): lax.all_to_all(jnp.concatenate([block, tag], axis=1), 'dom', 0, 0, tiled=...]
    unnamed x16 -> x12, local copies, waits for them, and re-layouts: 3.45 us -> 1.38 us
    all_to_all x1, starting transfers between devices: 5.52 us -> 3.7 us  [on_device(): back = lax.all_to_all(chosen, 'dom', 0, 0, tiled=True)]
  transfers between devices with their start and end apart: 6 -> 6, of which waited for: 3 -> 4; matrix products, arithmetic and copies ran while one was open for 19% -> 19% of each run, Pallas kernels for 0% -> 0%
where the time goes in v2:
time: 105 us
  waiting for transfers between devices  41 us (39%)
  starting transfers between devices  29.9 us (28%)
  local copies, waits for them, and re-layouts  25 us (24%)
  other arithmetic  8.02 us (8%)
  between operations  1.09 us (1%)
    all_to_all x1, waiting for transfers between devices, on_device(): lax.all_to_all(jnp.concatenate([block, tag], axis=1), 'dom', 0, 0, tiled=...  16.6 us
    ppermute x1, waiting for transfers between devices, on_device(): from_below = lax.ppermute(to_above, 'band', up)  11.2 us
    all_to_all x1, starting transfers between devices, on_device(): lax.all_to_all(jnp.concatenate([block, tag], axis=1), 'dom', 0, 0, tiled=...  9.49 us
    scatter x1, local copies, waits for them, and re-layouts, on_device(): jnp.zeros((rows * columns,), jnp.bool_).at[position].set(True)  9.19 us
    scatter x1, local copies, waits for them, and re-layouts, on_device(): jnp.zeros((rows * columns,), jnp.float32).at[position].set(obs_values)  8.3 us
    ppermute x1, waiting for transfers between devices, on_device(): from_above = lax.ppermute(to_below, 'band', down)  7.7 us
    ppermute x1, starting transfers between devices, on_device(): lax.ppermute(sea_depth[:margin], 'band', up)  5.97 us
    all_to_all x1, waiting for transfers between devices, on_device(): back = lax.all_to_all(chosen, 'dom', 0, 0, tiled=True)  5.51 us
  transfers between devices with their start and end apart: 6, of which 4 were waited for; matrix products, arithmetic and copies ran while one was open for 19% of the time, Pallas kernels for 0%

profile of v2, /device:TPU:36, one launch (start us, length us, event | category | flops | bytes accessed | tf_op | source)
XLA Modules:
  0.0 105.0 jit_solution(13259181660827438382)
XLA Ops:
  0.0 1.3 %copy.24 = f32[6,8,32,128]{3,2,1,0:T(8,128)S(1)} copy(f32[6,8,32,128]{3,1,2,0:T(8,128)} %bitcast.53) | data formatting | bytes 1572864
  1.3 0.5 copy.31
  2.4 1.0 concatenate.122
  3.4 9.5 %all-to-all-start = ((f32[32,56,128]{2,1,0:T(8,128)}), f32[32,56,128]{2,1,0:T(8,128)S(1)}, u32[]{:S(2)}, u32[]{:S(2)}) async-start(f32[32,56,128]{2,1,0:T(8,128)} %concatenate.122), calls=%async_computation | async-start | bytes 1835008 | tf_op jit(solution)/shard_map/all_to_all | solution.py:62
  12.9 3.5 %collective-permute-start.2 = (f32[8,4096]{1,0:T(8,128)S(1)}, f32[8,4096]{1,0:T(8,128)S(1)}, u32[]{:S(2)}, u32[]{:S(2)}) collective-permute-start(f32[8,4096]{1,0:T(8,128)S(1)} %get-tuple-element.98), channel_id=1, source_target_pairs={{0,1},{1,2},{2,3},{3,4},{4,5},{5,6},{6,7},{8,9},{9,10},{10,11},{11... | collective-permute-start | bytes 393224 | tf_op jit(solution)/shard_map/ppermute | solution.py:75
  16.4 6.0 %collective-permute-start.3 = (f32[8,4096]{1,0:T(8,128)S(1)}, f32[8,4096]{1,0:T(8,128)S(1)}, u32[]{:S(2)}, u32[]{:S(2)}) collective-permute-start(f32[8,4096]{1,0:T(8,128)S(1)} %get-tuple-element.97), channel_id=1, source_target_pairs={{1,0},{2,1},{3,2},{4,3},{5,4},{6,5},{7,6},{9,8},{10,9},{11,10},{12... | collective-permute-start | bytes 393224 | tf_op jit(solution)/shard_map/ppermute | solution.py:77
  22.5 16.6 %all-to-all-done = f32[32,56,128]{2,1,0:T(8,128)S(1)} async-done(((f32[32,56,128]{2,1,0:T(8,128)}), f32[32,56,128]{2,1,0:T(8,128)S(1)}, u32[]{:S(2)}, u32[]{:S(2)}) %all-to-all-start) | async-done | bytes 917536 | tf_op jit(solution)/shard_map/all_to_all | solution.py:62
  39.0 0.7 fusion.85
  39.8 0.6 gather_fusion
  40.4 1.0 broadcast_select_fusion
  41.4 3.7 %all-to-all-start.1 = ((f32[32,48,128]{2,1,0:T(8,128)}), f32[32,48,128]{2,1,0:T(8,128)S(1)}, u32[]{:S(2)}, u32[]{:S(2)}) async-start(f32[32,48,128]{2,1,0:T(8,128)} %broadcast_select_fusion), calls=%async_computation.1 | async-start | bytes 1572864 | tf_op jit(solution)/shard_map/all_to_all | solution.py:65
  45.1 9.2 %scatter_custom_fusion = pred[65536]{0:T(1024)(128)(4,1)S(1)} fusion(s32[2048]{0:T(1024)S(1)} %compare_select_fusion, pred[2048]{0:T(1024)(128)(4,1)S(1)} %broadcast.188, pred[]{:T(512)} %constant.31.clone.1), kind=kCustom, calls=%fused_computation.150 | custom fusion | bytes 65537 | tf_op jit(solution)/shard_map/scatter | solution.py:70
  54.4 8.3 %scatter_custom_fusion.1 = f32[65536]{0:T(1024)S(1)} fusion(s32[2048]{0:T(1024)S(1)} %compare_select_fusion, f32[2048]{0:T(1024)} %param.11, f32[]{:T(128)} %constant.35.clone.1), kind=kCustom, calls=%fused_computation.148 | custom fusion | bytes 262656 | tf_op jit(solution)/shard_map/scatter | solution.py:71
  62.9 5.5 %all-to-all-done.1 = f32[32,48,128]{2,1,0:T(8,128)S(1)} async-done(((f32[32,48,128]{2,1,0:T(8,128)}), f32[32,48,128]{2,1,0:T(8,128)S(1)}, u32[]{:S(2)}, u32[]{:S(2)}) %all-to-all-start.1) | async-done | bytes 786464 | tf_op jit(solution)/shard_map/all_to_all | solution.py:65
  68.6 1.1 %multiply_add_fusion.3 = f32[16,4096]{1,0:T(8,128)S(1)} fusion(f32[16,4096]{1,0:T(8,128)S(1)} %subtract_select_fusion), kind=kLoop, calls=%fused_computation.118 | loop fusion | flops 2097152 | bytes 524288 | tf_op jit(solution)/shard_map/add | solution.py:28
  69.9 5.2 %collective-permute-start.1 = (f32[40,4096]{1,0:T(8,128)S(1)}, f32[40,4096]{1,0:T(8,128)S(1)}, u32[]{:S(2)}, u32[]{:S(2)}) collective-permute-start(f32[40,4096]{1,0:T(8,128)S(1)} %get-tuple-element.96), channel_id=1, source_target_pairs={{1,0},{2,1},{3,2},{4,3},{5,4},{6,5},{7,6},{9,8},{10,9},{11,10},{12... | collective-permute-start | bytes 1966088 | tf_op jit(solution)/shard_map/ppermute | solution.py:93
  75.0 2.1 %collective-permute-start = (f32[40,4096]{1,0:T(8,128)S(1)}, f32[40,4096]{1,0:T(8,128)S(1)}, u32[]{:S(2)}, u32[]{:S(2)}) collective-permute-start(f32[40,4096]{1,0:T(8,128)S(1)} %get-tuple-element.95), channel_id=1, source_target_pairs={{0,1},{1,2},{2,3},{3,4},{4,5},{5,6},{6,7},{8,9},{9,10},{10,11},{11... | collective-permute-start | bytes 1966088 | tf_op jit(solution)/shard_map/ppermute | solution.py:92
  77.2 11.2 %collective-permute-done.1 = f32[40,4096]{1,0:T(8,128)S(1)} collective-permute-done((f32[40,4096]{1,0:T(8,128)S(1)}, f32[40,4096]{1,0:T(8,128)S(1)}, u32[]{:S(2)}, u32[]{:S(2)}) %collective-permute-start.1) | collective-permute-done | bytes 655392 | tf_op jit(solution)/shard_map/ppermute | solution.py:93
  88.4 7.7 %collective-permute-done = f32[40,4096]{1,0:T(8,128)S(1)} collective-permute-done((f32[40,4096]{1,0:T(8,128)S(1)}, f32[40,4096]{1,0:T(8,128)S(1)}, u32[]{:S(2)}, u32[]{:S(2)}) %collective-permute-start) | collective-permute-done | bytes 655392 | tf_op jit(solution)/shard_map/ppermute | solution.py:92
  96.6 0.9 slice-done
  97.5 0.9 fusion.10
  98.6 0.5 fusion.30
  100.9 0.4 fusion.92
  104.0 0.9 fusion.21
  (67 shorter events, 5.7 us)
Async XLA Ops:
  3.4 9.5 %copy-start = (f32[16,4096]{1,0:T(8,128)S(1)}, f32[16,4096]{1,0:T(8,128)}, u32[]{:S(2)}) copy-start(f32[16,4096]{1,0:T(8,128)} %param.8) | copy-start | bytes 786436
  3.4 35.7 %all-to-all-start = ((f32[32,56,128]{2,1,0:T(8,128)}), f32[32,56,128]{2,1,0:T(8,128)S(1)}, u32[]{:S(2)}, u32[]{:S(2)}) async-start(f32[32,56,128]{2,1,0:T(8,128)} %concatenate.122), calls=%async_computation | async-start | bytes 1835008 | tf_op jit(solution)/shard_map/all_to_all | solution.py:62
  12.9 9.5 %copy-start.3 = (s32[2048]{0:T(1024)S(1)}, s32[2048]{0:T(1024)}, u32[]{:S(2)}) copy-start(s32[2048]{0:T(1024)} %param.9) | copy-start | bytes 24580
  12.9 9.5 %copy-start.2 = (s32[2048]{0:T(1024)S(1)}, s32[2048]{0:T(1024)}, u32[]{:S(2)}) copy-start(s32[2048]{0:T(1024)} %param.10) | copy-start | bytes 24580
  12.9 49.9 %collective-permute-start.2 = (f32[8,4096]{1,0:T(8,128)S(1)}, f32[8,4096]{1,0:T(8,128)S(1)}, u32[]{:S(2)}, u32[]{:S(2)}) collective-permute-start(f32[8,4096]{1,0:T(8,128)S(1)} %get-tuple-element.98), channel_id=1, source_target_pairs={{0,1},{1,2},{2,3},{3,4},{4,5},{5,6},{6,7},{8,9},{9,10},{10,11},{11... | collective-permute-start | bytes 393224 | tf_op jit(solution)/shard_map/ppermute | solution.py:75
  16.4 46.4 %collective-permute-start.3 = (f32[8,4096]{1,0:T(8,128)S(1)}, f32[8,4096]{1,0:T(8,128)S(1)}, u32[]{:S(2)}, u32[]{:S(2)}) collective-permute-start(f32[8,4096]{1,0:T(8,128)S(1)} %get-tuple-element.97), channel_id=1, source_target_pairs={{1,0},{2,1},{3,2},{4,3},{5,4},{6,5},{7,6},{9,8},{10,9},{11,10},{12... | collective-permute-start | bytes 393224 | tf_op jit(solution)/shard_map/ppermute | solution.py:77
  41.4 27.0 %all-to-all-start.1 = ((f32[32,48,128]{2,1,0:T(8,128)}), f32[32,48,128]{2,1,0:T(8,128)S(1)}, u32[]{:S(2)}, u32[]{:S(2)}) async-start(f32[32,48,128]{2,1,0:T(8,128)} %broadcast_select_fusion), calls=%async_computation.1 | async-start | bytes 1572864 | tf_op jit(solution)/shard_map/all_to_all | solution.py:65
  69.9 18.5 %collective-permute-start.1 = (f32[40,4096]{1,0:T(8,128)S(1)}, f32[40,4096]{1,0:T(8,128)S(1)}, u32[]{:S(2)}, u32[]{:S(2)}) collective-permute-start(f32[40,4096]{1,0:T(8,128)S(1)} %get-tuple-element.96), channel_id=1, source_target_pairs={{1,0},{2,1},{3,2},{4,3},{5,4},{6,5},{7,6},{9,8},{10,9},{11,10},{12... | collective-permute-start | bytes 1966088 | tf_op jit(solution)/shard_map/ppermute | solution.py:93
  75.0 21.1 %collective-permute-start = (f32[40,4096]{1,0:T(8,128)S(1)}, f32[40,4096]{1,0:T(8,128)S(1)}, u32[]{:S(2)}, u32[]{:S(2)}) collective-permute-start(f32[40,4096]{1,0:T(8,128)S(1)} %get-tuple-element.95), channel_id=1, source_target_pairs={{0,1},{1,2},{2,3},{3,4},{4,5},{5,6},{6,7},{8,9},{9,10},{10,11},{11... | collective-permute-start | bytes 1966088 | tf_op jit(solution)/shard_map/ppermute | solution.py:92
  88.4 8.1 %copy-start.1 = (f32[40,4096]{1,0:T(8,128)}, f32[40,4096]{1,0:T(8,128)S(1)}, u32[]{:S(2)}) copy-start(f32[40,4096]{1,0:T(8,128)S(1)} %collective-permute-done.1) | copy-start | bytes 1966084
  96.5 1.0 slice-start

commit v3 on v2

--- a/solution.py
+++ b/solution.py
@@ -3,6 +3,8 @@
 import jax.numpy as jnp
 from jax import lax
 from jax.sharding import PartitionSpec as P
+from jax.experimental import pallas as pl
+from jax.experimental.pallas import tpu as pltpu
 
 STEPS = 4
 BW = 8
@@ -11,6 +13,7 @@
 TIME_STEP = 0.8
 NUDGE_GAIN = 0.5
 LENGTH_SCALE = 3.0
+INTERPRET = False
 
 
 def weights():
@@ -29,23 +32,54 @@
     return total
 
 
-def shift_rows(q, d):
-    if d > 0:
-        return jnp.concatenate([q[d:], jnp.zeros_like(q[:d])], axis=0)
-    return jnp.concatenate([jnp.zeros_like(q[:(-d)]), q[:d]], axis=0)
+def forecast_kernel(fa_ref, fb_ref, h_ref, u_ref, v_ref, sp_ref, d_ref, cor_ref, ins_ref,
+                    o_ref, sext_ref, pad_ref, hx_ref, ux_ref, vx_ref):
+    rows = h_ref.shape[0]
+    margin = 2 * STEPS
+    ext = rows + 2 * margin
+    columns = h_ref.shape[1]
+    sext_ref[0:rows] = fa_ref[0:rows]
+    sext_ref[rows:2 * rows] = sp_ref[...]
+    sext_ref[2 * rows:3 * rows] = fb_ref[0:rows]
+    increment = jnp.zeros((ext, columns), jnp.float32)
+    for offset, weight in zip(range(-BW, BW + 1), weights()):
+        lo = rows - margin + offset
+        increment = increment + weight * sext_ref[lo:lo + ext]
+    for i, (x_ref, own_ref) in enumerate(((hx_ref, h_ref), (ux_ref, u_ref), (vx_ref, v_ref))):
+        lo = rows + i * margin
+        x_ref[0:margin] = fa_ref[lo:lo + margin]
+        x_ref[margin:margin + rows] = own_ref[...]
+        x_ref[margin + rows:ext] = fb_ref[lo:lo + margin]
+    height = hx_ref[...] + NUDGE_GAIN * increment
+    east_vel = ux_ref[...]
+    north_vel = vx_ref[...]
+    depth = d_ref[...]
+    coriolis = cor_ref[...]
+    inside = ins_ref[...] > 0.5
+    pad_ref[0:8] = jnp.zeros((8, columns), jnp.float32)
+    pad_ref[8 + ext:16 + ext] = jnp.zeros((8, columns), jnp.float32)
 
+    def north(q):
+        pad_ref[8:8 + ext] = q
+        return 0.5 * (pad_ref[9:9 + ext] - pad_ref[7:7 + ext])
 
-def advance(height, east_vel, north_vel, depth, coriolis, inside):
-    flux_east = depth * east_vel
-    flux_north = depth * north_vel
-    east_diff = 0.5 * (jnp.roll(flux_east, -1, -1) - jnp.roll(flux_east, 1, -1))
-    north_diff = 0.5 * (shift_rows(flux_north, 1) - shift_rows(flux_north, -1))
-    new_height = jnp.where(inside, height - TIME_STEP * (east_diff + north_diff), jnp.float32(0.0))
-    slope_east = 0.5 * (jnp.roll(new_height, -1, -1) - jnp.roll(new_height, 1, -1))
-    slope_north = 0.5 * (shift_rows(new_height, 1) - shift_rows(new_height, -1))
-    new_east = east_vel + TIME_STEP * (coriolis * north_vel - slope_east)
-    new_north = north_vel + TIME_STEP * (-coriolis * east_vel - slope_north)
-    return new_height, new_east, new_north
+    def east(q):
+        return 0.5 * (pltpu.roll(q, columns - 1, 1) - pltpu.roll(q, 1, 1))
+
+    for _ in range(STEPS):
+        flux_east = depth * east_vel
+        flux_north = depth * north_vel
+        east_diff = east(flux_east)
+        north_diff = north(flux_north)
+        height = jnp.where(inside, height - TIME_STEP * (east_diff + north_diff), jnp.float32(0.0))
+        slope_east = east(height)
+        slope_north = north(height)
+        new_east = east_vel + TIME_STEP * (coriolis * north_vel - slope_east)
+        new_north = north_vel + TIME_STEP * (-coriolis * east_vel - slope_north)
+        east_vel, north_vel = new_east, new_north
+    o_ref[0] = height[margin:margin + rows]
+    o_ref[1] = east_vel[margin:margin + rows]
+    o_ref[2] = north_vel[margin:margin + rows]
 
 
 def on_device(ensemble, ancestors, sea_depth, obs_rows, obs_cols, obs_values):
@@ -92,24 +126,27 @@
     from_above = lax.ppermute(to_below, "band", down)
     from_below = lax.ppermute(to_above, "band", up)
 
-    spread_ext = jnp.concatenate([from_above[:rows], spread, from_below[:rows]], axis=0)
-    increment = smooth(spread_ext, 0)[rows - margin: 2 * rows + margin]
-
-    def ext(i, own):
-        lo = rows + i * margin
-        return jnp.concatenate([from_above[lo:lo + margin], own, from_below[lo:lo + margin]], axis=0)
-
-    height = ext(0, height) + NUDGE_GAIN * increment
-    east_vel = ext(1, east_vel)
-    north_vel = ext(2, north_vel)
-
     total_rows = rows * bands
-    global_rows = band_start - margin + jnp.arange(rows + 2 * margin)
-    inside = ((global_rows >= 0) & (global_rows < total_rows))[:, None]
+    ext_rows = rows + 2 * margin
+    global_rows = band_start - margin + jnp.arange(ext_rows)
+    inside = ((global_rows >= 0) & (global_rows < total_rows)).astype(jnp.float32)[:, None]
     coriolis = (0.1 + 0.4 * ((global_rows.astype(jnp.float32) + 0.5) / total_rows))[:, None]
-    for _ in range(STEPS):
-        height, east_vel, north_vel = advance(height, east_vel, north_vel, depth_ext, coriolis, inside)
-    out = jnp.stack([height, east_vel, north_vel], axis=0)[:, margin:margin + rows]
+    wide = (ext_rows, columns)
+    out = pl.pallas_call(
+        forecast_kernel,
+        interpret=INTERPRET,
+        out_shape=jax.ShapeDtypeStruct((fields, rows, columns), jnp.float32),
+        scratch_shapes=[
+            pltpu.VMEM((3 * rows, columns), jnp.float32),
+            pltpu.VMEM((ext_rows + 16, columns), jnp.float32),
+            pltpu.VMEM(wide, jnp.float32),
+            pltpu.VMEM(wide, jnp.float32),
+            pltpu.VMEM(wide, jnp.float32),
+        ],
+    )(
+        from_above, from_below, height, east_vel, north_vel, spread, depth_ext,
+        jnp.broadcast_to(coriolis, wide), jnp.broadcast_to(inside, wide),
+    )
     return out[None]
 
 

time: 105 us -> 111 us (1.057)
  the two profiles are of different devices: /device:TPU:36 before, /device:TPU:24 now
where the time goes in v3:
time: 111 us
  blocking collectives  35.5 us (32%)
  local copies, waits for them, and re-layouts  24.3 us (22%)
  starting transfers between devices  19.9 us (18%)
  waiting for transfers between devices  18.5 us (17%)
  Pallas kernels  7.72 us (7%)
  other arithmetic  3.86 us (3%)
    all_to_all x1, blocking collectives, on_device(): lax.all_to_all(jnp.concatenate([block, tag], axis=1), 'dom', 0, 0, tiled=...  35.5 us
    ppermute x1, waiting for transfers between devices, on_device(): from_above = lax.ppermute(to_below, 'band', down)  10.8 us
    scatter x1, local copies, waits for them, and re-layouts, on_device(): jnp.zeros((rows * columns,), jnp.bool_).at[position].set(True)  9.19 us
    scatter x1, local copies, waits for them, and re-layouts, on_device(): jnp.zeros((rows * columns,), jnp.float32).at[position].set(obs_values)  8.3 us
    ppermute x1, waiting for transfers between devices, on_device(): from_below = lax.ppermute(to_above, 'band', up)  7.73 us
    pallas_call x1, Pallas kernels, on_device(): pl.pallas_call(forecast_kernel, interpret=INTERPRET, out_shape=jax.ShapeD...  7.72 us
    ppermute x1, starting transfers between devices, on_device(): from_above = lax.ppermute(to_below, 'band', down)  7.52 us
    ppermute x1, starting transfers between devices, on_device(): lax.ppermute(sea_depth[rows - margin:], 'band', down)  4.3 us
  transfers between devices with their start and end apart: 5, of which 2 were waited for; matrix products, arithmetic and copies ran while one was open for 18% of the time, Pallas kernels for 0%

profile of v3, /device:TPU:24, one launch (start us, length us, event | category | flops | bytes accessed | tf_op | source)
XLA Modules:
  0.0 110.6 jit_solution(1470534114837181631)
XLA Ops:
  0.0 1.3 %copy.27 = f32[6,8,32,128]{3,2,1,0:T(8,128)S(1)} copy(f32[6,8,32,128]{3,1,2,0:T(8,128)} %bitcast.46) | data formatting | bytes 1572864
  1.3 0.5 copy.34
  2.5 35.5 %all_to_all.10 = f32[32,56,128]{2,1,0:T(8,128)S(1)} all-to-all(f32[32,56,128]{2,1,0:T(8,128)S(1)} %concatenate.12), channel_id=1, replica_groups=mesh['dom'=32,'band'=8] {'dom'}, dimensions={0} | all-to-all | bytes 1835008 | tf_op jit(solution)/shard_map/all_to_all | solution.py:96
  37.9 0.7 fusion.21
  38.7 0.6 gather_fusion
  39.3 1.0 broadcast_select_fusion
  40.3 4.0 %all-to-all-start.1 = ((f32[32,48,128]{2,1,0:T(8,128)}), f32[32,48,128]{2,1,0:T(8,128)S(1)}, u32[]{:S(2)}, u32[]{:S(2)}) async-start(f32[32,48,128]{2,1,0:T(8,128)} %broadcast_select_fusion), calls=%async_computation.1 | async-start | bytes 1572864 | tf_op jit(solution)/shard_map/all_to_all | solution.py:99
  44.4 4.3 %collective-permute-start.2 = (f32[8,4096]{1,0:T(8,128)S(1)}, f32[8,4096]{1,0:T(8,128)S(1)}, u32[]{:S(2)}, u32[]{:S(2)}) collective-permute-start(f32[8,4096]{1,0:T(8,128)S(1)} %get-tuple-element.14), channel_id=1, source_target_pairs={{0,1},{1,2},{2,3},{3,4},{4,5},{5,6},{6,7},{8,9},{9,10},{10,11},{11... | collective-permute-start | bytes 393224 | tf_op jit(solution)/shard_map/ppermute | solution.py:109
  48.7 1.9 %collective-permute-start.3 = (f32[8,4096]{1,0:T(8,128)S(1)}, f32[8,4096]{1,0:T(8,128)S(1)}, u32[]{:S(2)}, u32[]{:S(2)}) collective-permute-start(f32[8,4096]{1,0:T(8,128)S(1)} %get-tuple-element.15), channel_id=1, source_target_pairs={{1,0},{2,1},{3,2},{4,3},{5,4},{6,5},{7,6},{9,8},{10,9},{11,10},{12... | collective-permute-start | bytes 393224 | tf_op jit(solution)/shard_map/ppermute | solution.py:111
  50.7 8.3 %scatter_custom_fusion.1 = f32[65536]{0:T(1024)S(1)} fusion(s32[2048]{0:T(1024)S(1)} %compare_select_fusion, f32[2048]{0:T(1024)} %param.11, f32[]{:T(128)} %constant.31.clone.1), kind=kCustom, calls=%fused_computation.46 | custom fusion | bytes 262656 | tf_op jit(solution)/shard_map/scatter | solution.py:105
  59.1 9.2 %scatter_custom_fusion = pred[65536]{0:T(1024)(128)(4,1)S(1)} fusion(s32[2048]{0:T(1024)S(1)} %compare_select_fusion, pred[2048]{0:T(1024)(128)(4,1)S(1)} %broadcast.97, pred[]{:T(512)} %constant.24.clone.1), kind=kCustom, calls=%fused_computation.48 | custom fusion | bytes 65537 | tf_op jit(solution)/shard_map/scatter | solution.py:104
  68.4 0.9 pad_maximum_fusion.2.d_ref
  69.4 0.7 copy.35
  70.1 1.1 %multiply_add_fusion.sp_ref = f32[16,4096]{1,0:T(8,128)S(1)} fusion(f32[16,4096]{1,0:T(8,128)S(1)} %subtract_select_fusion), kind=kLoop, calls=%fused_computation.18 | loop fusion | flops 2097152 | bytes 524288 | tf_op jit(solution)/shard_map/add | solution.py:31
  71.3 0.1 fusion.3
  71.4 0.6 copy-done
  72.0 7.5 %collective-permute-start = (f32[40,4096]{1,0:T(8,128)S(1)}, f32[40,4096]{1,0:T(8,128)S(1)}, u32[]{:S(2)}, u32[]{:S(2)}) collective-permute-start(f32[40,4096]{1,0:T(8,128)S(1)} %get-tuple-element.17), channel_id=1, source_target_pairs={{0,1},{1,2},{2,3},{3,4},{4,5},{5,6},{6,7},{8,9},{9,10},{10,11},{11... | collective-permute-start | bytes 1966088 | tf_op jit(solution)/shard_map/ppermute | solution.py:126
  79.5 2.1 %collective-permute-start.1 = (f32[40,4096]{1,0:T(8,128)S(1)}, f32[40,4096]{1,0:T(8,128)S(1)}, u32[]{:S(2)}, u32[]{:S(2)}) collective-permute-start(f32[40,4096]{1,0:T(8,128)S(1)} %get-tuple-element.16), channel_id=1, source_target_pairs={{1,0},{2,1},{3,2},{4,3},{5,4},{6,5},{7,6},{9,8},{10,9},{11,10},{12... | collective-permute-start | bytes 1966088 | tf_op jit(solution)/shard_map/ppermute | solution.py:127
  81.6 0.8 copy_bitcast_fusion.1
  82.5 10.8 %collective-permute-done.fa_ref = f32[40,4096]{1,0:T(8,128)S(1)} collective-permute-done((f32[40,4096]{1,0:T(8,128)S(1)}, f32[40,4096]{1,0:T(8,128)S(1)}, u32[]{:S(2)}, u32[]{:S(2)}) %collective-permute-start) | collective-permute-done | bytes 655392 | tf_op jit(solution)/shard_map/ppermute | solution.py:126
  93.3 7.7 %collective-permute-done.1.fb_ref = f32[40,4096]{1,0:T(8,128)S(1)} collective-permute-done((f32[40,4096]{1,0:T(8,128)S(1)}, f32[40,4096]{1,0:T(8,128)S(1)}, u32[]{:S(2)}, u32[]{:S(2)}) %collective-permute-start.1) | collective-permute-done | bytes 655392 | tf_op jit(solution)/shard_map/ppermute | solution.py:127
  101.0 1.0 broadcast_in_dim.56.cor_ref
  102.0 0.9 broadcast_in_dim.57.ins_ref
  102.9 7.7 %shard_map.64 = f32[3,16,4096]{2,1,0:T(8,128)} custom-call(f32[40,4096]{1,0:T(8,128)} %copy-done.2, f32[40,4096]{1,0:T(8,128)} %copy-done.3, f32[16,4096]{1,0:T(8,128)} %bitcast.45, f32[16,4096]{1,0:T(8,128)} %get-tuple-element.19.u_ref, f32[16,4096]{1,0:T(8,128)} %get-tuple-element.18.v_ref, f32[16,4096]{1,0:T(8,128)} %copy-done, ...), custom_call_target="tpu_custom_call" | custom-call | tf_op jit(solution)/shard_map/pallas_call | solution.py:135
  (29 shorter events, 0.5 us)
Async XLA Ops:
  40.3 4.1 %copy-start.1 = (f32[16,4096]{1,0:T(8,128)S(1)}, f32[16,4096]{1,0:T(8,128)}, u32[]{:S(2)}) copy-start(f32[16,4096]{1,0:T(8,128)} %param.8) | copy-start | bytes 786436
  40.3 28.9 %all-to-all-start.1 = ((f32[32,48,128]{2,1,0:T(8,128)}), f32[32,48,128]{2,1,0:T(8,128)S(1)}, u32[]{:S(2)}, u32[]{:S(2)}) async-start(f32[32,48,128]{2,1,0:T(8,128)} %broadcast_select_fusion), calls=%async_computation.1 | async-start | bytes 1572864 | tf_op jit(solution)/shard_map/all_to_all | solution.py:99
  44.3 6.3 %copy-start.5 = (s32[2048]{0:T(1024)S(1)}, s32[2048]{0:T(1024)}, u32[]{:S(2)}) copy-start(s32[2048]{0:T(1024)} %param.9) | copy-start | bytes 24580
  44.4 6.3 %copy-start.4 = (s32[2048]{0:T(1024)S(1)}, s32[2048]{0:T(1024)}, u32[]{:S(2)}) copy-start(s32[2048]{0:T(1024)} %param.10) | copy-start | bytes 24580
  44.4 24.0 %collective-permute-start.2 = (f32[8,4096]{1,0:T(8,128)S(1)}, f32[8,4096]{1,0:T(8,128)S(1)}, u32[]{:S(2)}, u32[]{:S(2)}) collective-permute-start(f32[8,4096]{1,0:T(8,128)S(1)} %get-tuple-element.14), channel_id=1, source_target_pairs={{0,1},{1,2},{2,3},{3,4},{4,5},{5,6},{6,7},{8,9},{9,10},{10,11},{11... | collective-permute-start | bytes 393224 | tf_op jit(solution)/shard_map/ppermute | solution.py:109
  48.7 19.7 %collective-permute-start.3 = (f32[8,4096]{1,0:T(8,128)S(1)}, f32[8,4096]{1,0:T(8,128)S(1)}, u32[]{:S(2)}, u32[]{:S(2)}) collective-permute-start(f32[8,4096]{1,0:T(8,128)S(1)} %get-tuple-element.15), channel_id=1, source_target_pairs={{1,0},{2,1},{3,2},{4,3},{5,4},{6,5},{7,6},{9,8},{10,9},{11,10},{12... | collective-permute-start | bytes 393224 | tf_op jit(solution)/shard_map/ppermute | solution.py:111
  71.3 0.7 copy-start
  72.0 21.3 %collective-permute-start = (f32[40,4096]{1,0:T(8,128)S(1)}, f32[40,4096]{1,0:T(8,128)S(1)}, u32[]{:S(2)}, u32[]{:S(2)}) collective-permute-start(f32[40,4096]{1,0:T(8,128)S(1)} %get-tuple-element.17), channel_id=1, source_target_pairs={{0,1},{1,2},{2,3},{3,4},{4,5},{5,6},{6,7},{8,9},{9,10},{10,11},{11... | collective-permute-start | bytes 1966088 | tf_op jit(solution)/shard_map/ppermute | solution.py:126
  79.5 21.5 %collective-permute-start.1 = (f32[40,4096]{1,0:T(8,128)S(1)}, f32[40,4096]{1,0:T(8,128)S(1)}, u32[]{:S(2)}, u32[]{:S(2)}) collective-permute-start(f32[40,4096]{1,0:T(8,128)S(1)} %get-tuple-element.16), channel_id=1, source_target_pairs={{1,0},{2,1},{3,2},{4,3},{5,4},{6,5},{7,6},{9,8},{10,9},{11,10},{12... | collective-permute-start | bytes 1966088 | tf_op jit(solution)/shard_map/ppermute | solution.py:127
  93.3 9.7 %copy-start.2 = (f32[40,4096]{1,0:T(8,128)}, f32[40,4096]{1,0:T(8,128)S(1)}, u32[]{:S(2)}) copy-start(f32[40,4096]{1,0:T(8,128)S(1)} %collective-permute-done.fa_ref) | copy-start | bytes 1966084
  101.0 1.9 %copy-start.3 = (f32[40,4096]{1,0:T(8,128)}, f32[40,4096]{1,0:T(8,128)S(1)}, u32[]{:S(2)}) copy-start(f32[40,4096]{1,0:T(8,128)S(1)} %collective-permute-done.1.fb_ref) | copy-start | bytes 1966084

commit v4 on v3

--- a/solution.py
+++ b/solution.py
@@ -54,8 +54,8 @@
     east_vel = ux_ref[...]
     north_vel = vx_ref[...]
     depth = d_ref[...]
-    coriolis = cor_ref[...]
-    inside = ins_ref[...] > 0.5
+    coriolis = jnp.broadcast_to(cor_ref[:, 0:1], (ext, columns))
+    inside = jnp.broadcast_to(ins_ref[:, 0:1], (ext, columns)) > 0.5
     pad_ref[0:8] = jnp.zeros((8, columns), jnp.float32)
     pad_ref[8 + ext:16 + ext] = jnp.zeros((8, columns), jnp.float32)
 
@@ -101,8 +101,8 @@
 
     band_start = band * rows
     position = (obs_rows - band_start) * columns + obs_cols
-    observed = jnp.zeros((rows * columns,), jnp.bool_).at[position].set(True).reshape(rows, columns)
-    values = jnp.zeros((rows * columns,), jnp.float32).at[position].set(obs_values).reshape(rows, columns)
+    values = jnp.full((rows * columns,), jnp.nan, jnp.float32).at[position].set(obs_values)
+    values = values.reshape(rows, columns)
 
     depth_ext = jnp.concatenate(
         [
@@ -114,7 +114,7 @@
     )
 
     height, east_vel, north_vel = state[0], state[1], state[2]
-    scattered = jnp.where(observed, values - height, jnp.float32(0.0))
+    scattered = jnp.where(jnp.isnan(values), jnp.float32(0.0), values - height)
     spread = smooth(scattered, 1)
 
     to_below = jnp.concatenate(
@@ -145,7 +145,7 @@
         ],
     )(
         from_above, from_below, height, east_vel, north_vel, spread, depth_ext,
-        jnp.broadcast_to(coriolis, wide), jnp.broadcast_to(inside, wide),
+        jnp.broadcast_to(coriolis, (ext_rows, 128)), jnp.broadcast_to(inside, (ext_rows, 128)),
     )
     return out[None]
 

time: 111 us -> 105 us (0.946)
  the two profiles are of different devices: /device:TPU:24 before, /device:TPU:56 now
where the time goes in v4:
time: 105 us; the launch traced here: 104 us
  blocking collectives  35.6 us (34%)
  waiting for transfers between devices  26 us (25%)
  starting transfers between devices  16.3 us (16%)
  local copies, waits for them, and re-layouts  14.6 us (14%)
  Pallas kernels  7.27 us (7%)
  other arithmetic  3.82 us (4%)
    all_to_all x1, blocking collectives, on_device(): lax.all_to_all(jnp.concatenate([block, tag], axis=1), 'dom', 0, 0, tiled=...  35.6 us
    ppermute x1, waiting for transfers between devices, on_device(): from_above = lax.ppermute(to_below, 'band', down)  10.7 us
    scatter x1, local copies, waits for them, and re-layouts, on_device(): jnp.full((rows * columns,), jnp.nan, jnp.float32).at[position]  8.3 us
    ppermute x1, waiting for transfers between devices, on_device(): from_below = lax.ppermute(to_above, 'band', up)  7.64 us
    pallas_call x1, Pallas kernels, on_device(): pl.pallas_call(forecast_kernel, interpret=INTERPRET, out_shape=jax.ShapeD...  7.27 us
    all_to_all x1, waiting for transfers between devices, on_device(): back = lax.all_to_all(chosen, 'dom', 0, 0, tiled=True)  5.41 us
    ppermute x1, starting transfers between devices, on_device(): lax.ppermute(sea_depth[rows - margin:], 'band', down)  4.3 us
    ppermute x1, starting transfers between devices, on_device(): from_above = lax.ppermute(to_below, 'band', down)  4.28 us
  transfers between devices with their start and end apart: 5, of which 4 were waited for; matrix products, arithmetic and copies ran while one was open for 10% of the time, Pallas kernels for 0%

profile of v4, /device:TPU:56, one launch (start us, length us, event | category | flops | bytes accessed | tf_op | source)
XLA Modules:
  0.0 104.4 jit_solution(237042808973238837)
XLA Ops:
  0.0 1.3 %copy.27 = f32[6,8,32,128]{3,2,1,0:T(8,128)S(1)} copy(f32[6,8,32,128]{3,1,2,0:T(8,128)} %bitcast.46) | data formatting | bytes 1572864
  1.3 0.5 copy.34
  2.5 35.6 %all_to_all.10 = f32[32,56,128]{2,1,0:T(8,128)S(1)} all-to-all(f32[32,56,128]{2,1,0:T(8,128)S(1)} %concatenate.12), channel_id=1, replica_groups=mesh['dom'=32,'band'=8] {'dom'}, dimensions={0} | all-to-all | bytes 1835008 | tf_op jit(solution)/shard_map/all_to_all | solution.py:96
  38.1 0.7 fusion.19
  38.8 0.6 gather_fusion
  39.4 1.0 broadcast_select_fusion
  40.4 3.8 %all-to-all-start.1 = ((f32[32,48,128]{2,1,0:T(8,128)}), f32[32,48,128]{2,1,0:T(8,128)S(1)}, u32[]{:S(2)}, u32[]{:S(2)}) async-start(f32[32,48,128]{2,1,0:T(8,128)} %broadcast_select_fusion), calls=%async_computation.1 | async-start | bytes 1572864 | tf_op jit(solution)/shard_map/all_to_all | solution.py:99
  44.3 4.3 %collective-permute-start.2 = (f32[8,4096]{1,0:T(8,128)S(1)}, f32[8,4096]{1,0:T(8,128)S(1)}, u32[]{:S(2)}, u32[]{:S(2)}) collective-permute-start(f32[8,4096]{1,0:T(8,128)S(1)} %get-tuple-element.14), channel_id=1, source_target_pairs={{0,1},{1,2},{2,3},{3,4},{4,5},{5,6},{6,7},{8,9},{9,10},{10,11},{11... | collective-permute-start | bytes 393224 | tf_op jit(solution)/shard_map/ppermute | solution.py:109
  48.6 1.9 %collective-permute-start.3 = (f32[8,4096]{1,0:T(8,128)S(1)}, f32[8,4096]{1,0:T(8,128)S(1)}, u32[]{:S(2)}, u32[]{:S(2)}) collective-permute-start(f32[8,4096]{1,0:T(8,128)S(1)} %get-tuple-element.15), channel_id=1, source_target_pairs={{1,0},{2,1},{3,2},{4,3},{5,4},{6,5},{7,6},{9,8},{10,9},{11,10},{12... | collective-permute-start | bytes 393224 | tf_op jit(solution)/shard_map/ppermute | solution.py:111
  50.6 8.3 %scatter_custom_fusion = f32[65536]{0:T(1024)S(1)} fusion(s32[2048]{0:T(1024)S(1)} %compare_select_fusion, f32[2048]{0:T(1024)} %param.11, f32[]{:T(128)} %constant.22.clone.1), kind=kCustom, calls=%fused_computation.45 | custom fusion | bytes 262656 | tf_op jit(solution)/shard_map/scatter | solution.py:104
  59.0 2.3 %collective-permute-done.3 = f32[8,4096]{1,0:T(8,128)S(1)} collective-permute-done((f32[8,4096]{1,0:T(8,128)S(1)}, f32[8,4096]{1,0:T(8,128)S(1)}, u32[]{:S(2)}, u32[]{:S(2)}) %collective-permute-start.3) | collective-permute-done | bytes 131104 | tf_op jit(solution)/shard_map/ppermute | solution.py:111
  61.3 0.8 pad_maximum_fusion.2.d_ref
  62.1 5.4 %all-to-all-done.1 = f32[32,48,128]{2,1,0:T(8,128)S(1)} async-done(((f32[32,48,128]{2,1,0:T(8,128)}), f32[32,48,128]{2,1,0:T(8,128)S(1)}, u32[]{:S(2)}, u32[]{:S(2)}) %all-to-all-start.1) | async-done | bytes 786464 | tf_op jit(solution)/shard_map/all_to_all | solution.py:99
  67.7 0.8 copy.35
  68.5 1.1 %multiply_add_fusion.sp_ref = f32[16,4096]{1,0:T(8,128)S(1)} fusion(f32[16,4096]{1,0:T(8,128)S(1)} %subtract_select_fusion), kind=kLoop, calls=%fused_computation.17 | loop fusion | flops 2097152 | bytes 524288 | tf_op jit(solution)/shard_map/add | solution.py:31
  69.7 0.6 copy-done
  70.3 4.3 %collective-permute-start = (f32[40,4096]{1,0:T(8,128)S(1)}, f32[40,4096]{1,0:T(8,128)S(1)}, u32[]{:S(2)}, u32[]{:S(2)}) collective-permute-start(f32[40,4096]{1,0:T(8,128)S(1)} %get-tuple-element.17), channel_id=1, source_target_pairs={{0,1},{1,2},{2,3},{3,4},{4,5},{5,6},{6,7},{8,9},{9,10},{10,11},{11... | collective-permute-start | bytes 1966088 | tf_op jit(solution)/shard_map/ppermute | solution.py:126
  74.6 1.9 %collective-permute-start.1 = (f32[40,4096]{1,0:T(8,128)S(1)}, f32[40,4096]{1,0:T(8,128)S(1)}, u32[]{:S(2)}, u32[]{:S(2)}) collective-permute-start(f32[40,4096]{1,0:T(8,128)S(1)} %get-tuple-element.16), channel_id=1, source_target_pairs={{1,0},{2,1},{3,2},{4,3},{5,4},{6,5},{7,6},{9,8},{10,9},{11,10},{12... | collective-permute-start | bytes 1966088 | tf_op jit(solution)/shard_map/ppermute | solution.py:127
  76.5 0.8 copy_bitcast_fusion.1
  77.4 10.7 %collective-permute-done.fa_ref = f32[40,4096]{1,0:T(8,128)S(1)} collective-permute-done((f32[40,4096]{1,0:T(8,128)S(1)}, f32[40,4096]{1,0:T(8,128)S(1)}, u32[]{:S(2)}, u32[]{:S(2)}) %collective-permute-start) | collective-permute-done | bytes 655392 | tf_op jit(solution)/shard_map/ppermute | solution.py:126
  88.1 7.6 %collective-permute-done.1.fb_ref = f32[40,4096]{1,0:T(8,128)S(1)} collective-permute-done((f32[40,4096]{1,0:T(8,128)S(1)}, f32[40,4096]{1,0:T(8,128)S(1)}, u32[]{:S(2)}, u32[]{:S(2)}) %collective-permute-start.1) | collective-permute-done | bytes 655392 | tf_op jit(solution)/shard_map/ppermute | solution.py:127
  95.7 0.8 broadcast_in_dim.47.cor_ref
  96.5 0.7 broadcast_in_dim.48.ins_ref
  97.1 7.3 %shard_map.64 = f32[3,16,4096]{2,1,0:T(8,128)} custom-call(f32[40,4096]{1,0:T(8,128)} %copy-done.2, f32[40,4096]{1,0:T(8,128)} %copy-done.3, f32[16,4096]{1,0:T(8,128)} %bitcast.45, f32[16,4096]{1,0:T(8,128)} %get-tuple-element.19.u_ref, f32[16,4096]{1,0:T(8,128)} %get-tuple-element.18.v_ref, f32[16,4096]{1,0:T(8,128)} %copy-done, ...), custom_call_target="tpu_custom_call" | custom-call | tf_op jit(solution)/shard_map/pallas_call | solution.py:135
  (26 shorter events, 0.5 us)
Async XLA Ops:
  40.4 3.8 %copy-start.1 = (f32[16,4096]{1,0:T(8,128)S(1)}, f32[16,4096]{1,0:T(8,128)}, u32[]{:S(2)}) copy-start(f32[16,4096]{1,0:T(8,128)} %param.8) | copy-start | bytes 786436
  40.4 27.1 %all-to-all-start.1 = ((f32[32,48,128]{2,1,0:T(8,128)}), f32[32,48,128]{2,1,0:T(8,128)S(1)}, u32[]{:S(2)}, u32[]{:S(2)}) async-start(f32[32,48,128]{2,1,0:T(8,128)} %broadcast_select_fusion), calls=%async_computation.1 | async-start | bytes 1572864 | tf_op jit(solution)/shard_map/all_to_all | solution.py:99
  44.3 6.3 %copy-start.5 = (s32[2048]{0:T(1024)S(1)}, s32[2048]{0:T(1024)}, u32[]{:S(2)}) copy-start(s32[2048]{0:T(1024)} %param.9) | copy-start | bytes 24580
  44.3 6.3 %copy-start.4 = (s32[2048]{0:T(1024)S(1)}, s32[2048]{0:T(1024)}, u32[]{:S(2)}) copy-start(s32[2048]{0:T(1024)} %param.10) | copy-start | bytes 24580
  44.3 14.7 %collective-permute-start.2 = (f32[8,4096]{1,0:T(8,128)S(1)}, f32[8,4096]{1,0:T(8,128)S(1)}, u32[]{:S(2)}, u32[]{:S(2)}) collective-permute-start(f32[8,4096]{1,0:T(8,128)S(1)} %get-tuple-element.14), channel_id=1, source_target_pairs={{0,1},{1,2},{2,3},{3,4},{4,5},{5,6},{6,7},{8,9},{9,10},{10,11},{11... | collective-permute-start | bytes 393224 | tf_op jit(solution)/shard_map/ppermute | solution.py:109
  48.6 12.7 %collective-permute-start.3 = (f32[8,4096]{1,0:T(8,128)S(1)}, f32[8,4096]{1,0:T(8,128)S(1)}, u32[]{:S(2)}, u32[]{:S(2)}) collective-permute-start(f32[8,4096]{1,0:T(8,128)S(1)} %get-tuple-element.15), channel_id=1, source_target_pairs={{1,0},{2,1},{3,2},{4,3},{5,4},{6,5},{7,6},{9,8},{10,9},{11,10},{12... | collective-permute-start | bytes 393224 | tf_op jit(solution)/shard_map/ppermute | solution.py:111
  69.6 0.7 copy-start
  70.3 17.7 %collective-permute-start = (f32[40,4096]{1,0:T(8,128)S(1)}, f32[40,4096]{1,0:T(8,128)S(1)}, u32[]{:S(2)}, u32[]{:S(2)}) collective-permute-start(f32[40,4096]{1,0:T(8,128)S(1)} %get-tuple-element.17), channel_id=1, source_target_pairs={{0,1},{1,2},{2,3},{3,4},{4,5},{5,6},{6,7},{8,9},{9,10},{10,11},{11... | collective-permute-start | bytes 1966088 | tf_op jit(solution)/shard_map/ppermute | solution.py:126
  74.6 21.1 %collective-permute-start.1 = (f32[40,4096]{1,0:T(8,128)S(1)}, f32[40,4096]{1,0:T(8,128)S(1)}, u32[]{:S(2)}, u32[]{:S(2)}) collective-permute-start(f32[40,4096]{1,0:T(8,128)S(1)} %get-tuple-element.16), channel_id=1, source_target_pairs={{1,0},{2,1},{3,2},{4,3},{5,4},{6,5},{7,6},{9,8},{10,9},{11,10},{12... | collective-permute-start | bytes 1966088 | tf_op jit(solution)/shard_map/ppermute | solution.py:127
  88.0 9.1 %copy-start.2 = (f32[40,4096]{1,0:T(8,128)}, f32[40,4096]{1,0:T(8,128)S(1)}, u32[]{:S(2)}) copy-start(f32[40,4096]{1,0:T(8,128)S(1)} %collective-permute-done.fa_ref) | copy-start | bytes 1966084
  95.7 1.5 %copy-start.3 = (f32[40,4096]{1,0:T(8,128)}, f32[40,4096]{1,0:T(8,128)S(1)}, u32[]{:S(2)}) copy-start(f32[40,4096]{1,0:T(8,128)S(1)} %collective-permute-done.1.fb_ref) | copy-start | bytes 1966084

commit v5 on v4

--- a/solution.py
+++ b/solution.py
@@ -1,3 +1,4 @@
+import functools
 import numpy as np
 import jax
 import jax.numpy as jnp
@@ -32,30 +33,27 @@
     return total
 
 
-def forecast_kernel(fa_ref, fb_ref, h_ref, u_ref, v_ref, sp_ref, d_ref, cor_ref, ins_ref,
-                    o_ref, sext_ref, pad_ref, hx_ref, ux_ref, vx_ref):
+def forecast_kernel(fa_ref, fb_ref, h_ref, u_ref, v_ref, pf_ref, d_ref,
+                    o_ref, pad_ref, hx_ref, *, total_rows):
     rows = h_ref.shape[0]
     margin = 2 * STEPS
     ext = rows + 2 * margin
     columns = h_ref.shape[1]
-    sext_ref[0:rows] = fa_ref[0:rows]
-    sext_ref[rows:2 * rows] = sp_ref[...]
-    sext_ref[2 * rows:3 * rows] = fb_ref[0:rows]
-    increment = jnp.zeros((ext, columns), jnp.float32)
-    for offset, weight in zip(range(-BW, BW + 1), weights()):
-        lo = rows - margin + offset
-        increment = increment + weight * sext_ref[lo:lo + ext]
-    for i, (x_ref, own_ref) in enumerate(((hx_ref, h_ref), (ux_ref, u_ref), (vx_ref, v_ref))):
-        lo = rows + i * margin
-        x_ref[0:margin] = fa_ref[lo:lo + margin]
-        x_ref[margin:margin + rows] = own_ref[...]
-        x_ref[margin + rows:ext] = fb_ref[lo:lo + margin]
-    height = hx_ref[...] + NUDGE_GAIN * increment
-    east_vel = ux_ref[...]
-    north_vel = vx_ref[...]
+    half = rows // 2
+    hx_ref[0:margin] = fa_ref[2 * margin:3 * margin] + NUDGE_GAIN * pf_ref[0:margin]
+    hx_ref[margin:margin + half] = h_ref[0:half] + NUDGE_GAIN * (
+        pf_ref[margin:margin + half] + fa_ref[margin:2 * margin])
+    hx_ref[margin + half:margin + rows] = h_ref[half:rows] + NUDGE_GAIN * (
+        pf_ref[margin + half:margin + rows] + fb_ref[margin:2 * margin])
+    hx_ref[margin + rows:ext] = fb_ref[2 * margin:3 * margin] + NUDGE_GAIN * pf_ref[margin + rows:ext]
+    height = hx_ref[...]
+    east_vel = jnp.concatenate([fa_ref[3 * margin:4 * margin], u_ref[...], fb_ref[3 * margin:4 * margin]], axis=0)
+    north_vel = jnp.concatenate([fa_ref[0:margin], v_ref[...], fb_ref[0:margin]], axis=0)
+    band_start = lax.axis_index("band") * rows
+    global_rows = band_start - margin + lax.broadcasted_iota(jnp.int32, (ext, columns), 0)
+    inside = (global_rows >= 0) & (global_rows < total_rows)
+    coriolis = 0.1 + 0.4 * ((global_rows.astype(jnp.float32) + 0.5) / total_rows)
     depth = d_ref[...]
-    coriolis = jnp.broadcast_to(cor_ref[:, 0:1], (ext, columns))
-    inside = jnp.broadcast_to(ins_ref[:, 0:1], (ext, columns)) > 0.5
     pad_ref[0:8] = jnp.zeros((8, columns), jnp.float32)
     pad_ref[8 + ext:16 + ext] = jnp.zeros((8, columns), jnp.float32)
 
@@ -117,36 +115,38 @@
     scattered = jnp.where(jnp.isnan(values), jnp.float32(0.0), values - height)
     spread = smooth(scattered, 1)
 
+    partial = smooth(jnp.pad(spread, ((margin, margin), (0, 0))), 0)
     to_below = jnp.concatenate(
-        [spread, height[rows - margin:], east_vel[rows - margin:], north_vel[rows - margin:]], axis=0
+        [
+            north_vel[rows - margin:],
+            partial[rows + margin:],
+            height[rows - margin:] + NUDGE_GAIN * partial[rows:rows + margin],
+            east_vel[rows - margin:],
+        ],
+        axis=0,
     )
     to_above = jnp.concatenate(
-        [spread, height[:margin], east_vel[:margin], north_vel[:margin]], axis=0
+        [
+            north_vel[:margin],
+            partial[:margin],
+            height[:margin] + NUDGE_GAIN * partial[margin:2 * margin],
+            east_vel[:margin],
+        ],
+        axis=0,
     )
     from_above = lax.ppermute(to_below, "band", down)
     from_below = lax.ppermute(to_above, "band", up)
 
-    total_rows = rows * bands
     ext_rows = rows + 2 * margin
-    global_rows = band_start - margin + jnp.arange(ext_rows)
-    inside = ((global_rows >= 0) & (global_rows < total_rows)).astype(jnp.float32)[:, None]
-    coriolis = (0.1 + 0.4 * ((global_rows.astype(jnp.float32) + 0.5) / total_rows))[:, None]
-    wide = (ext_rows, columns)
     out = pl.pallas_call(
-        forecast_kernel,
+        functools.partial(forecast_kernel, total_rows=rows * bands),
         interpret=INTERPRET,
         out_shape=jax.ShapeDtypeStruct((fields, rows, columns), jnp.float32),
         scratch_shapes=[
-            pltpu.VMEM((3 * rows, columns), jnp.float32),
             pltpu.VMEM((ext_rows + 16, columns), jnp.float32),
-            pltpu.VMEM(wide, jnp.float32),
-            pltpu.VMEM(wide, jnp.float32),
-            pltpu.VMEM(wide, jnp.float32),
+            pltpu.VMEM((ext_rows, columns), jnp.float32),
         ],
-    )(
-        from_above, from_below, height, east_vel, north_vel, spread, depth_ext,
-        jnp.broadcast_to(coriolis, (ext_rows, 128)), jnp.broadcast_to(inside, (ext_rows, 128)),
-    )
+    )(from_above, from_below, height, east_vel, north_vel, partial, depth_ext)
     return out[None]
 
 

time: 105 us -> 102 us (0.971)
  the two profiles are of different devices: /device:TPU:56 before, /device:TPU:36 now
where the time goes in v5:
time: 102 us; the launch traced here: 101 us
  blocking collectives  35.3 us (35%)
  starting transfers between devices  20.4 us (20%)
  waiting for transfers between devices  20 us (20%)
  local copies, waits for them, and re-layouts  14.1 us (14%)
  Pallas kernels  6.14 us (6%)
  other arithmetic  4.65 us (5%)
    all_to_all x1, blocking collectives, on_device(): lax.all_to_all(jnp.concatenate([block, tag], axis=1), 'dom', 0, 0, tiled=...  35.3 us
    scatter x1, local copies, waits for them, and re-layouts, on_device(): jnp.full((rows * columns,), jnp.nan, jnp.float32).at[position]  8.3 us
    ppermute x1, waiting for transfers between devices, on_device(): from_above = lax.ppermute(to_below, 'band', down)  7.77 us
    ppermute x1, waiting for transfers between devices, on_device(): from_below = lax.ppermute(to_above, 'band', up)  7.71 us
    pallas_call x1, Pallas kernels, on_device(): pl.pallas_call(functools.partial(forecast_kernel, total_rows=rows * bands...  6.14 us
    ppermute x1, starting transfers between devices, on_device(): lax.ppermute(sea_depth[:margin], 'band', up)  5.97 us
    ppermute x1, starting transfers between devices, on_device(): from_below = lax.ppermute(to_above, 'band', up)  5.16 us
    all_to_all x1, waiting for transfers between devices, on_device(): back = lax.all_to_all(chosen, 'dom', 0, 0, tiled=True)  4.48 us
  transfers between devices with their start and end apart: 5, of which 3 were waited for; matrix products, arithmetic and copies ran while one was open for 10% of the time, Pallas kernels for 0%

profile of v5, /device:TPU:36, one launch (start us, length us, event | category | flops | bytes accessed | tf_op | source)
XLA Modules:
  0.0 101.4 jit_solution(7748457768309529051)
XLA Ops:
  0.0 1.3 %copy.27 = f32[6,8,32,128]{3,2,1,0:T(8,128)S(1)} copy(f32[6,8,32,128]{3,1,2,0:T(8,128)} %bitcast.51) | data formatting | bytes 1572864
  1.3 0.5 copy.34
  2.4 0.1 concatenate.12
  2.5 35.3 %all_to_all.10 = f32[32,56,128]{2,1,0:T(8,128)S(1)} all-to-all(f32[32,56,128]{2,1,0:T(8,128)S(1)} %concatenate.12), channel_id=1, replica_groups=mesh['dom'=32,'band'=8] {'dom'}, dimensions={0} | all-to-all | bytes 1835008 | tf_op jit(solution)/shard_map/all_to_all | solution.py:94
  37.8 0.7 fusion.49
  38.5 0.6 gather_fusion
  39.1 1.0 broadcast_select_fusion
  40.1 3.8 %all-to-all-start.1 = ((f32[32,48,128]{2,1,0:T(8,128)}), f32[32,48,128]{2,1,0:T(8,128)S(1)}, u32[]{:S(2)}, u32[]{:S(2)}) async-start(f32[32,48,128]{2,1,0:T(8,128)} %broadcast_select_fusion), calls=%async_computation.1 | async-start | bytes 1572864 | tf_op jit(solution)/shard_map/all_to_all | solution.py:97
  44.0 3.5 %collective-permute-start.2 = (f32[8,4096]{1,0:T(8,128)S(1)}, f32[8,4096]{1,0:T(8,128)S(1)}, u32[]{:S(2)}, u32[]{:S(2)}) collective-permute-start(f32[8,4096]{1,0:T(8,128)S(1)} %get-tuple-element.16), channel_id=1, source_target_pairs={{0,1},{1,2},{2,3},{3,4},{4,5},{5,6},{6,7},{8,9},{9,10},{10,11},{11... | collective-permute-start | bytes 393224 | tf_op jit(solution)/shard_map/ppermute | solution.py:107
  47.5 6.0 %collective-permute-start.3 = (f32[8,4096]{1,0:T(8,128)S(1)}, f32[8,4096]{1,0:T(8,128)S(1)}, u32[]{:S(2)}, u32[]{:S(2)}) collective-permute-start(f32[8,4096]{1,0:T(8,128)S(1)} %get-tuple-element.17), channel_id=1, source_target_pairs={{1,0},{2,1},{3,2},{4,3},{5,4},{6,5},{7,6},{9,8},{10,9},{11,10},{12... | collective-permute-start | bytes 393224 | tf_op jit(solution)/shard_map/ppermute | solution.py:109
  53.5 8.3 %scatter_custom_fusion = f32[65536]{0:T(1024)S(1)} fusion(s32[2048]{0:T(1024)S(1)} %compare_select_fusion, f32[2048]{0:T(1024)} %param.11, f32[]{:T(128)} %constant.21.clone.1), kind=kCustom, calls=%fused_computation.93 | custom fusion | bytes 262656 | tf_op jit(solution)/shard_map/scatter | solution.py:102
  61.9 0.8 pad_maximum_fusion.2.d_ref
  62.8 4.5 %all-to-all-done.1 = f32[32,48,128]{2,1,0:T(8,128)S(1)} async-done(((f32[32,48,128]{2,1,0:T(8,128)}), f32[32,48,128]{2,1,0:T(8,128)S(1)}, u32[]{:S(2)}, u32[]{:S(2)}) %all-to-all-start.1) | async-done | bytes 786464 | tf_op jit(solution)/shard_map/all_to_all | solution.py:97
  67.4 0.7 copy.35
  68.1 1.1 %multiply_add_fusion = f32[16,4096]{1,0:T(8,128)S(1)} fusion(f32[16,4096]{1,0:T(8,128)S(1)} %subtract_select_fusion), kind=kLoop, calls=%fused_computation.61 | loop fusion | flops 2097152 | bytes 524288 | tf_op jit(solution)/shard_map/add | solution.py:32
  69.3 0.8 fusion.16.pf_ref
  70.2 0.7 copy-done
  71.0 5.2 %collective-permute-start.1 = (f32[32,4096]{1,0:T(8,128)S(1)}, f32[32,4096]{1,0:T(8,128)S(1)}, u32[]{:S(2)}, u32[]{:S(2)}) collective-permute-start(f32[32,4096]{1,0:T(8,128)S(1)} %pad_maximum_fusion.1), channel_id=1, source_target_pairs={{1,0},{2,1},{3,2},{4,3},{5,4},{6,5},{7,6},{9,8},{10,9},{11,10},{12... | collective-permute-start | bytes 1572872 | tf_op jit(solution)/shard_map/ppermute | solution.py:138
  76.2 1.9 %collective-permute-start = (f32[32,4096]{1,0:T(8,128)S(1)}, f32[32,4096]{1,0:T(8,128)S(1)}, u32[]{:S(2)}, u32[]{:S(2)}) collective-permute-start(f32[32,4096]{1,0:T(8,128)S(1)} %pad_maximum_fusion), channel_id=1, source_target_pairs={{0,1},{1,2},{2,3},{3,4},{4,5},{5,6},{6,7},{8,9},{9,10},{10,11},{11... | collective-permute-start | bytes 1572872 | tf_op jit(solution)/shard_map/ppermute | solution.py:137
  78.1 0.8 copy_bitcast_fusion.1
  79.0 7.7 %collective-permute-done.1.fb_ref = f32[32,4096]{1,0:T(8,128)S(1)} collective-permute-done((f32[32,4096]{1,0:T(8,128)S(1)}, f32[32,4096]{1,0:T(8,128)S(1)}, u32[]{:S(2)}, u32[]{:S(2)}) %collective-permute-start.1) | collective-permute-done | bytes 524320 | tf_op jit(solution)/shard_map/ppermute | solution.py:138
  86.7 7.8 %collective-permute-done.fa_ref = f32[32,4096]{1,0:T(8,128)S(1)} collective-permute-done((f32[32,4096]{1,0:T(8,128)S(1)}, f32[32,4096]{1,0:T(8,128)S(1)}, u32[]{:S(2)}, u32[]{:S(2)}) %collective-permute-start) | collective-permute-done | bytes 524320 | tf_op jit(solution)/shard_map/ppermute | solution.py:137
  94.4 0.8 copy-done.3
  95.2 6.1 %shard_map.64 = f32[3,16,4096]{2,1,0:T(8,128)} custom-call(f32[32,4096]{1,0:T(8,128)} %copy-done.3, f32[32,4096]{1,0:T(8,128)} %copy-done.2, f32[16,4096]{1,0:T(8,128)} %bitcast.50, f32[16,4096]{1,0:T(8,128)} %get-tuple-element.19.u_ref, f32[16,4096]{1,0:T(8,128)} %get-tuple-element.18.v_ref, f32[32,4096]{1,0:T(8,128)} %copy-done, ...), custom_call_target="tpu_custom_call" | custom-call | tf_op jit(solution)/shard_map/pallas_call | solution.py:141
  (26 shorter events, 0.5 us)
Async XLA Ops:
  40.1 3.8 %copy-start.1 = (f32[16,4096]{1,0:T(8,128)S(1)}, f32[16,4096]{1,0:T(8,128)}, u32[]{:S(2)}) copy-start(f32[16,4096]{1,0:T(8,128)} %param.8) | copy-start | bytes 786436
  40.1 27.1 %all-to-all-start.1 = ((f32[32,48,128]{2,1,0:T(8,128)}), f32[32,48,128]{2,1,0:T(8,128)S(1)}, u32[]{:S(2)}, u32[]{:S(2)}) async-start(f32[32,48,128]{2,1,0:T(8,128)} %broadcast_select_fusion), calls=%async_computation.1 | async-start | bytes 1572864 | tf_op jit(solution)/shard_map/all_to_all | solution.py:97
  44.0 9.5 %copy-start.5 = (s32[2048]{0:T(1024)S(1)}, s32[2048]{0:T(1024)}, u32[]{:S(2)}) copy-start(s32[2048]{0:T(1024)} %param.9) | copy-start | bytes 24580
  44.0 9.5 %copy-start.4 = (s32[2048]{0:T(1024)S(1)}, s32[2048]{0:T(1024)}, u32[]{:S(2)}) copy-start(s32[2048]{0:T(1024)} %param.10) | copy-start | bytes 24580
  44.0 17.9 %collective-permute-start.2 = (f32[8,4096]{1,0:T(8,128)S(1)}, f32[8,4096]{1,0:T(8,128)S(1)}, u32[]{:S(2)}, u32[]{:S(2)}) collective-permute-start(f32[8,4096]{1,0:T(8,128)S(1)} %get-tuple-element.16), channel_id=1, source_target_pairs={{0,1},{1,2},{2,3},{3,4},{4,5},{5,6},{6,7},{8,9},{9,10},{10,11},{11... | collective-permute-start | bytes 393224 | tf_op jit(solution)/shard_map/ppermute | solution.py:107
  47.5 14.4 %collective-permute-start.3 = (f32[8,4096]{1,0:T(8,128)S(1)}, f32[8,4096]{1,0:T(8,128)S(1)}, u32[]{:S(2)}, u32[]{:S(2)}) collective-permute-start(f32[8,4096]{1,0:T(8,128)S(1)} %get-tuple-element.17), channel_id=1, source_target_pairs={{1,0},{2,1},{3,2},{4,3},{5,4},{6,5},{7,6},{9,8},{10,9},{11,10},{12... | collective-permute-start | bytes 393224 | tf_op jit(solution)/shard_map/ppermute | solution.py:109
  70.1 0.8 copy-start
  71.0 15.7 %collective-permute-start.1 = (f32[32,4096]{1,0:T(8,128)S(1)}, f32[32,4096]{1,0:T(8,128)S(1)}, u32[]{:S(2)}, u32[]{:S(2)}) collective-permute-start(f32[32,4096]{1,0:T(8,128)S(1)} %pad_maximum_fusion.1), channel_id=1, source_target_pairs={{1,0},{2,1},{3,2},{4,3},{5,4},{6,5},{7,6},{9,8},{10,9},{11,10},{12... | collective-permute-start | bytes 1572872 | tf_op jit(solution)/shard_map/ppermute | solution.py:138
  76.2 18.3 %collective-permute-start = (f32[32,4096]{1,0:T(8,128)S(1)}, f32[32,4096]{1,0:T(8,128)S(1)}, u32[]{:S(2)}, u32[]{:S(2)}) collective-permute-start(f32[32,4096]{1,0:T(8,128)S(1)} %pad_maximum_fusion), channel_id=1, source_target_pairs={{0,1},{1,2},{2,3},{3,4},{4,5},{5,6},{6,7},{8,9},{9,10},{10,11},{11... | collective-permute-start | bytes 1572872 | tf_op jit(solution)/shard_map/ppermute | solution.py:137
  86.7 7.8 %copy-start.2 = (f32[32,4096]{1,0:T(8,128)}, f32[32,4096]{1,0:T(8,128)S(1)}, u32[]{:S(2)}) copy-start(f32[32,4096]{1,0:T(8,128)S(1)} %collective-permute-done.1.fb_ref) | copy-start | bytes 1572868
  94.4 0.8 copy-start.3

commit v6 on v5

--- a/solution.py
+++ b/solution.py
@@ -80,6 +80,41 @@
     o_ref[2] = north_vel[margin:margin + rows]
 
 
+def prepare_kernel(h_ref, u_ref, v_ref, val_ref, below_ref, above_ref, pf_ref, scr_ref):
+    rows, columns = h_ref.shape
+    margin = 2 * STEPS
+    ext = rows + 2 * margin
+    values = val_ref[...]
+    height = h_ref[...]
+    scattered = jnp.where(values != values, jnp.float32(0.0), values - height)
+    column = lax.broadcasted_iota(jnp.int32, (rows, columns), 1)
+    spread = jnp.zeros((rows, columns), jnp.float32)
+    for offset, weight in zip(range(-BW, BW + 1), weights()):
+        if offset == 0:
+            piece = scattered
+        else:
+            piece = pltpu.roll(scattered, (-offset) % columns, 1)
+            valid = (column + offset >= 0) & (column + offset < columns)
+            piece = jnp.where(valid, piece, jnp.float32(0.0))
+        spread = spread + weight * piece
+    scr_ref[0:2 * margin] = jnp.zeros((2 * margin, columns), jnp.float32)
+    scr_ref[2 * margin:2 * margin + rows] = spread
+    scr_ref[2 * margin + rows:4 * margin + rows] = jnp.zeros((2 * margin, columns), jnp.float32)
+    partial = jnp.zeros((ext, columns), jnp.float32)
+    for offset, weight in zip(range(-BW, BW + 1), weights()):
+        lo = margin + offset
+        partial = partial + weight * scr_ref[lo:lo + ext]
+    pf_ref[...] = partial
+    below_ref[0:margin] = v_ref[rows - margin:rows]
+    below_ref[margin:2 * margin] = partial[rows + margin:ext]
+    below_ref[2 * margin:3 * margin] = h_ref[rows - margin:rows] + NUDGE_GAIN * partial[rows:rows + margin]
+    below_ref[3 * margin:4 * margin] = u_ref[rows - margin:rows]
+    above_ref[0:margin] = v_ref[0:margin]
+    above_ref[margin:2 * margin] = partial[0:margin]
+    above_ref[2 * margin:3 * margin] = h_ref[0:margin] + NUDGE_GAIN * partial[margin:2 * margin]
+    above_ref[3 * margin:4 * margin] = u_ref[0:margin]
+
+
 def on_device(ensemble, ancestors, sea_depth, obs_rows, obs_cols, obs_values):
     _, fields, rows, columns = ensemble.shape
     parts = lax.axis_size("dom")
@@ -93,7 +128,7 @@
     tag = jnp.broadcast_to(ancestors.astype(jnp.float32)[:, None, None], (parts, 8, columns // parts))
     crossed = lax.all_to_all(jnp.concatenate([block, tag], axis=1), "dom", 0, 0, tiled=True)
     lineage = crossed[:, fields * rows, 0].astype(jnp.int32)
-    chosen = jnp.take(crossed[:, :fields * rows], lineage, axis=0)
+    chosen = jnp.take(crossed[:, :fields * rows], lineage, axis=0, mode="clip")
     back = lax.all_to_all(chosen, "dom", 0, 0, tiled=True)
     state = back.transpose(1, 0, 2).reshape(fields, rows, columns)
 
@@ -112,28 +147,13 @@
     )
 
     height, east_vel, north_vel = state[0], state[1], state[2]
-    scattered = jnp.where(jnp.isnan(values), jnp.float32(0.0), values - height)
-    spread = smooth(scattered, 1)
-
-    partial = smooth(jnp.pad(spread, ((margin, margin), (0, 0))), 0)
-    to_below = jnp.concatenate(
-        [
-            north_vel[rows - margin:],
-            partial[rows + margin:],
-            height[rows - margin:] + NUDGE_GAIN * partial[rows:rows + margin],
-            east_vel[rows - margin:],
-        ],
-        axis=0,
-    )
-    to_above = jnp.concatenate(
-        [
-            north_vel[:margin],
-            partial[:margin],
-            height[:margin] + NUDGE_GAIN * partial[margin:2 * margin],
-            east_vel[:margin],
-        ],
-        axis=0,
-    )
+    halo = jax.ShapeDtypeStruct((4 * margin, columns), jnp.float32)
+    to_below, to_above, partial = pl.pallas_call(
+        prepare_kernel,
+        interpret=INTERPRET,
+        out_shape=(halo, halo, jax.ShapeDtypeStruct((rows + 2 * margin, columns), jnp.float32)),
+        scratch_shapes=[pltpu.VMEM((rows + 4 * margin, columns), jnp.float32)],
+    )(height, east_vel, north_vel, values)
     from_above = lax.ppermute(to_below, "band", down)
     from_below = lax.ppermute(to_above, "band", up)
 

time: 102 us -> 104 us (1.020)
  the two profiles are of different devices: /device:TPU:36 before, /device:TPU:56 now
where the time goes in v6:
time: 104 us; the launch traced here: 103 us
  blocking collectives  35.6 us (34%)
  waiting for transfers between devices  23.5 us (23%)
  starting transfers between devices  16.3 us (16%)
  local copies, waits for them, and re-layouts  14.8 us (14%)
  Pallas kernels  10.7 us (10%)
  other arithmetic  1.55 us (1%)
    all_to_all x1, blocking collectives, on_device(): lax.all_to_all(jnp.concatenate([block, tag], axis=1), 'dom', 0, 0, tiled=...  35.6 us
    scatter x1, local copies, waits for them, and re-layouts, on_device(): jnp.full((rows * columns,), jnp.nan, jnp.float32).at[position]  8.3 us
    ppermute x1, waiting for transfers between devices, on_device(): from_above = lax.ppermute(to_below, 'band', down)  8.02 us
    all_to_all x1, waiting for transfers between devices, on_device(): back = lax.all_to_all(chosen, 'dom', 0, 0, tiled=True)  7.9 us
    ppermute x1, waiting for transfers between devices, on_device(): from_below = lax.ppermute(to_above, 'band', up)  7.62 us
    pallas_call x1, Pallas kernels, on_device(): pl.pallas_call(functools.partial(forecast_kernel, total_rows=rows * bands...  6.14 us
    pallas_call x1, Pallas kernels, on_device(): pl.pallas_call(prepare_kernel, interpret=INTERPRET, out_shape=(halo, halo...  4.58 us
    ppermute x1, starting transfers between devices, on_device(): lax.ppermute(sea_depth[rows - margin:], 'band', down)  4.3 us
  transfers between devices with their start and end apart: 5, of which 3 were waited for; matrix products, arithmetic and copies ran while one was open for 11% of the time, Pallas kernels for 4%

profile of v6, /device:TPU:56, one launch (start us, length us, event | category | flops | bytes accessed | tf_op | source)
XLA Modules:
  0.0 103.3 jit_solution(8036851859272524304)
XLA Ops:
  0.7 1.3 %copy.21 = f32[6,8,32,128]{3,2,1,0:T(8,128)S(1)} copy(f32[6,8,32,128]{3,1,2,0:T(8,128)} %bitcast.29) | data formatting | bytes 1572864
  1.9 0.5 copy.26
  2.4 0.1 concatenate.6
  2.5 35.6 %all_to_all.10 = f32[32,56,128]{2,1,0:T(8,128)S(1)} all-to-all(f32[32,56,128]{2,1,0:T(8,128)S(1)} %concatenate.6), channel_id=1, replica_groups=mesh['dom'=32,'band'=8] {'dom'}, dimensions={0} | all-to-all | bytes 1835008 | tf_op jit(solution)/shard_map/all_to_all | solution.py:129
  38.1 0.7 fusion.2
  38.7 0.1 slice.33
  38.8 1.5 %gather_fusion = f32[32,48,128]{2,1,0:T(8,128)} fusion(f32[32,48,128]{2,1,0:T(8,128)S(1)} %slice.33, s32[1024]{0:T(1024)S(1)} %pad_clamp_fusion), kind=kCustom, calls=%fused_computation | custom fusion | bytes 1572992 | tf_op jit(solution)/shard_map/jit(_take)/gather | solution.py:131
  40.3 3.8 %all-to-all-start.1 = ((f32[32,48,128]{2,1,0:T(8,128)}), f32[32,48,128]{2,1,0:T(8,128)S(1)}, u32[]{:S(2)}, u32[]{:S(2)}) async-start(f32[32,48,128]{2,1,0:T(8,128)} %gather_fusion), calls=%async_computation.1 | async-start | bytes 1572864 | tf_op jit(solution)/shard_map/all_to_all | solution.py:132
  44.2 4.3 %collective-permute-start.2 = (f32[8,4096]{1,0:T(8,128)S(1)}, f32[8,4096]{1,0:T(8,128)S(1)}, u32[]{:S(2)}, u32[]{:S(2)}) collective-permute-start(f32[8,4096]{1,0:T(8,128)S(1)} %get-tuple-element.14), channel_id=1, source_target_pairs={{0,1},{1,2},{2,3},{3,4},{4,5},{5,6},{6,7},{8,9},{9,10},{10,11},{11... | collective-permute-start | bytes 393224 | tf_op jit(solution)/shard_map/ppermute | solution.py:142
  48.5 1.9 %collective-permute-start.3 = (f32[8,4096]{1,0:T(8,128)S(1)}, f32[8,4096]{1,0:T(8,128)S(1)}, u32[]{:S(2)}, u32[]{:S(2)}) collective-permute-start(f32[8,4096]{1,0:T(8,128)S(1)} %get-tuple-element.15), channel_id=1, source_target_pairs={{1,0},{2,1},{3,2},{4,3},{5,4},{6,5},{7,6},{9,8},{10,9},{11,10},{12... | collective-permute-start | bytes 393224 | tf_op jit(solution)/shard_map/ppermute | solution.py:144
  50.5 8.3 %scatter_custom_fusion = f32[65536]{0:T(1024)S(1)} fusion(s32[2048]{0:T(1024)S(1)} %compare_select_fusion, f32[2048]{0:T(1024)} %param.11, f32[]{:T(128)} %constant.6.clone.1), kind=kCustom, calls=%fused_computation.10 | custom fusion | bytes 262656 | tf_op jit(solution)/shard_map/scatter | solution.py:137
  58.8 0.7 reshape.26.val_ref
  59.5 7.9 %all-to-all-done.1 = f32[32,48,128]{2,1,0:T(8,128)S(1)} async-done(((f32[32,48,128]{2,1,0:T(8,128)}), f32[32,48,128]{2,1,0:T(8,128)S(1)}, u32[]{:S(2)}, u32[]{:S(2)}) %all-to-all-start.1) | async-done | bytes 786464 | tf_op jit(solution)/shard_map/all_to_all | solution.py:132
  67.4 0.1 slice_bitcast_fusion
  67.5 0.8 copy_bitcast_fusion.1
  68.3 0.7 copy.27
  69.0 4.6 %shard_map.64 = (f32[32,4096]{1,0:T(8,128)}, f32[32,4096]{1,0:T(8,128)}, f32[32,4096]{1,0:T(8,128)}) custom-call(f32[16,4096]{1,0:T(8,128)} %bitcast.27, f32[16,4096]{1,0:T(8,128)} %get-tuple-element.17.u_ref, f32[16,4096]{1,0:T(8,128)} %get-tuple-element.16.v_ref, f32[16,4096]{1,0:T(8,128)} %reshape.26.val_ref), custom_call_target="tpu_custom_call" | custom-call | tf_op jit(solution)/shard_map/pallas_call | solution.py:151
  73.6 4.3 %collective-permute-start = (f32[32,4096]{1,0:T(8,128)}, f32[32,4096]{1,0:T(8,128)S(1)}, u32[]{:S(2)}, u32[]{:S(2)}) collective-permute-start(f32[32,4096]{1,0:T(8,128)} %get-tuple-element.8), channel_id=1, source_target_pairs={{0,1},{1,2},{2,3},{3,4},{4,5},{5,6},{6,7},{8,9},{9,10},{10,11},{11... | collective-permute-start | bytes 1572872 | tf_op jit(solution)/shard_map/ppermute | solution.py:157
  77.9 1.9 %collective-permute-start.1 = (f32[32,4096]{1,0:T(8,128)}, f32[32,4096]{1,0:T(8,128)S(1)}, u32[]{:S(2)}, u32[]{:S(2)}) collective-permute-start(f32[32,4096]{1,0:T(8,128)} %get-tuple-element.9), channel_id=1, source_target_pairs={{1,0},{2,1},{3,2},{4,3},{5,4},{6,5},{7,6},{9,8},{10,9},{11,10},{12... | collective-permute-start | bytes 1572872 | tf_op jit(solution)/shard_map/ppermute | solution.py:158
  79.8 0.9 pad_maximum_fusion.d_ref
  80.7 8.0 %collective-permute-done.fa_ref = f32[32,4096]{1,0:T(8,128)S(1)} collective-permute-done((f32[32,4096]{1,0:T(8,128)}, f32[32,4096]{1,0:T(8,128)S(1)}, u32[]{:S(2)}, u32[]{:S(2)}) %collective-permute-start) | collective-permute-done | bytes 524320 | tf_op jit(solution)/shard_map/ppermute | solution.py:157
  88.7 7.6 %collective-permute-done.1.fb_ref = f32[32,4096]{1,0:T(8,128)S(1)} collective-permute-done((f32[32,4096]{1,0:T(8,128)}, f32[32,4096]{1,0:T(8,128)S(1)}, u32[]{:S(2)}, u32[]{:S(2)}) %collective-permute-start.1) | collective-permute-done | bytes 524320 | tf_op jit(solution)/shard_map/ppermute | solution.py:158
  96.4 0.8 copy-done.2
  97.2 6.1 %shard_map.65 = f32[3,16,4096]{2,1,0:T(8,128)} custom-call(f32[32,4096]{1,0:T(8,128)} %copy-done.1, f32[32,4096]{1,0:T(8,128)} %copy-done.2, f32[16,4096]{1,0:T(8,128)} %bitcast.28, f32[16,4096]{1,0:T(8,128)} %get-tuple-element.17.u_ref, f32[16,4096]{1,0:T(8,128)} %get-tuple-element.16.v_ref, f32[32,4096]{1,0:T(8,128)} %get-tuple-element.10.pf_ref, ...), custom_call_target="tpu_custom_call" | custom-call | tf_op jit(solution)/shard_map/pallas_call | solution.py:161
  (14 shorter events, 0.1 us)
Async XLA Ops:
  40.3 3.8 %copy-start = (f32[16,4096]{1,0:T(8,128)S(1)}, f32[16,4096]{1,0:T(8,128)}, u32[]{:S(2)}) copy-start(f32[16,4096]{1,0:T(8,128)} %param.8) | copy-start | bytes 786436
  40.3 27.1 %all-to-all-start.1 = ((f32[32,48,128]{2,1,0:T(8,128)}), f32[32,48,128]{2,1,0:T(8,128)S(1)}, u32[]{:S(2)}, u32[]{:S(2)}) async-start(f32[32,48,128]{2,1,0:T(8,128)} %gather_fusion), calls=%async_computation.1 | async-start | bytes 1572864 | tf_op jit(solution)/shard_map/all_to_all | solution.py:132
  44.1 6.3 %copy-start.4 = (s32[2048]{0:T(1024)S(1)}, s32[2048]{0:T(1024)}, u32[]{:S(2)}) copy-start(s32[2048]{0:T(1024)} %param.9) | copy-start | bytes 24580
  44.2 6.3 %copy-start.3 = (s32[2048]{0:T(1024)S(1)}, s32[2048]{0:T(1024)}, u32[]{:S(2)}) copy-start(s32[2048]{0:T(1024)} %param.10) | copy-start | bytes 24580
  44.2 35.6 %collective-permute-start.2 = (f32[8,4096]{1,0:T(8,128)S(1)}, f32[8,4096]{1,0:T(8,128)S(1)}, u32[]{:S(2)}, u32[]{:S(2)}) collective-permute-start(f32[8,4096]{1,0:T(8,128)S(1)} %get-tuple-element.14), channel_id=1, source_target_pairs={{0,1},{1,2},{2,3},{3,4},{4,5},{5,6},{6,7},{8,9},{9,10},{10,11},{11... | collective-permute-start | bytes 393224 | tf_op jit(solution)/shard_map/ppermute | solution.py:142
  48.5 31.3 %collective-permute-start.3 = (f32[8,4096]{1,0:T(8,128)S(1)}, f32[8,4096]{1,0:T(8,128)S(1)}, u32[]{:S(2)}, u32[]{:S(2)}) collective-permute-start(f32[8,4096]{1,0:T(8,128)S(1)} %get-tuple-element.15), channel_id=1, source_target_pairs={{1,0},{2,1},{3,2},{4,3},{5,4},{6,5},{7,6},{9,8},{10,9},{11,10},{12... | collective-permute-start | bytes 393224 | tf_op jit(solution)/shard_map/ppermute | solution.py:144
  73.6 15.1 %collective-permute-start = (f32[32,4096]{1,0:T(8,128)}, f32[32,4096]{1,0:T(8,128)S(1)}, u32[]{:S(2)}, u32[]{:S(2)}) collective-permute-start(f32[32,4096]{1,0:T(8,128)} %get-tuple-element.8), channel_id=1, source_target_pairs={{0,1},{1,2},{2,3},{3,4},{4,5},{5,6},{6,7},{8,9},{9,10},{10,11},{11... | collective-permute-start | bytes 1572872 | tf_op jit(solution)/shard_map/ppermute | solution.py:157
  77.9 18.5 %collective-permute-start.1 = (f32[32,4096]{1,0:T(8,128)}, f32[32,4096]{1,0:T(8,128)S(1)}, u32[]{:S(2)}, u32[]{:S(2)}) collective-permute-start(f32[32,4096]{1,0:T(8,128)} %get-tuple-element.9), channel_id=1, source_target_pairs={{1,0},{2,1},{3,2},{4,3},{5,4},{6,5},{7,6},{9,8},{10,9},{11,10},{12... | collective-permute-start | bytes 1572872 | tf_op jit(solution)/shard_map/ppermute | solution.py:158
  88.7 7.6 %copy-start.1 = (f32[32,4096]{1,0:T(8,128)}, f32[32,4096]{1,0:T(8,128)S(1)}, u32[]{:S(2)}) copy-start(f32[32,4096]{1,0:T(8,128)S(1)} %collective-permute-done.fa_ref) | copy-start | bytes 1572868
  96.4 0.8 copy-start.2

commit v7 on v5

--- a/solution.py
+++ b/solution.py
@@ -93,7 +93,7 @@
     tag = jnp.broadcast_to(ancestors.astype(jnp.float32)[:, None, None], (parts, 8, columns // parts))
     crossed = lax.all_to_all(jnp.concatenate([block, tag], axis=1), "dom", 0, 0, tiled=True)
     lineage = crossed[:, fields * rows, 0].astype(jnp.int32)
-    chosen = jnp.take(crossed[:, :fields * rows], lineage, axis=0)
+    chosen = jnp.take(crossed[:, :fields * rows], lineage, axis=0, mode="clip")
     back = lax.all_to_all(chosen, "dom", 0, 0, tiled=True)
     state = back.transpose(1, 0, 2).reshape(fields, rows, columns)
 

time: 102 us -> 102 us (level)
  other arithmetic: 4.65 us -> 3.63 us
where the time goes in v7:
time: 102 us; the launch traced here: 101 us
  blocking collectives  35.3 us (35%)
  starting transfers between devices  20.4 us (20%)
  waiting for transfers between devices  20 us (20%)
  local copies, waits for them, and re-layouts  14.9 us (15%)
  Pallas kernels  6.14 us (6%)
  other arithmetic  3.63 us (4%)
    all_to_all x1, blocking collectives, on_device(): lax.all_to_all(jnp.concatenate([block, tag], axis=1), 'dom', 0, 0, tiled=...  35.3 us
    scatter x1, local copies, waits for them, and re-layouts, on_device(): jnp.full((rows * columns,), jnp.nan, jnp.float32).at[position]  8.3 us
    ppermute x1, waiting for transfers between devices, on_device(): from_above = lax.ppermute(to_below, 'band', down)  7.77 us
    ppermute x1, waiting for transfers between devices, on_device(): from_below = lax.ppermute(to_above, 'band', up)  7.71 us
    pallas_call x1, Pallas kernels, on_device(): pl.pallas_call(functools.partial(forecast_kernel, total_rows=rows * bands...  6.14 us
    ppermute x1, starting transfers between devices, on_device(): lax.ppermute(sea_depth[:margin], 'band', up)  5.97 us
    ppermute x1, starting transfers between devices, on_device(): from_below = lax.ppermute(to_above, 'band', up)  5.16 us
    all_to_all x1, waiting for transfers between devices, on_device(): back = lax.all_to_all(chosen, 'dom', 0, 0, tiled=True)  4.48 us
  transfers between devices with their start and end apart: 5, of which 3 were waited for; matrix products, arithmetic and copies ran while one was open for 10% of the time, Pallas kernels for 0%

profile of v7, /device:TPU:36, one launch (start us, length us, event | category | flops | bytes accessed | tf_op | source)
XLA Modules:
  0.0 101.2 jit_solution(13821831954529722417)
XLA Ops:
  0.0 1.3 %copy.27 = f32[6,8,32,128]{3,2,1,0:T(8,128)S(1)} copy(f32[6,8,32,128]{3,1,2,0:T(8,128)} %bitcast.47) | data formatting | bytes 1572864
  1.3 0.5 copy.34
  2.4 0.1 concatenate.12
  2.5 35.3 %all_to_all.10 = f32[32,56,128]{2,1,0:T(8,128)S(1)} all-to-all(f32[32,56,128]{2,1,0:T(8,128)S(1)} %concatenate.12), channel_id=1, replica_groups=mesh['dom'=32,'band'=8] {'dom'}, dimensions={0} | all-to-all | bytes 1835008 | tf_op jit(solution)/shard_map/all_to_all | solution.py:94
  37.8 0.7 fusion.49
  38.4 0.1 slice.233
  38.5 1.5 %gather_fusion = f32[32,48,128]{2,1,0:T(8,128)} fusion(f32[32,48,128]{2,1,0:T(8,128)S(1)} %slice.233, s32[1024]{0:T(1024)S(1)} %pad_clamp_fusion), kind=kCustom, calls=%fused_computation | custom fusion | bytes 1572992 | tf_op jit(solution)/shard_map/jit(_take)/gather | solution.py:96
  40.0 3.8 %all-to-all-start.1 = ((f32[32,48,128]{2,1,0:T(8,128)}), f32[32,48,128]{2,1,0:T(8,128)S(1)}, u32[]{:S(2)}, u32[]{:S(2)}) async-start(f32[32,48,128]{2,1,0:T(8,128)} %gather_fusion), calls=%async_computation.1 | async-start | bytes 1572864 | tf_op jit(solution)/shard_map/all_to_all | solution.py:97
  43.9 3.5 %collective-permute-start.2 = (f32[8,4096]{1,0:T(8,128)S(1)}, f32[8,4096]{1,0:T(8,128)S(1)}, u32[]{:S(2)}, u32[]{:S(2)}) collective-permute-start(f32[8,4096]{1,0:T(8,128)S(1)} %get-tuple-element.16), channel_id=1, source_target_pairs={{0,1},{1,2},{2,3},{3,4},{4,5},{5,6},{6,7},{8,9},{9,10},{10,11},{11... | collective-permute-start | bytes 393224 | tf_op jit(solution)/shard_map/ppermute | solution.py:107
  47.4 6.0 %collective-permute-start.3 = (f32[8,4096]{1,0:T(8,128)S(1)}, f32[8,4096]{1,0:T(8,128)S(1)}, u32[]{:S(2)}, u32[]{:S(2)}) collective-permute-start(f32[8,4096]{1,0:T(8,128)S(1)} %get-tuple-element.17), channel_id=1, source_target_pairs={{1,0},{2,1},{3,2},{4,3},{5,4},{6,5},{7,6},{9,8},{10,9},{11,10},{12... | collective-permute-start | bytes 393224 | tf_op jit(solution)/shard_map/ppermute | solution.py:109
  53.4 8.3 %scatter_custom_fusion = f32[65536]{0:T(1024)S(1)} fusion(s32[2048]{0:T(1024)S(1)} %compare_select_fusion, f32[2048]{0:T(1024)} %param.11, f32[]{:T(128)} %constant.16.clone.1), kind=kCustom, calls=%fused_computation.92 | custom fusion | bytes 262656 | tf_op jit(solution)/shard_map/scatter | solution.py:102
  61.8 0.8 pad_maximum_fusion.2.d_ref
  62.6 4.5 %all-to-all-done.1 = f32[32,48,128]{2,1,0:T(8,128)S(1)} async-done(((f32[32,48,128]{2,1,0:T(8,128)}), f32[32,48,128]{2,1,0:T(8,128)S(1)}, u32[]{:S(2)}, u32[]{:S(2)}) %all-to-all-start.1) | async-done | bytes 786464 | tf_op jit(solution)/shard_map/all_to_all | solution.py:97
  67.2 0.7 copy.35
  68.0 1.1 %multiply_add_fusion = f32[16,4096]{1,0:T(8,128)S(1)} fusion(f32[16,4096]{1,0:T(8,128)S(1)} %subtract_select_fusion), kind=kLoop, calls=%fused_computation.60 | loop fusion | flops 2097152 | bytes 524288 | tf_op jit(solution)/shard_map/add | solution.py:32
  69.2 0.8 fusion.16.pf_ref
  70.0 0.7 copy-done
  70.8 5.2 %collective-permute-start.1 = (f32[32,4096]{1,0:T(8,128)S(1)}, f32[32,4096]{1,0:T(8,128)S(1)}, u32[]{:S(2)}, u32[]{:S(2)}) collective-permute-start(f32[32,4096]{1,0:T(8,128)S(1)} %pad_maximum_fusion.1), channel_id=1, source_target_pairs={{1,0},{2,1},{3,2},{4,3},{5,4},{6,5},{7,6},{9,8},{10,9},{11,10},{12... | collective-permute-start | bytes 1572872 | tf_op jit(solution)/shard_map/ppermute | solution.py:138
  76.0 1.9 %collective-permute-start = (f32[32,4096]{1,0:T(8,128)S(1)}, f32[32,4096]{1,0:T(8,128)S(1)}, u32[]{:S(2)}, u32[]{:S(2)}) collective-permute-start(f32[32,4096]{1,0:T(8,128)S(1)} %pad_maximum_fusion), channel_id=1, source_target_pairs={{0,1},{1,2},{2,3},{3,4},{4,5},{5,6},{6,7},{8,9},{9,10},{10,11},{11... | collective-permute-start | bytes 1572872 | tf_op jit(solution)/shard_map/ppermute | solution.py:137
  78.0 0.8 copy_bitcast_fusion.1
  78.8 7.7 %collective-permute-done.1.fb_ref = f32[32,4096]{1,0:T(8,128)S(1)} collective-permute-done((f32[32,4096]{1,0:T(8,128)S(1)}, f32[32,4096]{1,0:T(8,128)S(1)}, u32[]{:S(2)}, u32[]{:S(2)}) %collective-permute-start.1) | collective-permute-done | bytes 524320 | tf_op jit(solution)/shard_map/ppermute | solution.py:138
  86.5 7.8 %collective-permute-done.fa_ref = f32[32,4096]{1,0:T(8,128)S(1)} collective-permute-done((f32[32,4096]{1,0:T(8,128)S(1)}, f32[32,4096]{1,0:T(8,128)S(1)}, u32[]{:S(2)}, u32[]{:S(2)}) %collective-permute-start) | collective-permute-done | bytes 524320 | tf_op jit(solution)/shard_map/ppermute | solution.py:137
  94.3 0.8 copy-done.3
  95.1 6.1 %shard_map.64 = f32[3,16,4096]{2,1,0:T(8,128)} custom-call(f32[32,4096]{1,0:T(8,128)} %copy-done.3, f32[32,4096]{1,0:T(8,128)} %copy-done.2, f32[16,4096]{1,0:T(8,128)} %bitcast.46, f32[16,4096]{1,0:T(8,128)} %get-tuple-element.19.u_ref, f32[16,4096]{1,0:T(8,128)} %get-tuple-element.18.v_ref, f32[32,4096]{1,0:T(8,128)} %copy-done, ...), custom_call_target="tpu_custom_call" | custom-call | tf_op jit(solution)/shard_map/pallas_call | solution.py:141
  (23 shorter events, 0.4 us)
Async XLA Ops:
  40.0 3.8 %copy-start.1 = (f32[16,4096]{1,0:T(8,128)S(1)}, f32[16,4096]{1,0:T(8,128)}, u32[]{:S(2)}) copy-start(f32[16,4096]{1,0:T(8,128)} %param.8) | copy-start | bytes 786436
  40.0 27.1 %all-to-all-start.1 = ((f32[32,48,128]{2,1,0:T(8,128)}), f32[32,48,128]{2,1,0:T(8,128)S(1)}, u32[]{:S(2)}, u32[]{:S(2)}) async-start(f32[32,48,128]{2,1,0:T(8,128)} %gather_fusion), calls=%async_computation.1 | async-start | bytes 1572864 | tf_op jit(solution)/shard_map/all_to_all | solution.py:97
  43.8 9.5 %copy-start.5 = (s32[2048]{0:T(1024)S(1)}, s32[2048]{0:T(1024)}, u32[]{:S(2)}) copy-start(s32[2048]{0:T(1024)} %param.9) | copy-start | bytes 24580
  43.9 9.5 %copy-start.4 = (s32[2048]{0:T(1024)S(1)}, s32[2048]{0:T(1024)}, u32[]{:S(2)}) copy-start(s32[2048]{0:T(1024)} %param.10) | copy-start | bytes 24580
  43.9 17.9 %collective-permute-start.2 = (f32[8,4096]{1,0:T(8,128)S(1)}, f32[8,4096]{1,0:T(8,128)S(1)}, u32[]{:S(2)}, u32[]{:S(2)}) collective-permute-start(f32[8,4096]{1,0:T(8,128)S(1)} %get-tuple-element.16), channel_id=1, source_target_pairs={{0,1},{1,2},{2,3},{3,4},{4,5},{5,6},{6,7},{8,9},{9,10},{10,11},{11... | collective-permute-start | bytes 393224 | tf_op jit(solution)/shard_map/ppermute | solution.py:107
  47.4 14.4 %collective-permute-start.3 = (f32[8,4096]{1,0:T(8,128)S(1)}, f32[8,4096]{1,0:T(8,128)S(1)}, u32[]{:S(2)}, u32[]{:S(2)}) collective-permute-start(f32[8,4096]{1,0:T(8,128)S(1)} %get-tuple-element.17), channel_id=1, source_target_pairs={{1,0},{2,1},{3,2},{4,3},{5,4},{6,5},{7,6},{9,8},{10,9},{11,10},{12... | collective-permute-start | bytes 393224 | tf_op jit(solution)/shard_map/ppermute | solution.py:109
  70.0 0.8 copy-start
  70.8 15.7 %collective-permute-start.1 = (f32[32,4096]{1,0:T(8,128)S(1)}, f32[32,4096]{1,0:T(8,128)S(1)}, u32[]{:S(2)}, u32[]{:S(2)}) collective-permute-start(f32[32,4096]{1,0:T(8,128)S(1)} %pad_maximum_fusion.1), channel_id=1, source_target_pairs={{1,0},{2,1},{3,2},{4,3},{5,4},{6,5},{7,6},{9,8},{10,9},{11,10},{12... | collective-permute-start | bytes 1572872 | tf_op jit(solution)/shard_map/ppermute | solution.py:138
  76.0 18.3 %collective-permute-start = (f32[32,4096]{1,0:T(8,128)S(1)}, f32[32,4096]{1,0:T(8,128)S(1)}, u32[]{:S(2)}, u32[]{:S(2)}) collective-permute-start(f32[32,4096]{1,0:T(8,128)S(1)} %pad_maximum_fusion), channel_id=1, source_target_pairs={{0,1},{1,2},{2,3},{3,4},{4,5},{5,6},{6,7},{8,9},{9,10},{10,11},{11... | collective-permute-start | bytes 1572872 | tf_op jit(solution)/shard_map/ppermute | solution.py:137
  86.5 7.8 %copy-start.2 = (f32[32,4096]{1,0:T(8,128)}, f32[32,4096]{1,0:T(8,128)S(1)}, u32[]{:S(2)}) copy-start(f32[32,4096]{1,0:T(8,128)S(1)} %collective-permute-done.1.fb_ref) | copy-start | bytes 1572868
  94.3 0.8 copy-start.3

commit v8 on v7

--- a/solution.py
+++ b/solution.py
@@ -134,8 +134,10 @@
         ],
         axis=0,
     )
-    from_above = lax.ppermute(to_below, "band", down)
-    from_below = lax.ppermute(to_above, "band", up)
+    ring_down = [(i, (i + 1) % bands) for i in range(bands)]
+    ring_up = [((i + 1) % bands, i) for i in range(bands)]
+    from_above = jnp.where(band > 0, lax.ppermute(to_below, "band", ring_down), jnp.float32(0.0))
+    from_below = jnp.where(band < bands - 1, lax.ppermute(to_above, "band", ring_up), jnp.float32(0.0))
 
     ext_rows = rows + 2 * margin
     out = pl.pallas_call(

time: 102 us -> 100 us (0.980)
  the two profiles are of different devices: /device:TPU:36 before, /device:TPU:32 now
where the time goes in v8:
time: 100 us; the launch traced here: 99.9 us
  blocking collectives  35.6 us (36%)
  waiting for transfers between devices  23.9 us (24%)
  local copies, waits for them, and re-layouts  14.2 us (14%)
  starting transfers between devices  14 us (14%)
  Pallas kernels  6.14 us (6%)
  other arithmetic  5.27 us (5%)
    all_to_all x1, blocking collectives, on_device(): lax.all_to_all(jnp.concatenate([block, tag], axis=1), 'dom', 0, 0, tiled=...  35.6 us
    ppermute x1, waiting for transfers between devices, on_device(): lax.ppermute(to_above, 'band', ring_up)  9.58 us
    all_to_all x1, waiting for transfers between devices, on_device(): back = lax.all_to_all(chosen, 'dom', 0, 0, tiled=True)  9.16 us
    scatter x1, local copies, waits for them, and re-layouts, on_device(): jnp.full((rows * columns,), jnp.nan, jnp.float32).at[position]  8.3 us
    pallas_call x1, Pallas kernels, on_device(): pl.pallas_call(functools.partial(forecast_kernel, total_rows=rows * bands...  6.14 us
    ppermute x1, starting transfers between devices, on_device(): lax.ppermute(to_above, 'band', ring_up)  5.26 us
    ppermute x1, waiting for transfers between devices, on_device(): lax.ppermute(to_below, 'band', ring_down)  5.11 us
    all_to_all x1, starting transfers between devices, on_device(): back = lax.all_to_all(chosen, 'dom', 0, 0, tiled=True)  3.83 us
  transfers between devices with their start and end apart: 5, of which 3 were waited for; matrix products, arithmetic and copies ran while one was open for 11% of the time, Pallas kernels for 0%

profile of v8, /device:TPU:32, one launch (start us, length us, event | category | flops | bytes accessed | tf_op | source)
XLA Modules:
  0.0 99.9 jit_solution(4214294749337023673)
XLA Ops:
  0.0 1.3 %copy.27 = f32[6,8,32,128]{3,2,1,0:T(8,128)S(1)} copy(f32[6,8,32,128]{3,1,2,0:T(8,128)} %bitcast.47) | data formatting | bytes 1572864
  1.3 0.5 copy.34
  2.4 0.1 concatenate.12
  2.5 35.6 %all_to_all.10 = f32[32,56,128]{2,1,0:T(8,128)S(1)} all-to-all(f32[32,56,128]{2,1,0:T(8,128)S(1)} %concatenate.12), channel_id=1, replica_groups=mesh['dom'=32,'band'=8] {'dom'}, dimensions={0} | all-to-all | bytes 1835008 | tf_op jit(solution)/shard_map/all_to_all | solution.py:94
  38.1 0.7 fusion.49
  38.8 1.5 %gather_fusion = f32[32,48,128]{2,1,0:T(8,128)} fusion(f32[32,48,128]{2,1,0:T(8,128)S(1)} %slice.233, s32[1024]{0:T(1024)S(1)} %pad_clamp_fusion), kind=kCustom, calls=%fused_computation | custom fusion | bytes 1572992 | tf_op jit(solution)/shard_map/jit(_take)/gather | solution.py:96
  40.3 3.8 %all-to-all-start.1 = ((f32[32,48,128]{2,1,0:T(8,128)}), f32[32,48,128]{2,1,0:T(8,128)S(1)}, u32[]{:S(2)}, u32[]{:S(2)}) async-start(f32[32,48,128]{2,1,0:T(8,128)} %gather_fusion), calls=%async_computation.1 | async-start | bytes 1572864 | tf_op jit(solution)/shard_map/all_to_all | solution.py:97
  44.2 3.5 %collective-permute-start.2 = (f32[8,4096]{1,0:T(8,128)S(1)}, f32[8,4096]{1,0:T(8,128)S(1)}, u32[]{:S(2)}, u32[]{:S(2)}) collective-permute-start(f32[8,4096]{1,0:T(8,128)S(1)} %get-tuple-element.16), channel_id=1, source_target_pairs={{0,1},{1,2},{2,3},{3,4},{4,5},{5,6},{6,7},{8,9},{9,10},{10,11},{11... | collective-permute-start | bytes 393224 | tf_op jit(solution)/shard_map/ppermute | solution.py:107
  47.7 1.3 %collective-permute-start.3 = (f32[8,4096]{1,0:T(8,128)S(1)}, f32[8,4096]{1,0:T(8,128)S(1)}, u32[]{:S(2)}, u32[]{:S(2)}) collective-permute-start(f32[8,4096]{1,0:T(8,128)S(1)} %get-tuple-element.17), channel_id=1, source_target_pairs={{1,0},{2,1},{3,2},{4,3},{5,4},{6,5},{7,6},{9,8},{10,9},{11,10},{12... | collective-permute-start | bytes 393224 | tf_op jit(solution)/shard_map/ppermute | solution.py:109
  49.0 8.3 %scatter_custom_fusion = f32[65536]{0:T(1024)S(1)} fusion(s32[2048]{0:T(1024)S(1)} %compare_select_fusion, f32[2048]{0:T(1024)} %param.11, f32[]{:T(128)} %constant.19.clone.1), kind=kCustom, calls=%fused_computation.94 | custom fusion | bytes 262656 | tf_op jit(solution)/shard_map/scatter | solution.py:102
  57.4 0.8 pad_maximum_fusion.2.d_ref
  58.2 9.2 %all-to-all-done.1 = f32[32,48,128]{2,1,0:T(8,128)S(1)} async-done(((f32[32,48,128]{2,1,0:T(8,128)}), f32[32,48,128]{2,1,0:T(8,128)S(1)}, u32[]{:S(2)}, u32[]{:S(2)}) %all-to-all-start.1) | async-done | bytes 786464 | tf_op jit(solution)/shard_map/all_to_all | solution.py:97
  67.5 0.7 copy.35
  68.3 1.1 %multiply_add_fusion = f32[16,4096]{1,0:T(8,128)S(1)} fusion(f32[16,4096]{1,0:T(8,128)S(1)} %subtract_select_fusion), kind=kLoop, calls=%fused_computation.62 | loop fusion | flops 2097152 | bytes 524288 | tf_op jit(solution)/shard_map/add | solution.py:32
  69.5 0.8 fusion.16.pf_ref
  70.3 0.8 copy-done
  71.2 5.3 %collective-permute-start.1 = (f32[32,4096]{1,0:T(8,128)S(1)}, f32[32,4096]{1,0:T(8,128)S(1)}, u32[]{:S(2)}, u32[]{:S(2)}) collective-permute-start(f32[32,4096]{1,0:T(8,128)S(1)} %pad_maximum_fusion.1), channel_id=1, source_target_pairs={{1,0},{2,1},{3,2},{4,3},{5,4},{6,5},{7,6},{0,7},{9,8},{10,9},{11,1... | collective-permute-start | bytes 1572872 | tf_op jit(solution)/shard_map/ppermute | solution.py:140
  76.5 0.1 collective-permute-start
  76.5 0.8 copy_bitcast_fusion.1
  77.4 9.6 %collective-permute-done.1 = f32[32,4096]{1,0:T(8,128)S(1)} collective-permute-done((f32[32,4096]{1,0:T(8,128)S(1)}, f32[32,4096]{1,0:T(8,128)S(1)}, u32[]{:S(2)}, u32[]{:S(2)}) %collective-permute-start.1) | collective-permute-done | bytes 524320 | tf_op jit(solution)/shard_map/ppermute | solution.py:140
  87.0 0.8 broadcast_select_fusion.fb_ref
  87.8 5.1 %collective-permute-done = f32[32,4096]{1,0:T(8,128)S(1)} collective-permute-done((f32[32,4096]{1,0:T(8,128)S(1)}, f32[32,4096]{1,0:T(8,128)S(1)}, u32[]{:S(2)}, u32[]{:S(2)}) %collective-permute-start) | collective-permute-done | bytes 524320 | tf_op jit(solution)/shard_map/ppermute | solution.py:139
  92.9 0.8 broadcast_select_fusion.1.fa_ref
  93.7 6.1 %shard_map.64 = f32[3,16,4096]{2,1,0:T(8,128)} custom-call(f32[32,4096]{1,0:T(8,128)} %broadcast_select_fusion.1.fa_ref, f32[32,4096]{1,0:T(8,128)} %broadcast_select_fusion.fb_ref, f32[16,4096]{1,0:T(8,128)} %bitcast.46, f32[16,4096]{1,0:T(8,128)} %get-tuple-element.19.u_ref, f32[16,4096]{1,0:T(8,128)} %get-tuple-element.18.v_ref, f32[32,4096]{1,0:T(8,128)} %copy-done, ...), custom_call_target="tpu_custom_call" | custom-call | tf_op jit(solution)/shard_map/pallas_call | solution.py:143
  (21 shorter events, 0.5 us)
Async XLA Ops:
  40.3 3.8 %copy-start.1 = (f32[16,4096]{1,0:T(8,128)S(1)}, f32[16,4096]{1,0:T(8,128)}, u32[]{:S(2)}) copy-start(f32[16,4096]{1,0:T(8,128)} %param.8) | copy-start | bytes 786436
  40.3 27.1 %all-to-all-start.1 = ((f32[32,48,128]{2,1,0:T(8,128)}), f32[32,48,128]{2,1,0:T(8,128)S(1)}, u32[]{:S(2)}, u32[]{:S(2)}) async-start(f32[32,48,128]{2,1,0:T(8,128)} %gather_fusion), calls=%async_computation.1 | async-start | bytes 1572864 | tf_op jit(solution)/shard_map/all_to_all | solution.py:97
  44.1 4.9 %copy-start.3 = (s32[2048]{0:T(1024)S(1)}, s32[2048]{0:T(1024)}, u32[]{:S(2)}) copy-start(s32[2048]{0:T(1024)} %param.9) | copy-start | bytes 24580
  44.2 4.8 %copy-start.2 = (s32[2048]{0:T(1024)S(1)}, s32[2048]{0:T(1024)}, u32[]{:S(2)}) copy-start(s32[2048]{0:T(1024)} %param.10) | copy-start | bytes 24580
  44.2 13.2 %collective-permute-start.2 = (f32[8,4096]{1,0:T(8,128)S(1)}, f32[8,4096]{1,0:T(8,128)S(1)}, u32[]{:S(2)}, u32[]{:S(2)}) collective-permute-start(f32[8,4096]{1,0:T(8,128)S(1)} %get-tuple-element.16), channel_id=1, source_target_pairs={{0,1},{1,2},{2,3},{3,4},{4,5},{5,6},{6,7},{8,9},{9,10},{10,11},{11... | collective-permute-start | bytes 393224 | tf_op jit(solution)/shard_map/ppermute | solution.py:107
  47.7 9.7 %collective-permute-start.3 = (f32[8,4096]{1,0:T(8,128)S(1)}, f32[8,4096]{1,0:T(8,128)S(1)}, u32[]{:S(2)}, u32[]{:S(2)}) collective-permute-start(f32[8,4096]{1,0:T(8,128)S(1)} %get-tuple-element.17), channel_id=1, source_target_pairs={{1,0},{2,1},{3,2},{4,3},{5,4},{6,5},{7,6},{9,8},{10,9},{11,10},{12... | collective-permute-start | bytes 393224 | tf_op jit(solution)/shard_map/ppermute | solution.py:109
  70.3 0.8 copy-start
  71.2 15.8 %collective-permute-start.1 = (f32[32,4096]{1,0:T(8,128)S(1)}, f32[32,4096]{1,0:T(8,128)S(1)}, u32[]{:S(2)}, u32[]{:S(2)}) collective-permute-start(f32[32,4096]{1,0:T(8,128)S(1)} %pad_maximum_fusion.1), channel_id=1, source_target_pairs={{1,0},{2,1},{3,2},{4,3},{5,4},{6,5},{7,6},{0,7},{9,8},{10,9},{11,1... | collective-permute-start | bytes 1572872 | tf_op jit(solution)/shard_map/ppermute | solution.py:140
  76.5 16.4 %collective-permute-start = (f32[32,4096]{1,0:T(8,128)S(1)}, f32[32,4096]{1,0:T(8,128)S(1)}, u32[]{:S(2)}, u32[]{:S(2)}) collective-permute-start(f32[32,4096]{1,0:T(8,128)S(1)} %pad_maximum_fusion), channel_id=1, source_target_pairs={{0,1},{1,2},{2,3},{3,4},{4,5},{5,6},{6,7},{7,0},{8,9},{9,10},{10,1... | collective-permute-start | bytes 1572872 | tf_op jit(solution)/shard_map/ppermute | solution.py:139

commit v9 on v8

--- a/solution.py
+++ b/solution.py
@@ -40,16 +40,26 @@
     ext = rows + 2 * margin
     columns = h_ref.shape[1]
     half = rows // 2
-    hx_ref[0:margin] = fa_ref[2 * margin:3 * margin] + NUDGE_GAIN * pf_ref[0:margin]
+    band = lax.axis_index("band")
+    keep_above = jnp.where(band > 0, jnp.float32(1.0), jnp.float32(0.0))
+    keep_below = jnp.where(band < total_rows // rows - 1, jnp.float32(1.0), jnp.float32(0.0))
+
+    def above(lo, hi):
+        return fa_ref[lo:hi] * keep_above
+
+    def below(lo, hi):
+        return fb_ref[lo:hi] * keep_below
+
+    hx_ref[0:margin] = above(2 * margin, 3 * margin) + NUDGE_GAIN * pf_ref[0:margin]
     hx_ref[margin:margin + half] = h_ref[0:half] + NUDGE_GAIN * (
-        pf_ref[margin:margin + half] + fa_ref[margin:2 * margin])
+        pf_ref[margin:margin + half] + above(margin, 2 * margin))
     hx_ref[margin + half:margin + rows] = h_ref[half:rows] + NUDGE_GAIN * (
-        pf_ref[margin + half:margin + rows] + fb_ref[margin:2 * margin])
-    hx_ref[margin + rows:ext] = fb_ref[2 * margin:3 * margin] + NUDGE_GAIN * pf_ref[margin + rows:ext]
+        pf_ref[margin + half:margin + rows] + below(margin, 2 * margin))
+    hx_ref[margin + rows:ext] = below(2 * margin, 3 * margin) + NUDGE_GAIN * pf_ref[margin + rows:ext]
     height = hx_ref[...]
-    east_vel = jnp.concatenate([fa_ref[3 * margin:4 * margin], u_ref[...], fb_ref[3 * margin:4 * margin]], axis=0)
-    north_vel = jnp.concatenate([fa_ref[0:margin], v_ref[...], fb_ref[0:margin]], axis=0)
-    band_start = lax.axis_index("band") * rows
+    east_vel = jnp.concatenate([above(3 * margin, 4 * margin), u_ref[...], below(3 * margin, 4 * margin)], axis=0)
+    north_vel = jnp.concatenate([above(0, margin), v_ref[...], below(0, margin)], axis=0)
+    band_start = band * rows
     global_rows = band_start - margin + lax.broadcasted_iota(jnp.int32, (ext, columns), 0)
     inside = (global_rows >= 0) & (global_rows < total_rows)
     coriolis = 0.1 + 0.4 * ((global_rows.astype(jnp.float32) + 0.5) / total_rows)
@@ -136,8 +146,8 @@
     )
     ring_down = [(i, (i + 1) % bands) for i in range(bands)]
     ring_up = [((i + 1) % bands, i) for i in range(bands)]
-    from_above = jnp.where(band > 0, lax.ppermute(to_below, "band", ring_down), jnp.float32(0.0))
-    from_below = jnp.where(band < bands - 1, lax.ppermute(to_above, "band", ring_up), jnp.float32(0.0))
+    from_above = lax.ppermute(to_below, "band", ring_down)
+    from_below = lax.ppermute(to_above, "band", ring_up)
 
     ext_rows = rows + 2 * margin
     out = pl.pallas_call(

time: 100 us -> 100 us (level)
  other arithmetic: 5.27 us -> 3.63 us
    select_n x2 -> x0, other arithmetic: 1.64 us -> none  [the longest x1 0.83 us: on_device(): jnp.where(band > 0, lax.ppermute(to_below, 'band', ring_down), jnp.float3...]
    unnamed x10 -> x14, local copies, waits for them, and re-layouts: 2.12 us -> 2.9 us
  transfers between devices with their start and end apart: 5 -> 5, of which waited for: 3 -> 3; matrix products, arithmetic and copies ran while one was open for 11% -> 10% of each run, Pallas kernels for 0% -> 0%
where the time goes in v9:
time: 100 us; the launch traced here: 99.8 us
  blocking collectives  35.6 us (36%)
  waiting for transfers between devices  24.7 us (25%)
  local copies, waits for them, and re-layouts  14.9 us (15%)
  starting transfers between devices  14 us (14%)
  Pallas kernels  6.14 us (6%)
  other arithmetic  3.63 us (4%)
    all_to_all x1, blocking collectives, on_device(): lax.all_to_all(jnp.concatenate([block, tag], axis=1), 'dom', 0, 0, tiled=...  35.6 us
    ppermute x1, waiting for transfers between devices, on_device(): from_below = lax.ppermute(to_above, 'band', ring_up)  9.57 us
    all_to_all x1, waiting for transfers between devices, on_device(): back = lax.all_to_all(chosen, 'dom', 0, 0, tiled=True)  9.16 us
    scatter x1, local copies, waits for them, and re-layouts, on_device(): jnp.full((rows * columns,), jnp.nan, jnp.float32).at[position]  8.3 us
    pallas_call x1, Pallas kernels, on_device(): pl.pallas_call(functools.partial(forecast_kernel, total_rows=rows * bands...  6.14 us
    ppermute x1, waiting for transfers between devices, on_device(): from_above = lax.ppermute(to_below, 'band', ring_down)  5.93 us
    ppermute x1, starting transfers between devices, on_device(): from_below = lax.ppermute(to_above, 'band', ring_up)  5.26 us
    all_to_all x1, starting transfers between devices, on_device(): back = lax.all_to_all(chosen, 'dom', 0, 0, tiled=True)  3.83 us
  transfers between devices with their start and end apart: 5, of which 3 were waited for; matrix products, arithmetic and copies ran while one was open for 10% of the time, Pallas kernels for 0%

profile of v9, /device:TPU:32, one launch (start us, length us, event | category | flops | bytes accessed | tf_op | source)
XLA Modules:
  0.0 99.8 jit_solution(14467076901613288942)
XLA Ops:
  0.0 1.3 %copy.27 = f32[6,8,32,128]{3,2,1,0:T(8,128)S(1)} copy(f32[6,8,32,128]{3,1,2,0:T(8,128)} %bitcast.47) | data formatting | bytes 1572864
  1.3 0.5 copy.34
  2.4 0.1 concatenate.12
  2.5 35.6 %all_to_all.10 = f32[32,56,128]{2,1,0:T(8,128)S(1)} all-to-all(f32[32,56,128]{2,1,0:T(8,128)S(1)} %concatenate.12), channel_id=1, replica_groups=mesh['dom'=32,'band'=8] {'dom'}, dimensions={0} | all-to-all | bytes 1835008 | tf_op jit(solution)/shard_map/all_to_all | solution.py:104
  38.1 0.7 fusion.49
  38.7 0.1 slice.233
  38.8 1.5 %gather_fusion = f32[32,48,128]{2,1,0:T(8,128)} fusion(f32[32,48,128]{2,1,0:T(8,128)S(1)} %slice.233, s32[1024]{0:T(1024)S(1)} %pad_clamp_fusion), kind=kCustom, calls=%fused_computation | custom fusion | bytes 1572992 | tf_op jit(solution)/shard_map/jit(_take)/gather | solution.py:106
  40.3 3.8 %all-to-all-start.1 = ((f32[32,48,128]{2,1,0:T(8,128)}), f32[32,48,128]{2,1,0:T(8,128)S(1)}, u32[]{:S(2)}, u32[]{:S(2)}) async-start(f32[32,48,128]{2,1,0:T(8,128)} %gather_fusion), calls=%async_computation.1 | async-start | bytes 1572864 | tf_op jit(solution)/shard_map/all_to_all | solution.py:107
  44.2 3.5 %collective-permute-start.2 = (f32[8,4096]{1,0:T(8,128)S(1)}, f32[8,4096]{1,0:T(8,128)S(1)}, u32[]{:S(2)}, u32[]{:S(2)}) collective-permute-start(f32[8,4096]{1,0:T(8,128)S(1)} %get-tuple-element.16), channel_id=1, source_target_pairs={{0,1},{1,2},{2,3},{3,4},{4,5},{5,6},{6,7},{8,9},{9,10},{10,11},{11... | collective-permute-start | bytes 393224 | tf_op jit(solution)/shard_map/ppermute | solution.py:117
  47.7 1.3 %collective-permute-start.3 = (f32[8,4096]{1,0:T(8,128)S(1)}, f32[8,4096]{1,0:T(8,128)S(1)}, u32[]{:S(2)}, u32[]{:S(2)}) collective-permute-start(f32[8,4096]{1,0:T(8,128)S(1)} %get-tuple-element.17), channel_id=1, source_target_pairs={{1,0},{2,1},{3,2},{4,3},{5,4},{6,5},{7,6},{9,8},{10,9},{11,10},{12... | collective-permute-start | bytes 393224 | tf_op jit(solution)/shard_map/ppermute | solution.py:119
  49.0 8.3 %scatter_custom_fusion = f32[65536]{0:T(1024)S(1)} fusion(s32[2048]{0:T(1024)S(1)} %compare_select_fusion, f32[2048]{0:T(1024)} %param.11, f32[]{:T(128)} %constant.16.clone.1), kind=kCustom, calls=%fused_computation.92 | custom fusion | bytes 262656 | tf_op jit(solution)/shard_map/scatter | solution.py:112
  57.4 0.8 pad_maximum_fusion.2.d_ref
  58.2 9.2 %all-to-all-done.1 = f32[32,48,128]{2,1,0:T(8,128)S(1)} async-done(((f32[32,48,128]{2,1,0:T(8,128)}), f32[32,48,128]{2,1,0:T(8,128)S(1)}, u32[]{:S(2)}, u32[]{:S(2)}) %all-to-all-start.1) | async-done | bytes 786464 | tf_op jit(solution)/shard_map/all_to_all | solution.py:107
  67.5 0.7 copy.35
  68.3 1.1 %multiply_add_fusion = f32[16,4096]{1,0:T(8,128)S(1)} fusion(f32[16,4096]{1,0:T(8,128)S(1)} %subtract_select_fusion), kind=kLoop, calls=%fused_computation.60 | loop fusion | flops 2097152 | bytes 524288 | tf_op jit(solution)/shard_map/add | solution.py:32
  69.5 0.8 fusion.16.pf_ref
  70.3 0.7 copy-done
  71.1 5.3 %collective-permute-start.1 = (f32[32,4096]{1,0:T(8,128)S(1)}, f32[32,4096]{1,0:T(8,128)S(1)}, u32[]{:S(2)}, u32[]{:S(2)}) collective-permute-start(f32[32,4096]{1,0:T(8,128)S(1)} %pad_maximum_fusion.1), channel_id=1, source_target_pairs={{1,0},{2,1},{3,2},{4,3},{5,4},{6,5},{7,6},{0,7},{9,8},{10,9},{11,1... | collective-permute-start | bytes 1572872 | tf_op jit(solution)/shard_map/ppermute | solution.py:150
  76.4 0.1 collective-permute-start
  76.5 0.8 copy_bitcast_fusion.1
  77.3 9.6 %collective-permute-done.1.fb_ref = f32[32,4096]{1,0:T(8,128)S(1)} collective-permute-done((f32[32,4096]{1,0:T(8,128)S(1)}, f32[32,4096]{1,0:T(8,128)S(1)}, u32[]{:S(2)}, u32[]{:S(2)}) %collective-permute-start.1) | collective-permute-done | bytes 524320 | tf_op jit(solution)/shard_map/ppermute | solution.py:150
  86.9 5.9 %collective-permute-done.fa_ref = f32[32,4096]{1,0:T(8,128)S(1)} collective-permute-done((f32[32,4096]{1,0:T(8,128)S(1)}, f32[32,4096]{1,0:T(8,128)S(1)}, u32[]{:S(2)}, u32[]{:S(2)}) %collective-permute-start) | collective-permute-done | bytes 524320 | tf_op jit(solution)/shard_map/ppermute | solution.py:149
  92.9 0.8 copy-done.3
  93.7 6.1 %shard_map.64 = f32[3,16,4096]{2,1,0:T(8,128)} custom-call(f32[32,4096]{1,0:T(8,128)} %copy-done.3, f32[32,4096]{1,0:T(8,128)} %copy-done.2, f32[16,4096]{1,0:T(8,128)} %bitcast.46, f32[16,4096]{1,0:T(8,128)} %get-tuple-element.19.u_ref, f32[16,4096]{1,0:T(8,128)} %get-tuple-element.18.v_ref, f32[32,4096]{1,0:T(8,128)} %copy-done, ...), custom_call_target="tpu_custom_call" | custom-call | tf_op jit(solution)/shard_map/pallas_call | solution.py:153
  (23 shorter events, 0.4 us)
Async XLA Ops:
  40.3 3.8 %copy-start.1 = (f32[16,4096]{1,0:T(8,128)S(1)}, f32[16,4096]{1,0:T(8,128)}, u32[]{:S(2)}) copy-start(f32[16,4096]{1,0:T(8,128)} %param.8) | copy-start | bytes 786436
  40.3 27.1 %all-to-all-start.1 = ((f32[32,48,128]{2,1,0:T(8,128)}), f32[32,48,128]{2,1,0:T(8,128)S(1)}, u32[]{:S(2)}, u32[]{:S(2)}) async-start(f32[32,48,128]{2,1,0:T(8,128)} %gather_fusion), calls=%async_computation.1 | async-start | bytes 1572864 | tf_op jit(solution)/shard_map/all_to_all | solution.py:107
  44.1 4.9 %copy-start.5 = (s32[2048]{0:T(1024)S(1)}, s32[2048]{0:T(1024)}, u32[]{:S(2)}) copy-start(s32[2048]{0:T(1024)} %param.9) | copy-start | bytes 24580
  44.2 4.8 %copy-start.4 = (s32[2048]{0:T(1024)S(1)}, s32[2048]{0:T(1024)}, u32[]{:S(2)}) copy-start(s32[2048]{0:T(1024)} %param.10) | copy-start | bytes 24580
  44.2 13.2 %collective-permute-start.2 = (f32[8,4096]{1,0:T(8,128)S(1)}, f32[8,4096]{1,0:T(8,128)S(1)}, u32[]{:S(2)}, u32[]{:S(2)}) collective-permute-start(f32[8,4096]{1,0:T(8,128)S(1)} %get-tuple-element.16), channel_id=1, source_target_pairs={{0,1},{1,2},{2,3},{3,4},{4,5},{5,6},{6,7},{8,9},{9,10},{10,11},{11... | collective-permute-start | bytes 393224 | tf_op jit(solution)/shard_map/ppermute | solution.py:117
  47.7 9.7 %collective-permute-start.3 = (f32[8,4096]{1,0:T(8,128)S(1)}, f32[8,4096]{1,0:T(8,128)S(1)}, u32[]{:S(2)}, u32[]{:S(2)}) collective-permute-start(f32[8,4096]{1,0:T(8,128)S(1)} %get-tuple-element.17), channel_id=1, source_target_pairs={{1,0},{2,1},{3,2},{4,3},{5,4},{6,5},{7,6},{9,8},{10,9},{11,10},{12... | collective-permute-start | bytes 393224 | tf_op jit(solution)/shard_map/ppermute | solution.py:119
  70.3 0.8 copy-start
  71.1 15.8 %collective-permute-start.1 = (f32[32,4096]{1,0:T(8,128)S(1)}, f32[32,4096]{1,0:T(8,128)S(1)}, u32[]{:S(2)}, u32[]{:S(2)}) collective-permute-start(f32[32,4096]{1,0:T(8,128)S(1)} %pad_maximum_fusion.1), channel_id=1, source_target_pairs={{1,0},{2,1},{3,2},{4,3},{5,4},{6,5},{7,6},{0,7},{9,8},{10,9},{11,1... | collective-permute-start | bytes 1572872 | tf_op jit(solution)/shard_map/ppermute | solution.py:150
  76.4 16.4 %collective-permute-start = (f32[32,4096]{1,0:T(8,128)S(1)}, f32[32,4096]{1,0:T(8,128)S(1)}, u32[]{:S(2)}, u32[]{:S(2)}) collective-permute-start(f32[32,4096]{1,0:T(8,128)S(1)} %pad_maximum_fusion), channel_id=1, source_target_pairs={{0,1},{1,2},{2,3},{3,4},{4,5},{5,6},{6,7},{7,0},{8,9},{9,10},{10,1... | collective-permute-start | bytes 1572872 | tf_op jit(solution)/shard_map/ppermute | solution.py:149
  86.9 5.9 %copy-start.2 = (f32[32,4096]{1,0:T(8,128)}, f32[32,4096]{1,0:T(8,128)S(1)}, u32[]{:S(2)}) copy-start(f32[32,4096]{1,0:T(8,128)S(1)} %collective-permute-done.1.fb_ref) | copy-start | bytes 1572868
  92.9 0.8 copy-start.3

commit v10 on v9

--- a/solution.py
+++ b/solution.py
@@ -154,11 +154,13 @@
         functools.partial(forecast_kernel, total_rows=rows * bands),
         interpret=INTERPRET,
         out_shape=jax.ShapeDtypeStruct((fields, rows, columns), jnp.float32),
+        in_specs=[pl.BlockSpec(memory_space=pltpu.VMEM)] * 7,
         scratch_shapes=[
             pltpu.VMEM((ext_rows + 16, columns), jnp.float32),
             pltpu.VMEM((ext_rows, columns), jnp.float32),
         ],
-    )(from_above, from_below, height, east_vel, north_vel, partial, depth_ext)
+    )(*[pltpu.with_memory_space_constraint(x, pltpu.VMEM)
+        for x in (from_above, from_below, height, east_vel, north_vel, partial, depth_ext)])
     return out[None]
 
 

time: 100 us -> 96.2 us (0.962)
  local copies, waits for them, and re-layouts: 14.9 us -> 11.9 us
  Pallas kernels: 6.14 us -> 4.42 us
  waiting for transfers between devices: 24.7 us -> 26.3 us
    pallas_call x1, Pallas kernels: 6.14 us -> 4.42 us  [on_device(): pl.pallas_call(functools.partial(forecast_kernel, total_rows=rows * bands...]
    unnamed x14 -> x8, local copies, waits for them, and re-layouts: 2.9 us -> 1.34 us
    squeeze x2, local copies, waits for them, and re-layouts: 1.55 us -> 0.06 us  [on_device(): height, east_vel, north_vel = (state[0], state[1], state[2])]
  transfers between devices with their start and end apart: 5 -> 5, of which waited for: 3 -> 3; matrix products, arithmetic and copies ran while one was open for 10% -> 9% of each run, Pallas kernels for 0% -> 0%
where the time goes in v10:
time: 96.2 us; the launch traced here: 95.8 us
  blocking collectives  35.6 us (37%)
  waiting for transfers between devices  26.3 us (27%)
  starting transfers between devices  14 us (15%)
  local copies, waits for them, and re-layouts  11.9 us (12%)
  Pallas kernels  4.42 us (5%)
  other arithmetic  2.82 us (3%)
    all_to_all x1, blocking collectives, on_device(): lax.all_to_all(jnp.concatenate([block, tag], axis=1), 'dom', 0, 0, tiled=...  35.6 us
    ppermute x1, waiting for transfers between devices, on_device(): from_below = lax.ppermute(to_above, 'band', ring_up)  10.4 us
    all_to_all x1, waiting for transfers between devices, on_device(): back = lax.all_to_all(chosen, 'dom', 0, 0, tiled=True)  9.96 us
    scatter x1, local copies, waits for them, and re-layouts, on_device(): jnp.full((rows * columns,), jnp.nan, jnp.float32).at[position]  8.3 us
    ppermute x1, waiting for transfers between devices, on_device(): from_above = lax.ppermute(to_below, 'band', ring_down)  5.94 us
    ppermute x1, starting transfers between devices, on_device(): from_below = lax.ppermute(to_above, 'band', ring_up)  5.26 us
    pallas_call x1, Pallas kernels, on_device(): pl.pallas_call(functools.partial(forecast_kernel, total_rows=rows * bands...  4.42 us
    all_to_all x1, starting transfers between devices, on_device(): back = lax.all_to_all(chosen, 'dom', 0, 0, tiled=True)  3.83 us
  transfers between devices with their start and end apart: 5, of which 3 were waited for; matrix products, arithmetic and copies ran while one was open for 9% of the time, Pallas kernels for 0%

profile of v10, /device:TPU:32, one launch (start us, length us, event | category | flops | bytes accessed | tf_op | source)
XLA Modules:
  0.0 95.8 jit_solution(12406151547004008580)
XLA Ops:
  0.0 1.3 %copy.27 = f32[6,8,32,128]{3,2,1,0:T(8,128)S(1)} copy(f32[6,8,32,128]{3,1,2,0:T(8,128)} %bitcast.47) | data formatting | bytes 1572864
  1.3 0.5 copy.34
  2.4 0.1 concatenate.12
  2.5 35.6 %all_to_all.10 = f32[32,56,128]{2,1,0:T(8,128)S(1)} all-to-all(f32[32,56,128]{2,1,0:T(8,128)S(1)} %concatenate.12), channel_id=1, replica_groups=mesh['dom'=32,'band'=8] {'dom'}, dimensions={0} | all-to-all | bytes 1835008 | tf_op jit(solution)/shard_map/all_to_all | solution.py:104
  38.1 0.7 fusion.49
  38.7 0.1 slice.233
  38.8 1.5 %gather_fusion = f32[32,48,128]{2,1,0:T(8,128)} fusion(f32[32,48,128]{2,1,0:T(8,128)S(1)} %slice.233, s32[1024]{0:T(1024)S(1)} %pad_clamp_fusion), kind=kCustom, calls=%fused_computation | custom fusion | bytes 1572992 | tf_op jit(solution)/shard_map/jit(_take)/gather | solution.py:106
  40.3 3.8 %all-to-all-start.1 = ((f32[32,48,128]{2,1,0:T(8,128)}), f32[32,48,128]{2,1,0:T(8,128)S(1)}, u32[]{:S(2)}, u32[]{:S(2)}) async-start(f32[32,48,128]{2,1,0:T(8,128)} %gather_fusion), calls=%async_computation.1 | async-start | bytes 1572864 | tf_op jit(solution)/shard_map/all_to_all | solution.py:107
  44.1 0.0 copy-start.2
  44.2 0.0 copy-start.1
  44.2 3.5 %collective-permute-start.2 = (f32[8,4096]{1,0:T(8,128)S(1)}, f32[8,4096]{1,0:T(8,128)S(1)}, u32[]{:S(2)}, u32[]{:S(2)}) collective-permute-start(f32[8,4096]{1,0:T(8,128)S(1)} %get-tuple-element.16), channel_id=1, source_target_pairs={{0,1},{1,2},{2,3},{3,4},{4,5},{5,6},{6,7},{8,9},{9,10},{10,11},{11... | collective-permute-start | bytes 393224 | tf_op jit(solution)/shard_map/ppermute | solution.py:117
  47.7 1.3 %collective-permute-start.3 = (f32[8,4096]{1,0:T(8,128)S(1)}, f32[8,4096]{1,0:T(8,128)S(1)}, u32[]{:S(2)}, u32[]{:S(2)}) collective-permute-start(f32[8,4096]{1,0:T(8,128)S(1)} %get-tuple-element.17), channel_id=1, source_target_pairs={{1,0},{2,1},{3,2},{4,3},{5,4},{6,5},{7,6},{9,8},{10,9},{11,10},{12... | collective-permute-start | bytes 393224 | tf_op jit(solution)/shard_map/ppermute | solution.py:119
  49.0 8.3 %scatter_custom_fusion = f32[65536]{0:T(1024)S(1)} fusion(s32[2048]{0:T(1024)S(1)} %compare_select_fusion, f32[2048]{0:T(1024)} %param.11, f32[]{:T(128)} %constant.16.clone.1), kind=kCustom, calls=%fused_computation.92 | custom fusion | bytes 262656 | tf_op jit(solution)/shard_map/scatter | solution.py:112
  57.3 0.1 reshape.32
  57.4 0.0 collective-permute-done.2
  57.4 10.0 %all-to-all-done.1 = f32[32,48,128]{2,1,0:T(8,128)S(1)} async-done(((f32[32,48,128]{2,1,0:T(8,128)}), f32[32,48,128]{2,1,0:T(8,128)S(1)}, u32[]{:S(2)}, u32[]{:S(2)}) %all-to-all-start.1) | async-done | bytes 786464 | tf_op jit(solution)/shard_map/all_to_all | solution.py:107
  67.4 0.1 slice_bitcast_fusion
  67.6 1.1 %multiply_add_fusion = f32[16,4096]{1,0:T(8,128)S(1)} fusion(f32[16,4096]{1,0:T(8,128)S(1)} %subtract_select_fusion), kind=kLoop, calls=%fused_computation.60 | loop fusion | flops 2097152 | bytes 524288 | tf_op jit(solution)/shard_map/add | solution.py:32
  68.8 0.8 fusion.16.pf_ref
  69.7 5.3 %collective-permute-start.1 = (f32[32,4096]{1,0:T(8,128)S(1)}, f32[32,4096]{1,0:T(8,128)S(1)}, u32[]{:S(2)}, u32[]{:S(2)}) collective-permute-start(f32[32,4096]{1,0:T(8,128)S(1)} %pad_maximum_fusion.1), channel_id=1, source_target_pairs={{1,0},{2,1},{3,2},{4,3},{5,4},{6,5},{7,6},{0,7},{9,8},{10,9},{11,1... | collective-permute-start | bytes 1572872 | tf_op jit(solution)/shard_map/ppermute | solution.py:150
  75.0 0.1 collective-permute-start
  75.1 10.4 %collective-permute-done.1.fb_ref = f32[32,4096]{1,0:T(8,128)S(1)} collective-permute-done((f32[32,4096]{1,0:T(8,128)S(1)}, f32[32,4096]{1,0:T(8,128)S(1)}, u32[]{:S(2)}, u32[]{:S(2)}) %collective-permute-start.1) | collective-permute-done | bytes 524320 | tf_op jit(solution)/shard_map/ppermute | solution.py:150
  85.5 5.9 %collective-permute-done.fa_ref = f32[32,4096]{1,0:T(8,128)S(1)} collective-permute-done((f32[32,4096]{1,0:T(8,128)S(1)}, f32[32,4096]{1,0:T(8,128)S(1)}, u32[]{:S(2)}, u32[]{:S(2)}) %collective-permute-start) | collective-permute-done | bytes 524320 | tf_op jit(solution)/shard_map/ppermute | solution.py:149
  91.4 4.4 %shard_map.64 = f32[3,16,4096]{2,1,0:T(8,128)} custom-call(f32[32,4096]{1,0:T(8,128)S(1)} %collective-permute-done.fa_ref, f32[32,4096]{1,0:T(8,128)S(1)} %collective-permute-done.1.fb_ref, f32[16,4096]{1,0:T(8,128)S(1)} %bitcast.41, f32[16,4096]{1,0:T(8,128)S(1)} %get-tuple-element.19.u_ref, f32[16,4096]{1,0:T(8,128)S(1)} %get-tuple-element.18.v_ref, ...), custom_call_target="tpu_custom_call" | custom-call | tf_op jit(solution)/shard_map/pallas_call | solution.py:153
  (17 shorter events, 0.4 us)
Async XLA Ops:
  40.3 3.8 %copy-start = (f32[16,4096]{1,0:T(8,128)S(1)}, f32[16,4096]{1,0:T(8,128)}, u32[]{:S(2)}) copy-start(f32[16,4096]{1,0:T(8,128)} %param.8) | copy-start | bytes 786436
  40.3 27.1 %all-to-all-start.1 = ((f32[32,48,128]{2,1,0:T(8,128)}), f32[32,48,128]{2,1,0:T(8,128)S(1)}, u32[]{:S(2)}, u32[]{:S(2)}) async-start(f32[32,48,128]{2,1,0:T(8,128)} %gather_fusion), calls=%async_computation.1 | async-start | bytes 1572864 | tf_op jit(solution)/shard_map/all_to_all | solution.py:107
  44.1 4.9 %copy-start.2 = (s32[2048]{0:T(1024)S(1)}, s32[2048]{0:T(1024)}, u32[]{:S(2)}) copy-start(s32[2048]{0:T(1024)} %param.9) | copy-start | bytes 24580
  44.2 4.8 %copy-start.1 = (s32[2048]{0:T(1024)S(1)}, s32[2048]{0:T(1024)}, u32[]{:S(2)}) copy-start(s32[2048]{0:T(1024)} %param.10) | copy-start | bytes 24580
  44.2 13.2 %collective-permute-start.2 = (f32[8,4096]{1,0:T(8,128)S(1)}, f32[8,4096]{1,0:T(8,128)S(1)}, u32[]{:S(2)}, u32[]{:S(2)}) collective-permute-start(f32[8,4096]{1,0:T(8,128)S(1)} %get-tuple-element.16), channel_id=1, source_target_pairs={{0,1},{1,2},{2,3},{3,4},{4,5},{5,6},{6,7},{8,9},{9,10},{10,11},{11... | collective-permute-start | bytes 393224 | tf_op jit(solution)/shard_map/ppermute | solution.py:117
  47.7 9.7 %collective-permute-start.3 = (f32[8,4096]{1,0:T(8,128)S(1)}, f32[8,4096]{1,0:T(8,128)S(1)}, u32[]{:S(2)}, u32[]{:S(2)}) collective-permute-start(f32[8,4096]{1,0:T(8,128)S(1)} %get-tuple-element.17), channel_id=1, source_target_pairs={{1,0},{2,1},{3,2},{4,3},{5,4},{6,5},{7,6},{9,8},{10,9},{11,10},{12... | collective-permute-start | bytes 393224 | tf_op jit(solution)/shard_map/ppermute | solution.py:119
  69.7 15.8 %collective-permute-start.1 = (f32[32,4096]{1,0:T(8,128)S(1)}, f32[32,4096]{1,0:T(8,128)S(1)}, u32[]{:S(2)}, u32[]{:S(2)}) collective-permute-start(f32[32,4096]{1,0:T(8,128)S(1)} %pad_maximum_fusion.1), channel_id=1, source_target_pairs={{1,0},{2,1},{3,2},{4,3},{5,4},{6,5},{7,6},{0,7},{9,8},{10,9},{11,1... | collective-permute-start | bytes 1572872 | tf_op jit(solution)/shard_map/ppermute | solution.py:150
  75.0 16.4 %collective-permute-start = (f32[32,4096]{1,0:T(8,128)S(1)}, f32[32,4096]{1,0:T(8,128)S(1)}, u32[]{:S(2)}, u32[]{:S(2)}) collective-permute-start(f32[32,4096]{1,0:T(8,128)S(1)} %pad_maximum_fusion), channel_id=1, source_target_pairs={{0,1},{1,2},{2,3},{3,4},{4,5},{5,6},{6,7},{7,0},{8,9},{9,10},{10,1... | collective-permute-start | bytes 1572872 | tf_op jit(solution)/shard_map/ppermute | solution.py:149

commit v11 on v10

--- a/solution.py
+++ b/solution.py
@@ -90,6 +90,17 @@
     o_ref[2] = north_vel[margin:margin + rows]
 
 
+def take_kernel(lineage_ref, src_ref, out_ref, sems):
+    count, rows = out_ref.shape[0], out_ref.shape[1]
+    copies = []
+    for c in range(count):
+        copy = pltpu.make_async_copy(src_ref.at[lineage_ref[c], pl.ds(0, rows)], out_ref.at[c], sems.at[c])
+        copy.start()
+        copies.append(copy)
+    for copy in copies:
+        copy.wait()
+
+
 def on_device(ensemble, ancestors, sea_depth, obs_rows, obs_cols, obs_values):
     _, fields, rows, columns = ensemble.shape
     parts = lax.axis_size("dom")
@@ -102,8 +113,19 @@
     block = ensemble.reshape(fields * rows, parts, columns // parts).transpose(1, 0, 2)
     tag = jnp.broadcast_to(ancestors.astype(jnp.float32)[:, None, None], (parts, 8, columns // parts))
     crossed = lax.all_to_all(jnp.concatenate([block, tag], axis=1), "dom", 0, 0, tiled=True)
-    lineage = crossed[:, fields * rows, 0].astype(jnp.int32)
-    chosen = jnp.take(crossed[:, :fields * rows], lineage, axis=0, mode="clip")
+    lineage = jnp.clip(crossed[:, fields * rows, 0].astype(jnp.int32), 0, parts - 1)
+    chosen = pl.pallas_call(
+        take_kernel,
+        interpret=INTERPRET,
+        out_shape=jax.ShapeDtypeStruct((parts, fields * rows, columns // parts), jnp.float32),
+        grid_spec=pltpu.PrefetchScalarGridSpec(
+            num_scalar_prefetch=1,
+            grid=(1,),
+            in_specs=[pl.BlockSpec(memory_space=pl.ANY)],
+            out_specs=pl.BlockSpec(memory_space=pl.ANY),
+            scratch_shapes=[pltpu.SemaphoreType.DMA((parts,))],
+        ),
+    )(lineage, pltpu.with_memory_space_constraint(crossed, pltpu.VMEM))
     back = lax.all_to_all(chosen, "dom", 0, 0, tiled=True)
     state = back.transpose(1, 0, 2).reshape(fields, rows, columns)
 

time: 96.2 us -> 97.1 us (level)
  Pallas kernels: 4.42 us -> 6.23 us
  local copies, waits for them, and re-layouts: 11.9 us -> 10.4 us
    pallas_call x0 -> x1, Pallas kernels: none -> 1.8 us  [on_device(): pl.pallas_call(take_kernel, interpret=INTERPRET, out_shape=jax.ShapeDtype...]
    gather x1 -> x0, local copies, waits for them, and re-layouts: 1.48 us -> none  [on_device(): chosen = jnp.take(crossed[:, :fields * rows], lineage, axis=0, mode='clip')]
    min x0 -> x1, other arithmetic: none -> 1.23 us  [on_device(): jnp.clip(crossed[:, fields * rows, 0].astype(jnp.int32), 0, parts - 1)]
where the time goes in v11:
time: 97.1 us; the launch traced here: 96.7 us
  blocking collectives  35.6 us (37%)
  waiting for transfers between devices  26.3 us (27%)
  starting transfers between devices  14 us (14%)
  local copies, waits for them, and re-layouts  10.4 us (11%)
  Pallas kernels  6.23 us (6%)
  other arithmetic  3.39 us (3%)
    all_to_all x1, blocking collectives, on_device(): lax.all_to_all(jnp.concatenate([block, tag], axis=1), 'dom', 0, 0, tiled=...  35.6 us
    ppermute x1, waiting for transfers between devices, on_device(): from_below = lax.ppermute(to_above, 'band', ring_up)  10.4 us
    all_to_all x1, waiting for transfers between devices, on_device(): back = lax.all_to_all(chosen, 'dom', 0, 0, tiled=True)  9.96 us
    scatter x1, local copies, waits for them, and re-layouts, on_device(): jnp.full((rows * columns,), jnp.nan, jnp.float32).at[position]  8.3 us
    ppermute x1, waiting for transfers between devices, on_device(): from_above = lax.ppermute(to_below, 'band', ring_down)  5.93 us
    ppermute x1, starting transfers between devices, on_device(): from_below = lax.ppermute(to_above, 'band', ring_up)  5.26 us
    pallas_call x1, Pallas kernels, on_device(): pl.pallas_call(functools.partial(forecast_kernel, total_rows=rows * bands...  4.42 us
    all_to_all x1, starting transfers between devices, on_device(): back = lax.all_to_all(chosen, 'dom', 0, 0, tiled=True)  3.84 us
  transfers between devices with their start and end apart: 5, of which 3 were waited for; matrix products, arithmetic and copies ran while one was open for 9% of the time, Pallas kernels for 0%

profile of v11, /device:TPU:32, one launch (start us, length us, event | category | flops | bytes accessed | tf_op | source)
XLA Modules:
  0.0 96.7 jit_solution(2981785367382085425)
XLA Ops:
  0.0 1.3 %copy.17 = f32[6,8,32,128]{3,2,1,0:T(8,128)S(1)} copy(f32[6,8,32,128]{3,1,2,0:T(8,128)} %bitcast.47) | data formatting | bytes 1572864
  1.3 0.5 copy.24
  2.4 0.1 concatenate.12
  2.5 35.6 %all_to_all.10.src_ref = f32[32,56,128]{2,1,0:T(8,128)S(1)} all-to-all(f32[32,56,128]{2,1,0:T(8,128)S(1)} %concatenate.12), channel_id=1, replica_groups=mesh['dom'=32,'band'=8] {'dom'}, dimensions={0} | all-to-all | bytes 1835008 | tf_op jit(solution)/shard_map/all_to_all | solution.py:115
  38.1 1.2 %fusion.50.lineage_ref = s32[32]{0:T(128)} fusion(f32[32,56,128]{2,1,0:T(8,128)S(1)} %all_to_all.10.src_ref), kind=kLoop, calls=%fused_computation.96 | loop fusion | flops 64 | bytes 256 | tf_op jit(solution)/shard_map/jit(clip)/min | solution.py:116
  39.3 1.8 %shard_map.64 = f32[32,48,128]{2,1,0:T(8,128)} custom-call(s32[32]{0:T(128)} %fusion.50.lineage_ref, f32[32,56,128]{2,1,0:T(8,128)S(1)} %all_to_all.10.src_ref), custom_call_target="tpu_custom_call" | custom-call | tf_op jit(solution)/shard_map/pallas_call | solution.py:117
  41.1 0.0 copy-start
  41.1 3.8 %all-to-all-start.1 = ((f32[32,48,128]{2,1,0:T(8,128)}), f32[32,48,128]{2,1,0:T(8,128)S(1)}, u32[]{:S(2)}, u32[]{:S(2)}) async-start(f32[32,48,128]{2,1,0:T(8,128)} %shard_map.64), calls=%async_computation.1 | async-start | bytes 1572864 | tf_op jit(solution)/shard_map/all_to_all | solution.py:129
  45.0 0.0 copy-start.2
  45.0 0.0 copy-start.1
  45.0 3.5 %collective-permute-start.2 = (f32[8,4096]{1,0:T(8,128)S(1)}, f32[8,4096]{1,0:T(8,128)S(1)}, u32[]{:S(2)}, u32[]{:S(2)}) collective-permute-start(f32[8,4096]{1,0:T(8,128)S(1)} %get-tuple-element.16), channel_id=1, source_target_pairs={{0,1},{1,2},{2,3},{3,4},{4,5},{5,6},{6,7},{8,9},{9,10},{10,11},{11... | collective-permute-start | bytes 393224 | tf_op jit(solution)/shard_map/ppermute | solution.py:139
  48.5 1.3 %collective-permute-start.3 = (f32[8,4096]{1,0:T(8,128)S(1)}, f32[8,4096]{1,0:T(8,128)S(1)}, u32[]{:S(2)}, u32[]{:S(2)}) collective-permute-start(f32[8,4096]{1,0:T(8,128)S(1)} %get-tuple-element.17), channel_id=1, source_target_pairs={{1,0},{2,1},{3,2},{4,3},{5,4},{6,5},{7,6},{9,8},{10,9},{11,10},{12... | collective-permute-start | bytes 393224 | tf_op jit(solution)/shard_map/ppermute | solution.py:141
  49.9 8.3 %scatter_custom_fusion = f32[65536]{0:T(1024)S(1)} fusion(s32[2048]{0:T(1024)S(1)} %compare_select_fusion, f32[2048]{0:T(1024)} %param.11, f32[]{:T(128)} %constant.19.clone.1), kind=kCustom, calls=%fused_computation.91 | custom fusion | bytes 262656 | tf_op jit(solution)/shard_map/scatter | solution.py:134
  58.2 0.1 reshape.25
  58.2 0.0 collective-permute-done.2
  58.3 10.0 %all-to-all-done.1 = f32[32,48,128]{2,1,0:T(8,128)S(1)} async-done(((f32[32,48,128]{2,1,0:T(8,128)}), f32[32,48,128]{2,1,0:T(8,128)S(1)}, u32[]{:S(2)}, u32[]{:S(2)}) %all-to-all-start.1) | async-done | bytes 786464 | tf_op jit(solution)/shard_map/all_to_all | solution.py:129
  68.3 0.1 slice_bitcast_fusion
  68.4 1.1 %multiply_add_fusion = f32[16,4096]{1,0:T(8,128)S(1)} fusion(f32[16,4096]{1,0:T(8,128)S(1)} %subtract_select_fusion), kind=kLoop, calls=%fused_computation.59 | loop fusion | flops 2097152 | bytes 524288 | tf_op jit(solution)/shard_map/add | solution.py:32
  69.6 0.8 fusion.16.pf_ref
  70.5 5.3 %collective-permute-start.1 = (f32[32,4096]{1,0:T(8,128)S(1)}, f32[32,4096]{1,0:T(8,128)S(1)}, u32[]{:S(2)}, u32[]{:S(2)}) collective-permute-start(f32[32,4096]{1,0:T(8,128)S(1)} %pad_maximum_fusion.1), channel_id=1, source_target_pairs={{1,0},{2,1},{3,2},{4,3},{5,4},{6,5},{7,6},{0,7},{9,8},{10,9},{11,1... | collective-permute-start | bytes 1572872 | tf_op jit(solution)/shard_map/ppermute | solution.py:172
  75.8 0.1 collective-permute-start
  76.0 10.4 %collective-permute-done.1.fb_ref = f32[32,4096]{1,0:T(8,128)S(1)} collective-permute-done((f32[32,4096]{1,0:T(8,128)S(1)}, f32[32,4096]{1,0:T(8,128)S(1)}, u32[]{:S(2)}, u32[]{:S(2)}) %collective-permute-start.1) | collective-permute-done | bytes 524320 | tf_op jit(solution)/shard_map/ppermute | solution.py:172
  86.3 5.9 %collective-permute-done.fa_ref = f32[32,4096]{1,0:T(8,128)S(1)} collective-permute-done((f32[32,4096]{1,0:T(8,128)S(1)}, f32[32,4096]{1,0:T(8,128)S(1)}, u32[]{:S(2)}, u32[]{:S(2)}) %collective-permute-start) | collective-permute-done | bytes 524320 | tf_op jit(solution)/shard_map/ppermute | solution.py:171
  92.3 4.4 %shard_map.65 = f32[3,16,4096]{2,1,0:T(8,128)} custom-call(f32[32,4096]{1,0:T(8,128)S(1)} %collective-permute-done.fa_ref, f32[32,4096]{1,0:T(8,128)S(1)} %collective-permute-done.1.fb_ref, f32[16,4096]{1,0:T(8,128)S(1)} %bitcast.41, f32[16,4096]{1,0:T(8,128)S(1)} %get-tuple-element.19.u_ref, f32[16,4096]{1,0:T(8,128)S(1)} %get-tuple-element.18.v_ref, ...), custom_call_target="tpu_custom_call" | custom-call | tf_op jit(solution)/shard_map/pallas_call | solution.py:175
  (15 shorter events, 0.4 us)
Async XLA Ops:
  41.1 3.9 %copy-start = (f32[16,4096]{1,0:T(8,128)S(1)}, f32[16,4096]{1,0:T(8,128)}, u32[]{:S(2)}) copy-start(f32[16,4096]{1,0:T(8,128)} %param.8) | copy-start | bytes 786436
  41.1 27.1 %all-to-all-start.1 = ((f32[32,48,128]{2,1,0:T(8,128)}), f32[32,48,128]{2,1,0:T(8,128)S(1)}, u32[]{:S(2)}, u32[]{:S(2)}) async-start(f32[32,48,128]{2,1,0:T(8,128)} %shard_map.64), calls=%async_computation.1 | async-start | bytes 1572864 | tf_op jit(solution)/shard_map/all_to_all | solution.py:129
  45.0 4.9 %copy-start.2 = (s32[2048]{0:T(1024)S(1)}, s32[2048]{0:T(1024)}, u32[]{:S(2)}) copy-start(s32[2048]{0:T(1024)} %param.9) | copy-start | bytes 24580
  45.0 4.8 %copy-start.1 = (s32[2048]{0:T(1024)S(1)}, s32[2048]{0:T(1024)}, u32[]{:S(2)}) copy-start(s32[2048]{0:T(1024)} %param.10) | copy-start | bytes 24580
  45.0 13.2 %collective-permute-start.2 = (f32[8,4096]{1,0:T(8,128)S(1)}, f32[8,4096]{1,0:T(8,128)S(1)}, u32[]{:S(2)}, u32[]{:S(2)}) collective-permute-start(f32[8,4096]{1,0:T(8,128)S(1)} %get-tuple-element.16), channel_id=1, source_target_pairs={{0,1},{1,2},{2,3},{3,4},{4,5},{5,6},{6,7},{8,9},{9,10},{10,11},{11... | collective-permute-start | bytes 393224 | tf_op jit(solution)/shard_map/ppermute | solution.py:139
  48.5 9.7 %collective-permute-start.3 = (f32[8,4096]{1,0:T(8,128)S(1)}, f32[8,4096]{1,0:T(8,128)S(1)}, u32[]{:S(2)}, u32[]{:S(2)}) collective-permute-start(f32[8,4096]{1,0:T(8,128)S(1)} %get-tuple-element.17), channel_id=1, source_target_pairs={{1,0},{2,1},{3,2},{4,3},{5,4},{6,5},{7,6},{9,8},{10,9},{11,10},{12... | collective-permute-start | bytes 393224 | tf_op jit(solution)/shard_map/ppermute | solution.py:141
  70.5 15.8 %collective-permute-start.1 = (f32[32,4096]{1,0:T(8,128)S(1)}, f32[32,4096]{1,0:T(8,128)S(1)}, u32[]{:S(2)}, u32[]{:S(2)}) collective-permute-start(f32[32,4096]{1,0:T(8,128)S(1)} %pad_maximum_fusion.1), channel_id=1, source_target_pairs={{1,0},{2,1},{3,2},{4,3},{5,4},{6,5},{7,6},{0,7},{9,8},{10,9},{11,1... | collective-permute-start | bytes 1572872 | tf_op jit(solution)/shard_map/ppermute | solution.py:172
  75.8 16.4 %collective-permute-start = (f32[32,4096]{1,0:T(8,128)S(1)}, f32[32,4096]{1,0:T(8,128)S(1)}, u32[]{:S(2)}, u32[]{:S(2)}) collective-permute-start(f32[32,4096]{1,0:T(8,128)S(1)} %pad_maximum_fusion), channel_id=1, source_target_pairs={{0,1},{1,2},{2,3},{3,4},{4,5},{5,6},{6,7},{7,0},{8,9},{9,10},{10,1... | collective-permute-start | bytes 1572872 | tf_op jit(solution)/shard_map/ppermute | solution.py:171

commit v12 on v10

--- a/solution.py
+++ b/solution.py
@@ -144,9 +144,8 @@
         ],
         axis=0,
     )
-    ring_down = [(i, (i + 1) % bands) for i in range(bands)]
     ring_up = [((i + 1) % bands, i) for i in range(bands)]
-    from_above = lax.ppermute(to_below, "band", ring_down)
+    from_above = lax.ppermute(to_below, "band", down)
     from_below = lax.ppermute(to_above, "band", ring_up)
 
     ext_rows = rows + 2 * margin

time: 96.2 us -> 95.8 us (level)
  the two profiles are of different devices: /device:TPU:32 before, /device:TPU:36 now
where the time goes in v12:
time: 95.8 us; the launch traced here: 95.4 us
  blocking collectives  35.3 us (37%)
  waiting for transfers between devices  21.6 us (23%)
  starting transfers between devices  18.5 us (19%)
  local copies, waits for them, and re-layouts  11.9 us (12%)
  Pallas kernels  4.42 us (5%)
  other arithmetic  2.82 us (3%)
    all_to_all x1, blocking collectives, on_device(): lax.all_to_all(jnp.concatenate([block, tag], axis=1), 'dom', 0, 0, tiled=...  35.3 us
    ppermute x1, waiting for transfers between devices, on_device(): from_below = lax.ppermute(to_above, 'band', ring_up)  8.53 us
    scatter x1, local copies, waits for them, and re-layouts, on_device(): jnp.full((rows * columns,), jnp.nan, jnp.float32).at[position]  8.3 us
    ppermute x1, waiting for transfers between devices, on_device(): from_above = lax.ppermute(to_below, 'band', down)  7.75 us
    ppermute x1, starting transfers between devices, on_device(): lax.ppermute(sea_depth[:margin], 'band', up)  5.97 us
    all_to_all x1, waiting for transfers between devices, on_device(): back = lax.all_to_all(chosen, 'dom', 0, 0, tiled=True)  5.28 us
    pallas_call x1, Pallas kernels, on_device(): pl.pallas_call(functools.partial(forecast_kernel, total_rows=rows * bands...  4.42 us
    all_to_all x1, starting transfers between devices, on_device(): back = lax.all_to_all(chosen, 'dom', 0, 0, tiled=True)  3.83 us
  transfers between devices with their start and end apart: 5, of which 3 were waited for; matrix products, arithmetic and copies ran while one was open for 9% of the time, Pallas kernels for 0%

profile of v12, /device:TPU:36, one launch (start us, length us, event | category | flops | bytes accessed | tf_op | source)
XLA Modules:
  0.0 95.4 jit_solution(17017369415460971017)
XLA Ops:
  0.0 1.3 %copy.27 = f32[6,8,32,128]{3,2,1,0:T(8,128)S(1)} copy(f32[6,8,32,128]{3,1,2,0:T(8,128)} %bitcast.47) | data formatting | bytes 1572864
  1.3 0.5 copy.34
  2.4 0.1 concatenate.12
  2.5 35.3 %all_to_all.10 = f32[32,56,128]{2,1,0:T(8,128)S(1)} all-to-all(f32[32,56,128]{2,1,0:T(8,128)S(1)} %concatenate.12), channel_id=1, replica_groups=mesh['dom'=32,'band'=8] {'dom'}, dimensions={0} | all-to-all | bytes 1835008 | tf_op jit(solution)/shard_map/all_to_all | solution.py:104
  37.8 0.7 fusion.49
  38.4 0.1 slice.233
  38.5 1.5 %gather_fusion = f32[32,48,128]{2,1,0:T(8,128)} fusion(f32[32,48,128]{2,1,0:T(8,128)S(1)} %slice.233, s32[1024]{0:T(1024)S(1)} %pad_clamp_fusion), kind=kCustom, calls=%fused_computation | custom fusion | bytes 1572992 | tf_op jit(solution)/shard_map/jit(_take)/gather | solution.py:106
  40.0 3.8 %all-to-all-start.1 = ((f32[32,48,128]{2,1,0:T(8,128)}), f32[32,48,128]{2,1,0:T(8,128)S(1)}, u32[]{:S(2)}, u32[]{:S(2)}) async-start(f32[32,48,128]{2,1,0:T(8,128)} %gather_fusion), calls=%async_computation.1 | async-start | bytes 1572864 | tf_op jit(solution)/shard_map/all_to_all | solution.py:107
  43.8 0.0 copy-start.2
  43.9 0.0 copy-start.1
  43.9 3.5 %collective-permute-start.2 = (f32[8,4096]{1,0:T(8,128)S(1)}, f32[8,4096]{1,0:T(8,128)S(1)}, u32[]{:S(2)}, u32[]{:S(2)}) collective-permute-start(f32[8,4096]{1,0:T(8,128)S(1)} %get-tuple-element.16), channel_id=1, source_target_pairs={{0,1},{1,2},{2,3},{3,4},{4,5},{5,6},{6,7},{8,9},{9,10},{10,11},{11... | collective-permute-start | bytes 393224 | tf_op jit(solution)/shard_map/ppermute | solution.py:117
  47.4 6.0 %collective-permute-start.3 = (f32[8,4096]{1,0:T(8,128)S(1)}, f32[8,4096]{1,0:T(8,128)S(1)}, u32[]{:S(2)}, u32[]{:S(2)}) collective-permute-start(f32[8,4096]{1,0:T(8,128)S(1)} %get-tuple-element.17), channel_id=1, source_target_pairs={{1,0},{2,1},{3,2},{4,3},{5,4},{6,5},{7,6},{9,8},{10,9},{11,10},{12... | collective-permute-start | bytes 393224 | tf_op jit(solution)/shard_map/ppermute | solution.py:119
  53.4 8.3 %scatter_custom_fusion = f32[65536]{0:T(1024)S(1)} fusion(s32[2048]{0:T(1024)S(1)} %compare_select_fusion, f32[2048]{0:T(1024)} %param.11, f32[]{:T(128)} %constant.16.clone.1), kind=kCustom, calls=%fused_computation.92 | custom fusion | bytes 262656 | tf_op jit(solution)/shard_map/scatter | solution.py:112
  61.7 0.1 reshape.32
  61.8 0.0 collective-permute-done.2
  61.8 5.3 %all-to-all-done.1 = f32[32,48,128]{2,1,0:T(8,128)S(1)} async-done(((f32[32,48,128]{2,1,0:T(8,128)}), f32[32,48,128]{2,1,0:T(8,128)S(1)}, u32[]{:S(2)}, u32[]{:S(2)}) %all-to-all-start.1) | async-done | bytes 786464 | tf_op jit(solution)/shard_map/all_to_all | solution.py:107
  67.1 0.1 slice_bitcast_fusion
  67.3 1.1 %multiply_add_fusion = f32[16,4096]{1,0:T(8,128)S(1)} fusion(f32[16,4096]{1,0:T(8,128)S(1)} %subtract_select_fusion), kind=kLoop, calls=%fused_computation.60 | loop fusion | flops 2097152 | bytes 524288 | tf_op jit(solution)/shard_map/add | solution.py:32
  68.5 0.8 fusion.16.pf_ref
  69.4 3.3 %collective-permute-start.1 = (f32[32,4096]{1,0:T(8,128)S(1)}, f32[32,4096]{1,0:T(8,128)S(1)}, u32[]{:S(2)}, u32[]{:S(2)}) collective-permute-start(f32[32,4096]{1,0:T(8,128)S(1)} %pad_maximum_fusion.1), channel_id=1, source_target_pairs={{1,0},{2,1},{3,2},{4,3},{5,4},{6,5},{7,6},{0,7},{9,8},{10,9},{11,1... | collective-permute-start | bytes 1572872 | tf_op jit(solution)/shard_map/ppermute | solution.py:149
  72.8 1.9 %collective-permute-start = (f32[32,4096]{1,0:T(8,128)S(1)}, f32[32,4096]{1,0:T(8,128)S(1)}, u32[]{:S(2)}, u32[]{:S(2)}) collective-permute-start(f32[32,4096]{1,0:T(8,128)S(1)} %pad_maximum_fusion), channel_id=1, source_target_pairs={{0,1},{1,2},{2,3},{3,4},{4,5},{5,6},{6,7},{8,9},{9,10},{10,11},{11... | collective-permute-start | bytes 1572872 | tf_op jit(solution)/shard_map/ppermute | solution.py:148
  74.7 8.5 %collective-permute-done.1.fb_ref = f32[32,4096]{1,0:T(8,128)S(1)} collective-permute-done((f32[32,4096]{1,0:T(8,128)S(1)}, f32[32,4096]{1,0:T(8,128)S(1)}, u32[]{:S(2)}, u32[]{:S(2)}) %collective-permute-start.1) | collective-permute-done | bytes 524320 | tf_op jit(solution)/shard_map/ppermute | solution.py:149
  83.3 7.8 %collective-permute-done.fa_ref = f32[32,4096]{1,0:T(8,128)S(1)} collective-permute-done((f32[32,4096]{1,0:T(8,128)S(1)}, f32[32,4096]{1,0:T(8,128)S(1)}, u32[]{:S(2)}, u32[]{:S(2)}) %collective-permute-start) | collective-permute-done | bytes 524320 | tf_op jit(solution)/shard_map/ppermute | solution.py:148
  91.0 4.4 %shard_map.64 = f32[3,16,4096]{2,1,0:T(8,128)} custom-call(f32[32,4096]{1,0:T(8,128)S(1)} %collective-permute-done.fa_ref, f32[32,4096]{1,0:T(8,128)S(1)} %collective-permute-done.1.fb_ref, f32[16,4096]{1,0:T(8,128)S(1)} %bitcast.41, f32[16,4096]{1,0:T(8,128)S(1)} %get-tuple-element.19.u_ref, f32[16,4096]{1,0:T(8,128)S(1)} %get-tuple-element.18.v_ref, ...), custom_call_target="tpu_custom_call" | custom-call | tf_op jit(solution)/shard_map/pallas_call | solution.py:152
  (17 shorter events, 0.4 us)
Async XLA Ops:
  40.0 3.8 %copy-start = (f32[16,4096]{1,0:T(8,128)S(1)}, f32[16,4096]{1,0:T(8,128)}, u32[]{:S(2)}) copy-start(f32[16,4096]{1,0:T(8,128)} %param.8) | copy-start | bytes 786436
  40.0 27.1 %all-to-all-start.1 = ((f32[32,48,128]{2,1,0:T(8,128)}), f32[32,48,128]{2,1,0:T(8,128)S(1)}, u32[]{:S(2)}, u32[]{:S(2)}) async-start(f32[32,48,128]{2,1,0:T(8,128)} %gather_fusion), calls=%async_computation.1 | async-start | bytes 1572864 | tf_op jit(solution)/shard_map/all_to_all | solution.py:107
  43.8 9.5 %copy-start.2 = (s32[2048]{0:T(1024)S(1)}, s32[2048]{0:T(1024)}, u32[]{:S(2)}) copy-start(s32[2048]{0:T(1024)} %param.9) | copy-start | bytes 24580
  43.9 9.5 %copy-start.1 = (s32[2048]{0:T(1024)S(1)}, s32[2048]{0:T(1024)}, u32[]{:S(2)}) copy-start(s32[2048]{0:T(1024)} %param.10) | copy-start | bytes 24580
  43.9 17.9 %collective-permute-start.2 = (f32[8,4096]{1,0:T(8,128)S(1)}, f32[8,4096]{1,0:T(8,128)S(1)}, u32[]{:S(2)}, u32[]{:S(2)}) collective-permute-start(f32[8,4096]{1,0:T(8,128)S(1)} %get-tuple-element.16), channel_id=1, source_target_pairs={{0,1},{1,2},{2,3},{3,4},{4,5},{5,6},{6,7},{8,9},{9,10},{10,11},{11... | collective-permute-start | bytes 393224 | tf_op jit(solution)/shard_map/ppermute | solution.py:117
  47.4 14.4 %collective-permute-start.3 = (f32[8,4096]{1,0:T(8,128)S(1)}, f32[8,4096]{1,0:T(8,128)S(1)}, u32[]{:S(2)}, u32[]{:S(2)}) collective-permute-start(f32[8,4096]{1,0:T(8,128)S(1)} %get-tuple-element.17), channel_id=1, source_target_pairs={{1,0},{2,1},{3,2},{4,3},{5,4},{6,5},{7,6},{9,8},{10,9},{11,10},{12... | collective-permute-start | bytes 393224 | tf_op jit(solution)/shard_map/ppermute | solution.py:119
  69.4 13.9 %collective-permute-start.1 = (f32[32,4096]{1,0:T(8,128)S(1)}, f32[32,4096]{1,0:T(8,128)S(1)}, u32[]{:S(2)}, u32[]{:S(2)}) collective-permute-start(f32[32,4096]{1,0:T(8,128)S(1)} %pad_maximum_fusion.1), channel_id=1, source_target_pairs={{1,0},{2,1},{3,2},{4,3},{5,4},{6,5},{7,6},{0,7},{9,8},{10,9},{11,1... | collective-permute-start | bytes 1572872 | tf_op jit(solution)/shard_map/ppermute | solution.py:149
  72.8 18.3 %collective-permute-start = (f32[32,4096]{1,0:T(8,128)S(1)}, f32[32,4096]{1,0:T(8,128)S(1)}, u32[]{:S(2)}, u32[]{:S(2)}) collective-permute-start(f32[32,4096]{1,0:T(8,128)S(1)} %pad_maximum_fusion), channel_id=1, source_target_pairs={{0,1},{1,2},{2,3},{3,4},{4,5},{5,6},{6,7},{8,9},{9,10},{10,11},{11... | collective-permute-start | bytes 1572872 | tf_op jit(solution)/shard_map/ppermute | solution.py:148

commit v13 on v12

--- a/solution.py
+++ b/solution.py
@@ -41,11 +41,10 @@
     columns = h_ref.shape[1]
     half = rows // 2
     band = lax.axis_index("band")
-    keep_above = jnp.where(band > 0, jnp.float32(1.0), jnp.float32(0.0))
     keep_below = jnp.where(band < total_rows // rows - 1, jnp.float32(1.0), jnp.float32(0.0))
 
     def above(lo, hi):
-        return fa_ref[lo:hi] * keep_above
+        return fa_ref[lo:hi]
 
     def below(lo, hi):
         return fb_ref[lo:hi] * keep_below
@@ -60,9 +59,9 @@
     east_vel = jnp.concatenate([above(3 * margin, 4 * margin), u_ref[...], below(3 * margin, 4 * margin)], axis=0)
     north_vel = jnp.concatenate([above(0, margin), v_ref[...], below(0, margin)], axis=0)
     band_start = band * rows
-    global_rows = band_start - margin + lax.broadcasted_iota(jnp.int32, (ext, columns), 0)
-    inside = (global_rows >= 0) & (global_rows < total_rows)
-    coriolis = 0.1 + 0.4 * ((global_rows.astype(jnp.float32) + 0.5) / total_rows)
+    global_rows = band_start - margin + lax.broadcasted_iota(jnp.int32, (ext, 1), 0)
+    inside = jnp.broadcast_to((global_rows >= 0) & (global_rows < total_rows), (ext, columns))
+    coriolis = jnp.broadcast_to(0.1 + 0.4 * ((global_rows.astype(jnp.float32) + 0.5) / total_rows), (ext, columns))
     depth = d_ref[...]
     pad_ref[0:8] = jnp.zeros((8, columns), jnp.float32)
     pad_ref[8 + ext:16 + ext] = jnp.zeros((8, columns), jnp.float32)
@@ -172,6 +171,7 @@
         P("band"),
         P("band"),
     )
+
     return jax.shard_map(
         on_device,
         mesh=mesh,

time: 95.8 us -> 95.8 us (level)
  no operation moved by 1% of the time
where the time goes in v13:
time: 95.8 us; the launch traced here: 95.4 us
  blocking collectives  35.3 us (37%)
  waiting for transfers between devices  21.6 us (23%)
  starting transfers between devices  18.5 us (19%)
  local copies, waits for them, and re-layouts  11.9 us (12%)
  Pallas kernels  4.36 us (5%)
  other arithmetic  2.82 us (3%)
    all_to_all x1, blocking collectives, on_device(): lax.all_to_all(jnp.concatenate([block, tag], axis=1), 'dom', 0, 0, tiled=...  35.3 us
    ppermute x1, waiting for transfers between devices, on_device(): from_below = lax.ppermute(to_above, 'band', ring_up)  8.53 us
    scatter x1, local copies, waits for them, and re-layouts, on_device(): jnp.full((rows * columns,), jnp.nan, jnp.float32).at[position]  8.3 us
    ppermute x1, waiting for transfers between devices, on_device(): from_above = lax.ppermute(to_below, 'band', down)  7.75 us
    ppermute x1, starting transfers between devices, on_device(): lax.ppermute(sea_depth[:margin], 'band', up)  5.97 us
    all_to_all x1, waiting for transfers between devices, on_device(): back = lax.all_to_all(chosen, 'dom', 0, 0, tiled=True)  5.28 us
    pallas_call x1, Pallas kernels, on_device(): pl.pallas_call(functools.partial(forecast_kernel, total_rows=rows * bands...  4.36 us
    all_to_all x1, starting transfers between devices, on_device(): back = lax.all_to_all(chosen, 'dom', 0, 0, tiled=True)  3.83 us
  transfers between devices with their start and end apart: 5, of which 3 were waited for; matrix products, arithmetic and copies ran while one was open for 9% of the time, Pallas kernels for 0%

profile of v13, /device:TPU:36, one launch (start us, length us, event | category | flops | bytes accessed | tf_op | source)
XLA Modules:
  0.0 95.4 jit_solution(4702263891171414660)
XLA Ops:
  0.0 1.3 %copy.27 = f32[6,8,32,128]{3,2,1,0:T(8,128)S(1)} copy(f32[6,8,32,128]{3,1,2,0:T(8,128)} %bitcast.47) | data formatting | bytes 1572864
  1.3 0.5 copy.34
  2.4 0.1 concatenate.12
  2.5 35.3 %all_to_all.10 = f32[32,56,128]{2,1,0:T(8,128)S(1)} all-to-all(f32[32,56,128]{2,1,0:T(8,128)S(1)} %concatenate.12), channel_id=1, replica_groups=mesh['dom'=32,'band'=8] {'dom'}, dimensions={0} | all-to-all | bytes 1835008 | tf_op jit(solution)/shard_map/all_to_all | solution.py:103
  37.8 0.7 fusion.49
  38.4 0.1 slice.233
  38.5 1.5 %gather_fusion = f32[32,48,128]{2,1,0:T(8,128)} fusion(f32[32,48,128]{2,1,0:T(8,128)S(1)} %slice.233, s32[1024]{0:T(1024)S(1)} %pad_clamp_fusion), kind=kCustom, calls=%fused_computation | custom fusion | bytes 1572992 | tf_op jit(solution)/shard_map/jit(_take)/gather | solution.py:105
  40.0 3.8 %all-to-all-start.1 = ((f32[32,48,128]{2,1,0:T(8,128)}), f32[32,48,128]{2,1,0:T(8,128)S(1)}, u32[]{:S(2)}, u32[]{:S(2)}) async-start(f32[32,48,128]{2,1,0:T(8,128)} %gather_fusion), calls=%async_computation.1 | async-start | bytes 1572864 | tf_op jit(solution)/shard_map/all_to_all | solution.py:106
  43.8 0.0 copy-start.2
  43.9 0.0 copy-start.1
  43.9 3.5 %collective-permute-start.2 = (f32[8,4096]{1,0:T(8,128)S(1)}, f32[8,4096]{1,0:T(8,128)S(1)}, u32[]{:S(2)}, u32[]{:S(2)}) collective-permute-start(f32[8,4096]{1,0:T(8,128)S(1)} %get-tuple-element.16), channel_id=1, source_target_pairs={{0,1},{1,2},{2,3},{3,4},{4,5},{5,6},{6,7},{8,9},{9,10},{10,11},{11... | collective-permute-start | bytes 393224 | tf_op jit(solution)/shard_map/ppermute | solution.py:116
  47.4 6.0 %collective-permute-start.3 = (f32[8,4096]{1,0:T(8,128)S(1)}, f32[8,4096]{1,0:T(8,128)S(1)}, u32[]{:S(2)}, u32[]{:S(2)}) collective-permute-start(f32[8,4096]{1,0:T(8,128)S(1)} %get-tuple-element.17), channel_id=1, source_target_pairs={{1,0},{2,1},{3,2},{4,3},{5,4},{6,5},{7,6},{9,8},{10,9},{11,10},{12... | collective-permute-start | bytes 393224 | tf_op jit(solution)/shard_map/ppermute | solution.py:118
  53.4 8.3 %scatter_custom_fusion = f32[65536]{0:T(1024)S(1)} fusion(s32[2048]{0:T(1024)S(1)} %compare_select_fusion, f32[2048]{0:T(1024)} %param.11, f32[]{:T(128)} %constant.16.clone.1), kind=kCustom, calls=%fused_computation.92 | custom fusion | bytes 262656 | tf_op jit(solution)/shard_map/scatter | solution.py:111
  61.7 0.1 reshape.32
  61.8 0.0 collective-permute-done.2
  61.8 5.3 %all-to-all-done.1 = f32[32,48,128]{2,1,0:T(8,128)S(1)} async-done(((f32[32,48,128]{2,1,0:T(8,128)}), f32[32,48,128]{2,1,0:T(8,128)S(1)}, u32[]{:S(2)}, u32[]{:S(2)}) %all-to-all-start.1) | async-done | bytes 786464 | tf_op jit(solution)/shard_map/all_to_all | solution.py:106
  67.1 0.1 slice_bitcast_fusion
  67.3 1.1 %multiply_add_fusion = f32[16,4096]{1,0:T(8,128)S(1)} fusion(f32[16,4096]{1,0:T(8,128)S(1)} %subtract_select_fusion), kind=kLoop, calls=%fused_computation.60 | loop fusion | flops 2097152 | bytes 524288 | tf_op jit(solution)/shard_map/add | solution.py:32
  68.5 0.8 fusion.16.pf_ref
  69.4 3.3 %collective-permute-start.1 = (f32[32,4096]{1,0:T(8,128)S(1)}, f32[32,4096]{1,0:T(8,128)S(1)}, u32[]{:S(2)}, u32[]{:S(2)}) collective-permute-start(f32[32,4096]{1,0:T(8,128)S(1)} %pad_maximum_fusion.1), channel_id=1, source_target_pairs={{1,0},{2,1},{3,2},{4,3},{5,4},{6,5},{7,6},{0,7},{9,8},{10,9},{11,1... | collective-permute-start | bytes 1572872 | tf_op jit(solution)/shard_map/ppermute | solution.py:148
  72.8 1.9 %collective-permute-start = (f32[32,4096]{1,0:T(8,128)S(1)}, f32[32,4096]{1,0:T(8,128)S(1)}, u32[]{:S(2)}, u32[]{:S(2)}) collective-permute-start(f32[32,4096]{1,0:T(8,128)S(1)} %pad_maximum_fusion), channel_id=1, source_target_pairs={{0,1},{1,2},{2,3},{3,4},{4,5},{5,6},{6,7},{8,9},{9,10},{10,11},{11... | collective-permute-start | bytes 1572872 | tf_op jit(solution)/shard_map/ppermute | solution.py:147
  74.7 8.5 %collective-permute-done.1.fb_ref = f32[32,4096]{1,0:T(8,128)S(1)} collective-permute-done((f32[32,4096]{1,0:T(8,128)S(1)}, f32[32,4096]{1,0:T(8,128)S(1)}, u32[]{:S(2)}, u32[]{:S(2)}) %collective-permute-start.1) | collective-permute-done | bytes 524320 | tf_op jit(solution)/shard_map/ppermute | solution.py:148
  83.3 7.8 %collective-permute-done.fa_ref = f32[32,4096]{1,0:T(8,128)S(1)} collective-permute-done((f32[32,4096]{1,0:T(8,128)S(1)}, f32[32,4096]{1,0:T(8,128)S(1)}, u32[]{:S(2)}, u32[]{:S(2)}) %collective-permute-start) | collective-permute-done | bytes 524320 | tf_op jit(solution)/shard_map/ppermute | solution.py:147
  91.0 4.4 %shard_map.64 = f32[3,16,4096]{2,1,0:T(8,128)} custom-call(f32[32,4096]{1,0:T(8,128)S(1)} %collective-permute-done.fa_ref, f32[32,4096]{1,0:T(8,128)S(1)} %collective-permute-done.1.fb_ref, f32[16,4096]{1,0:T(8,128)S(1)} %bitcast.41, f32[16,4096]{1,0:T(8,128)S(1)} %get-tuple-element.19.u_ref, f32[16,4096]{1,0:T(8,128)S(1)} %get-tuple-element.18.v_ref, ...), custom_call_target="tpu_custom_call" | custom-call | tf_op jit(solution)/shard_map/pallas_call | solution.py:151
  (17 shorter events, 0.4 us)
Async XLA Ops:
  40.0 3.8 %copy-start = (f32[16,4096]{1,0:T(8,128)S(1)}, f32[16,4096]{1,0:T(8,128)}, u32[]{:S(2)}) copy-start(f32[16,4096]{1,0:T(8,128)} %param.8) | copy-start | bytes 786436
  40.0 27.1 %all-to-all-start.1 = ((f32[32,48,128]{2,1,0:T(8,128)}), f32[32,48,128]{2,1,0:T(8,128)S(1)}, u32[]{:S(2)}, u32[]{:S(2)}) async-start(f32[32,48,128]{2,1,0:T(8,128)} %gather_fusion), calls=%async_computation.1 | async-start | bytes 1572864 | tf_op jit(solution)/shard_map/all_to_all | solution.py:106
  43.8 9.5 %copy-start.2 = (s32[2048]{0:T(1024)S(1)}, s32[2048]{0:T(1024)}, u32[]{:S(2)}) copy-start(s32[2048]{0:T(1024)} %param.9) | copy-start | bytes 24580
  43.9 9.5 %copy-start.1 = (s32[2048]{0:T(1024)S(1)}, s32[2048]{0:T(1024)}, u32[]{:S(2)}) copy-start(s32[2048]{0:T(1024)} %param.10) | copy-start | bytes 24580
  43.9 17.9 %collective-permute-start.2 = (f32[8,4096]{1,0:T(8,128)S(1)}, f32[8,4096]{1,0:T(8,128)S(1)}, u32[]{:S(2)}, u32[]{:S(2)}) collective-permute-start(f32[8,4096]{1,0:T(8,128)S(1)} %get-tuple-element.16), channel_id=1, source_target_pairs={{0,1},{1,2},{2,3},{3,4},{4,5},{5,6},{6,7},{8,9},{9,10},{10,11},{11... | collective-permute-start | bytes 393224 | tf_op jit(solution)/shard_map/ppermute | solution.py:116
  47.4 14.4 %collective-permute-start.3 = (f32[8,4096]{1,0:T(8,128)S(1)}, f32[8,4096]{1,0:T(8,128)S(1)}, u32[]{:S(2)}, u32[]{:S(2)}) collective-permute-start(f32[8,4096]{1,0:T(8,128)S(1)} %get-tuple-element.17), channel_id=1, source_target_pairs={{1,0},{2,1},{3,2},{4,3},{5,4},{6,5},{7,6},{9,8},{10,9},{11,10},{12... | collective-permute-start | bytes 393224 | tf_op jit(solution)/shard_map/ppermute | solution.py:118
  69.4 13.9 %collective-permute-start.1 = (f32[32,4096]{1,0:T(8,128)S(1)}, f32[32,4096]{1,0:T(8,128)S(1)}, u32[]{:S(2)}, u32[]{:S(2)}) collective-permute-start(f32[32,4096]{1,0:T(8,128)S(1)} %pad_maximum_fusion.1), channel_id=1, source_target_pairs={{1,0},{2,1},{3,2},{4,3},{5,4},{6,5},{7,6},{0,7},{9,8},{10,9},{11,1... | collective-permute-start | bytes 1572872 | tf_op jit(solution)/shard_map/ppermute | solution.py:148
  72.8 18.3 %collective-permute-start = (f32[32,4096]{1,0:T(8,128)S(1)}, f32[32,4096]{1,0:T(8,128)S(1)}, u32[]{:S(2)}, u32[]{:S(2)}) collective-permute-start(f32[32,4096]{1,0:T(8,128)S(1)} %pad_maximum_fusion), channel_id=1, source_target_pairs={{0,1},{1,2},{2,3},{3,4},{4,5},{5,6},{6,7},{8,9},{9,10},{10,11},{11... | collective-permute-start | bytes 1572872 | tf_op jit(solution)/shard_map/ppermute | solution.py:147
